TPU v7x, 1024 devices: a whole 4x8x16 slice. The times are simulated.
1024 devices in a mesh: ctx: 64 (over y, x, core), exp: 16 (over z).
Axes of the slice: x: 4, y: 8, z: 16, core: 2. Of those that a mesh axis runs over, the one named last changes fastest.
Arguments:
- queries: bfloat16 [16384, 4096], P(('ctx', 'exp')), may hold values from -1.25 to 1.25
- keys: bfloat16 [16384, 4096], P(('ctx', 'exp')), may hold values from -0.75 to 0.75
- values: bfloat16 [16384, 4096], P(('ctx', 'exp')), may hold values from -6 to 6
- out_grad: bfloat16 [16384, 4096], P(('ctx', 'exp')), may hold values from -1.5 to 1.5
- decay_rate: float32 [32], P('exp'), may hold values from 1.2207031e-06 to 0.04
- doc_lengths: int32 [8], replicated, may hold values from 1 to 8192, 16384 in all
Outputs:
- attn_out: bfloat16 [16384, 4096], P('ctx', 'exp')
- grad_queries: bfloat16 [16384, 4096], P('ctx', 'exp')
- grad_keys: bfloat16 [16384, 4096], P('ctx', 'exp')
- grad_values: bfloat16 [16384, 4096], P('ctx', 'exp')
Inputs may be any that keep to these rules, and one draw needn't show every extreme that they name: `doc_lengths`: lengths of the 8 documents in order, summing to 16384; the longest is exactly 8192.
All inputs are finite; a program needn't handle non-finite values.
Results may differ from a plain program's by a relative error of at most 0.0033.
Values may be sent and summed in bfloat16 or wider, within the bound.
No kernel may reach another device: no remote copies, remote signals or barrier semaphores. Data moves between devices by JAX's collectives and lax.ppermute only.
A program may use at most 64 MiB of HBM per device.

v0:
```python
import jax
import jax.numpy as jnp
from jax import lax
from jax.sharding import Mesh
from jax.sharding import PartitionSpec as P

DH = 128
CTX = ("ctx_0", "ctx_1", "ctx_2")
CTX_EXP = ("ctx_0", "ctx_1", "ctx_2", "exp")


def nothing_yet(value, identity):
    return jax.tree.map(
        lambda part, zero: jnp.zeros_like(part) + jnp.asarray(zero, part.dtype), value, identity
    )


def carried_in(value, axes, combine, identity, reverse):
    before = start = nothing_yet(value, identity)
    total = value
    for axis in reversed(axes):
        size, position = (lax.axis_size(axis), lax.axis_index(axis))
        pieces = jax.tree.map(lambda part: lax.all_gather(part, axis), total)
        inside, total = (start, start)
        for k in reversed(range(size)) if reverse else range(size):
            passed = k > position if reverse else k < position
            total = combine(total, jax.tree.map(lambda part: part[k], pieces))
            inside = jax.tree.map(lambda new, old: jnp.where(passed, new, old), total, inside)
        before = combine(inside, before)
    return before


def in_one_piece(arrays, axis, split_dim, concat_dim, along):
    widths = [a.shape[along] for a in arrays]
    both = jnp.concatenate(arrays, axis=along)
    out = lax.all_to_all(both, axis, split_axis=split_dim, concat_axis=concat_dim, tiled=True)
    return tuple(jnp.split(out, [sum(widths[:k]) for k in range(1, len(widths))], axis=along))


def segment_of(positions, doc_ends):
    return jnp.sum((doc_ends[None, :] <= positions[:, None]).astype(jnp.int32), axis=1)


def group_masks(group_index, doc_lengths, decays, group_len):
    doc_ends = jnp.cumsum(doc_lengths)
    offsets = jnp.arange(group_len, dtype=jnp.int32)
    first_row = group_index * group_len
    segment = segment_of(first_row + offsets, doc_ends)
    segment_prev = segment_of(first_row - 1 + jnp.zeros((1,), jnp.int32), doc_ends)[0]
    segment_last = segment[group_len - 1]
    enters = (segment == segment_prev).astype(jnp.float32)
    leaves = (segment == segment_last).astype(jnp.float32)
    distance = (offsets[:, None] - offsets[None, :]).astype(jnp.float32)
    allowed = (offsets[:, None] >= offsets[None, :]) & (segment[:, None] == segment[None, :])
    weights = jnp.where(
        allowed[None], jnp.exp(-decays[:, None, None] * jnp.maximum(distance, 0.0)[None]), 0.0
    )
    offsets_f = offsets.astype(jnp.float32)
    enter_w = jnp.exp(-decays[:, None] * (offsets_f + 1.0)[None]) * enters[None]
    leave_w = jnp.exp(-decays[:, None] * (group_len - 1.0 - offsets_f)[None]) * leaves[None]
    return (weights, enter_w, leave_w)


def span_factor(anchor_a, anchor_b, group_gap, doc_ends, decays, group_len):
    same = (segment_of(anchor_a, doc_ends) == segment_of(anchor_b, doc_ends)).astype(jnp.float32)
    gap = jnp.maximum(group_gap, 0).astype(jnp.float32)
    return jnp.exp(-decays * (group_len * gap)) * same


def make_forward_combine(doc_ends, decays, group_len):

    def combine(earlier, later):
        early_last, early_state = earlier
        late_last, late_state = later
        factor = span_factor(
            early_last * group_len + group_len - 1,
            late_last * group_len + group_len - 1,
            late_last - early_last,
            doc_ends,
            decays,
            group_len,
        )
        factor = jnp.where(late_last < 0, 1.0, factor)
        last = jnp.where(late_last < 0, early_last, late_last)
        return (last, factor[:, None, None] * early_state + late_state)

    return combine


def make_backward_combine(doc_ends, decays, group_len):

    def combine(earlier, later):
        high_first, high_state = earlier
        low_first, low_state = later
        factor = span_factor(
            high_first * group_len - 1,
            low_first * group_len - 1,
            high_first - low_first,
            doc_ends,
            decays,
            group_len,
        )
        factor = jnp.where(low_first < 0, 1.0, factor)
        first = jnp.where(low_first < 0, high_first, low_first)
        return (first, low_state + factor[:, None, None] * high_state)

    return combine


def forward_chain(k_wide, v_wide, leave_w, group_here, doc_ends, decays, group_len):
    precise = lax.Precision.HIGHEST
    forward_term = jnp.einsum("hj,jhd,jhe->hde", leave_w, k_wide, v_wide, precision=precise)
    sentinel = jnp.full((1,), -1, jnp.int32)
    combine = make_forward_combine(doc_ends, decays, group_len)
    return carried_in(
        (group_here, forward_term), CTX, combine, (sentinel, jnp.zeros_like(forward_term)), False
    )[1]


def on_device(queries, keys, values, out_grad, decay_rate, doc_lengths):
    precise = lax.Precision.HIGHEST
    rows_in = queries.shape[0]
    group_len = rows_in * lax.axis_size("exp")
    group_index = lax.axis_index(CTX)
    doc_ends = jnp.cumsum(doc_lengths)
    group_here = jnp.zeros((1,), jnp.int32) + group_index
    weights, enter_w, leave_w = group_masks(group_index, doc_lengths, decay_rate, group_len)
    q_rows, k_rows, v_rows, g_rows = in_one_piece(
        (
            queries.reshape(rows_in, -1, DH),
            keys.reshape(rows_in, -1, DH),
            values.reshape(rows_in, -1, DH),
            out_grad.reshape(rows_in, -1, DH),
        ),
        "exp",
        1,
        0,
        2,
    )
    k_wide = k_rows.astype(jnp.float32)
    v_wide = v_rows.astype(jnp.float32)
    state_in = forward_chain(k_wide, v_wide, leave_w, group_here, doc_ends, decay_rate, group_len)
    q_wide = q_rows.astype(jnp.float32)
    g_wide = g_rows.astype(jnp.float32)
    backward_term = jnp.einsum("hi,ihd,ihe->hde", enter_w, q_wide, g_wide, precision=precise)
    sentinel = jnp.full((1,), -1, jnp.int32)
    backward = make_backward_combine(doc_ends, decay_rate, group_len)
    state_next = carried_in(
        (group_here, backward_term), CTX, backward, (sentinel, jnp.zeros_like(backward_term)), True
    )[1]
    enter_t = enter_w.T[:, :, None]
    leave_t = leave_w.T[:, :, None]
    scores = (
        jnp.einsum("ihd,jhd->hij", q_rows, k_rows, preferred_element_type=jnp.float32) * weights
    ).astype(jnp.bfloat16)
    attended = jnp.einsum("hij,jhd->ihd", scores, v_rows, preferred_element_type=jnp.float32)
    attended = (
        attended + jnp.einsum("ihd,hde->ihe", q_wide, state_in, precision=precise) * enter_t
    ).astype(jnp.bfloat16)
    grads_loc = (
        jnp.einsum("ihd,jhd->hij", g_rows, v_rows, preferred_element_type=jnp.float32) * weights
    ).astype(jnp.bfloat16)
    grad_q = jnp.einsum("hij,jhd->ihd", grads_loc, k_rows, preferred_element_type=jnp.float32)
    grad_q = (
        grad_q + jnp.einsum("ihe,hde->ihd", g_wide, state_in, precision=precise) * enter_t
    ).astype(jnp.bfloat16)
    grad_k = jnp.einsum("hij,ihd->jhd", grads_loc, q_rows, preferred_element_type=jnp.float32)
    grad_k = (
        grad_k + jnp.einsum("jhe,hde->jhd", v_wide, state_next, precision=precise) * leave_t
    ).astype(jnp.bfloat16)
    grad_v = jnp.einsum("hij,ihe->jhe", scores, g_rows, preferred_element_type=jnp.float32)
    grad_v = (
        grad_v + jnp.einsum("jhd,hde->jhe", k_wide, state_next, precision=precise) * leave_t
    ).astype(jnp.bfloat16)
    return (
        attended.reshape(group_len, -1),
        grad_q.reshape(group_len, -1),
        grad_k.reshape(group_len, -1),
        grad_v.reshape(group_len, -1),
    )


def solution(mesh):
    split = Mesh(
        mesh.devices.reshape(8, 4, 2, mesh.shape["exp"]), ("ctx_0", "ctx_1", "ctx_2", "exp")
    )
    placed = (P(CTX_EXP, None), P(CTX_EXP, None), P(CTX_EXP, None), P(CTX_EXP, None), P("exp"), P())
    return jax.shard_map(
        on_device,
        mesh=split,
        in_specs=placed,
        out_specs=(P(CTX, "exp"), P(CTX, "exp"), P(CTX, "exp"), P(CTX, "exp")),
        check_vma=False,
    )
```

profile of v0, /device:TPU:8, one launch (start us, length us, event | category | flops | bytes accessed | tf_op | source)
XLA Modules:
  0.0 289.1 jit_solution(9924108145143657622)
XLA Ops:
  7.2 1.3 dynamic-slice
  9.2 1.8 all-reduce
  11.6 1.3 dynamic-slice.1
  13.0 1.4 dynamic-update-slice.1
  14.4 1.4 dynamic-update-slice.3
  15.9 8.9 %all-reduce.6 = (s32[4]{0:T(128)S(1)}, s32[4]{0:T(128)S(1)}) all-reduce(s32[4]{0:T(128)S(1)} %dynamic-update-slice.3, s32[4]{0:T(128)S(1)} %dynamic-update-slice.1), channel_id=6, replica_groups=mesh['ctx_0'=8,'ctx_1'=4,'ctx_2'=2,'exp'=16] {'ctx_1'}, use_global_device_ids=true, to_apply=%add.3 | all-reduce | flops 8 | bytes 64
  26.1 1.4 dynamic-slice.2
  27.4 1.0 copy.85
  28.4 0.9 copy-done.1
  29.3 0.9 copy-done.2
  30.3 1.1 copy.63
  31.4 1.8 fusion.138
  33.2 1.4 dynamic-update-slice.2
  34.6 1.4 dynamic-update-slice.4
  36.0 18.9 %all-to-all-start = ((bf16[16,32,512]{2,0,1:T(8,128)(2,1)}), bf16[16,32,512]{2,0,1:T(8,128)(2,1)S(1)}, u32[]{:S(2)}, u32[]{:S(2)}) async-start(bf16[16,32,512]{2,0,1:T(8,128)(2,1)} %copy.63), calls=%async_computation | async-start | bytes 1048576 | tf_op jit(solution)/shard_map/all_to_all | solution.py:36
  54.9 13.2 %all-reduce.5 = (s32[8]{0:T(128)S(1)}, s32[8]{0:T(128)S(1)}) all-reduce(s32[8]{0:T(128)S(1)} %dynamic-update-slice.4, s32[8]{0:T(128)S(1)} %dynamic-update-slice.2), channel_id=7, replica_groups=mesh['ctx_0'=8,'ctx_1'=4,'ctx_2'=2,'exp'=16] {'ctx_0'}, use_global_device_ids=true, to_apply=%add.4 | all-reduce | flops 16 | bytes 128
  86.1 1.8 fusion.143
  89.8 1.1 fusion.145
  108.4 1.1 fusion.141
  135.1 1.0 fusion.77
  146.1 1.0 fusion.111
  147.2 1.0 fusion.112
  165.4 1.3 compare_convert_fusion.30
  168.0 2.0 all-gather.3
  170.1 13.2 %all_gather.69 = f32[4,2,128,128]{3,2,1,0:T(8,128)S(1)} all-gather(f32[1,2,128,128]{3,2,1,0:T(8,128)S(1)} %fusion.47), channel_id=1, replica_groups=mesh['ctx_0'=8,'ctx_1'=4,'ctx_2'=2,'exp'=16] {'ctx_1'}, dimensions={0}, use_global_device_ids=true | all-gather | bytes 655360 | tf_op jit(solution)/shard_map/all_gather | solution.py:23
  215.4 2.0 all-gather.2
  217.5 13.4 %all_gather.63 = f32[4,2,128,128]{3,2,1,0:T(8,128)S(1)} all-gather(f32[1,2,128,128]{3,2,1,0:T(8,128)S(1)} %bitcast_add_fusion.9), channel_id=1, replica_groups=mesh['ctx_0'=8,'ctx_1'=4,'ctx_2'=2,'exp'=16] {'ctx_1'}, dimensions={0}, use_global_device_ids=true | all-gather | bytes 655360 | tf_op jit(solution)/shard_map/all_gather | solution.py:23
  232.4 1.6 fusion.31
  234.7 41.5 %all-gather.9.cloned.1.call-done = f32[8,2,128,128]{3,2,1,0:T(8,128)} async-done(((f32[1,2,128,128]{3,2,1,0:T(8,128)}), f32[8,2,128,128]{3,2,1,0:T(8,128)}) %all-gather.9.cloned.1.call-update) | async-done | bytes 1048592 | tf_op jit(solution)/shard_map/all_gather | solution.py:23
  276.1 1.6 fusion.35
  278.6 0.8 copy.76
  280.5 0.8 copy.74
  (64 shorter events, 14.4 us)
Async XLA Ops:
  27.4 1.0 copy-start
  28.4 0.9 copy-start.1
  29.3 0.9 copy-start.2
  36.0 131.5 %all-to-all-start = ((bf16[16,32,512]{2,0,1:T(8,128)(2,1)}), bf16[16,32,512]{2,0,1:T(8,128)(2,1)S(1)}, u32[]{:S(2)}, u32[]{:S(2)}) async-start(bf16[16,32,512]{2,0,1:T(8,128)(2,1)} %copy.63), calls=%async_computation | async-start | bytes 1048576 | tf_op jit(solution)/shard_map/all_to_all | solution.py:36
  54.9 177.5 %all-gather.11.cloned.1.call-start = ((), (), s32[]{:S(2)}) async-start(), calls=%async_computation.2 | async-start | bytes 1179648 | tf_op jit(solution)/shard_map/all_gather | solution.py:23
  134.2 0.7 copy-start.4
  166.7 0.7 copy-start.3
  184.1 92.0 %all-gather.9.cloned.1.call-start = ((), (), s32[]{:S(2)}) async-start(), calls=%async_computation.1 | async-start | bytes 1179648 | tf_op jit(solution)/shard_map/all_gather | solution.py:23
Sparse Core Ops, SparseCore 0:
  184.2 43.1 all-gather.10
  231.8 44.2 all-gather.8
where the time goes:
time: 291 us; the launch traced here: 289 us
  between operations  132 us (45%)
  blocking collectives  54.5 us (19%)
  waiting for transfers between devices  41.5 us (14%)
  local copies, waits for them, and re-layouts  20.6 us (7%)
  starting transfers between devices  18.9 us (6%)
  other arithmetic  18.5 us (6%)
  matrix products  3.6 us (1%)
    all_gather x2, waiting for transfers between devices, carried_in(): pieces = jax.tree.map(lambda part: lax.all_gather(part, axis), total)  41.5 us
    all_gather x4, blocking collectives, carried_in(): pieces = jax.tree.map(lambda part: lax.all_gather(part, axis), total)  30.6 us
    unnamed x3, blocking collectives  23.9 us
    all_to_all x1, starting transfers between devices, in_one_piece(): lax.all_to_all(both, axis, split_axis=split_dim, concat_axis=concat_dim,...  18.9 us
    unnamed x31, local copies, waits for them, and re-layouts  17.5 us
  transfers between devices with their start and end apart: 3, of which 1 were waited for; matrix products, arithmetic and copies ran while one was open for 5% of the time, Pallas kernels for 0%

commit v1 on v0

v1 whole, which is shorter than its diff:
```python
import jax
import jax.numpy as jnp
from jax import lax
from jax.sharding import PartitionSpec as P

DH = 128


def in_one_piece(arrays, axis, split_dim, concat_dim, along):
    widths = [a.shape[along] for a in arrays]
    both = jnp.concatenate(arrays, axis=along)
    out = lax.all_to_all(both, axis, split_axis=split_dim, concat_axis=concat_dim, tiled=True)
    return tuple(jnp.split(out, [sum(widths[:k]) for k in range(1, len(widths))], axis=along))


def segment_of(positions, doc_ends):
    return jnp.sum((doc_ends[None, :] <= positions[:, None]).astype(jnp.int32), axis=1)


def group_masks(group_index, doc_ends, decays, group_len):
    offsets = jnp.arange(group_len, dtype=jnp.int32)
    first_row = group_index * group_len
    segment = segment_of(first_row + offsets, doc_ends)
    segment_prev = segment_of(first_row - 1 + jnp.zeros((1,), jnp.int32), doc_ends)[0]
    segment_last = segment[group_len - 1]
    enters = (segment == segment_prev).astype(jnp.float32)
    leaves = (segment == segment_last).astype(jnp.float32)
    distance = (offsets[:, None] - offsets[None, :]).astype(jnp.float32)
    allowed = (offsets[:, None] >= offsets[None, :]) & (segment[:, None] == segment[None, :])
    weights = jnp.where(
        allowed[None], jnp.exp(-decays[:, None, None] * jnp.maximum(distance, 0.0)[None]), 0.0
    )
    offsets_f = offsets.astype(jnp.float32)
    enter_w = jnp.exp(-decays[:, None] * (offsets_f + 1.0)[None]) * enters[None]
    leave_w = jnp.exp(-decays[:, None] * (group_len - 1.0 - offsets_f)[None]) * leaves[None]
    return (weights, enter_w, leave_w)


def decayed_scan(term, anchors, here, decays, group_len, count, forward):
    total = term
    shift = 1
    while shift < count:
        if forward:
            pairs = [(i, i + shift) for i in range(count - shift)]
            other = jnp.maximum(here - shift, 0)
        else:
            pairs = [(i + shift, i) for i in range(count - shift)]
            other = jnp.minimum(here + shift, count - 1)
        incoming = lax.ppermute(total, "ctx", pairs)
        same = (anchors[here] == anchors[other]).astype(jnp.float32)
        factor = jnp.exp(-decays * float(group_len * shift)) * same
        total = total + factor[:, None, None] * incoming
        shift *= 2
    if forward:
        pairs = [(i, i + 1) for i in range(count - 1)]
    else:
        pairs = [(i + 1, i) for i in range(count - 1)]
    return lax.ppermute(total, "ctx", pairs)


def on_device(queries, keys, values, out_grad, decay_rate, doc_lengths):
    precise = lax.Precision.HIGHEST
    rows_in = queries.shape[0]
    count = lax.axis_size("ctx")
    group_len = rows_in * lax.axis_size("exp")
    here = lax.axis_index("ctx")
    doc_ends = jnp.cumsum(doc_lengths)
    weights, enter_w, leave_w = group_masks(here, doc_ends, decay_rate, group_len)
    starts = jnp.arange(count, dtype=jnp.int32) * group_len
    end_segments = segment_of(starts + (group_len - 1), doc_ends)
    before_segments = segment_of(starts - 1, doc_ends)
    q_rows, k_rows, v_rows, g_rows = in_one_piece(
        (
            queries.reshape(rows_in, -1, DH),
            keys.reshape(rows_in, -1, DH),
            values.reshape(rows_in, -1, DH),
            out_grad.reshape(rows_in, -1, DH),
        ),
        "exp",
        1,
        0,
        2,
    )
    k_wide = k_rows.astype(jnp.float32)
    v_wide = v_rows.astype(jnp.float32)
    q_wide = q_rows.astype(jnp.float32)
    g_wide = g_rows.astype(jnp.float32)
    enter_t = enter_w.T[:, :, None]
    leave_t = leave_w.T[:, :, None]
    forward_term = jnp.einsum("jhd,jhe->hde", k_wide * leave_t, v_wide, precision=precise)
    backward_term = jnp.einsum("ihd,ihe->hde", q_wide * enter_t, g_wide, precision=precise)
    state_in = decayed_scan(
        forward_term, end_segments, here, decay_rate, group_len, count, True
    )
    state_next = decayed_scan(
        backward_term, before_segments, here, decay_rate, group_len, count, False
    )
    scores = (
        jnp.einsum("ihd,jhd->hij", q_rows, k_rows, preferred_element_type=jnp.float32) * weights
    ).astype(jnp.bfloat16)
    grads_loc = (
        jnp.einsum("ihd,jhd->hij", g_rows, v_rows, preferred_element_type=jnp.float32) * weights
    ).astype(jnp.bfloat16)
    attended = jnp.einsum("hij,jhd->ihd", scores, v_rows, preferred_element_type=jnp.float32)
    grad_q = jnp.einsum("hij,jhd->ihd", grads_loc, k_rows, preferred_element_type=jnp.float32)
    grad_k = jnp.einsum("hij,ihd->jhd", grads_loc, q_rows, preferred_element_type=jnp.float32)
    grad_v = jnp.einsum("hij,ihe->jhe", scores, g_rows, preferred_element_type=jnp.float32)
    attended = (
        attended + jnp.einsum("ihd,hde->ihe", q_wide, state_in, precision=precise) * enter_t
    ).astype(jnp.bfloat16)
    grad_q = (
        grad_q + jnp.einsum("ihe,hde->ihd", g_wide, state_in, precision=precise) * enter_t
    ).astype(jnp.bfloat16)
    grad_k = (
        grad_k + jnp.einsum("jhe,hde->jhd", v_wide, state_next, precision=precise) * leave_t
    ).astype(jnp.bfloat16)
    grad_v = (
        grad_v + jnp.einsum("jhd,hde->jhe", k_wide, state_next, precision=precise) * leave_t
    ).astype(jnp.bfloat16)
    return (
        attended.reshape(group_len, -1),
        grad_q.reshape(group_len, -1),
        grad_k.reshape(group_len, -1),
        grad_v.reshape(group_len, -1),
    )


def solution(mesh):
    placed = (
        P(("ctx", "exp"), None),
        P(("ctx", "exp"), None),
        P(("ctx", "exp"), None),
        P(("ctx", "exp"), None),
        P("exp"),
        P(),
    )
    return jax.shard_map(
        on_device,
        mesh=mesh,
        in_specs=placed,
        out_specs=(P("ctx", "exp"), P("ctx", "exp"), P("ctx", "exp"), P("ctx", "exp")),
        check_vma=False,
    )
```

time: 291 us -> 133 us (0.46)
  the two profiles are of different devices: /device:TPU:8 before, /device:TPU:40 now
where the time goes in v1:
time: 133 us; the launch traced here: 132 us
  starting transfers between devices  69.6 us (52%)
  waiting for transfers between devices  29.8 us (22%)
  between operations  15.8 us (12%)
  local copies, waits for them, and re-layouts  10 us (8%)
  other arithmetic  3.59 us (3%)
  matrix products  3.58 us (3%)
    ppermute x12, starting transfers between devices, decayed_scan(): incoming = lax.ppermute(total, 'ctx', pairs)  46.9 us
    all_to_all x1, starting transfers between devices, in_one_piece(): lax.all_to_all(both, axis, split_axis=split_dim, concat_axis=concat_dim,...  18.9 us
    ppermute x12, waiting for transfers between devices, decayed_scan(): incoming = lax.ppermute(total, 'ctx', pairs)  15.3 us
    all_to_all x1, waiting for transfers between devices, in_one_piece(): lax.all_to_all(both, axis, split_axis=split_dim, concat_axis=concat_dim,...  9.17 us
    unnamed x18, local copies, waits for them, and re-layouts  7.12 us
    ppermute x2, waiting for transfers between devices, decayed_scan(): return lax.ppermute(total, 'ctx', pairs)  5.3 us
    ppermute x2, starting transfers between devices, decayed_scan(): return lax.ppermute(total, 'ctx', pairs)  3.84 us
  transfers between devices with their start and end apart: 15, of which 9 were waited for; matrix products, arithmetic and copies ran while one was open for 5% of the time, Pallas kernels for 0%

profile of v1, /device:TPU:40, one launch (start us, length us, event | category | flops | bytes accessed | tf_op | source)
XLA Modules:
  0.0 132.4 jit_solution(14271240822858250119)
XLA Ops:
  0.6 1.0 copy.145
  1.7 0.9 copy-done.1
  2.5 0.9 copy-done.2
  3.5 1.1 copy.103
  4.6 18.9 %all-to-all-start = ((bf16[16,32,512]{2,0,1:T(8,128)(2,1)}), bf16[16,32,512]{2,0,1:T(8,128)(2,1)S(1)}, u32[]{:S(2)}, u32[]{:S(2)}) async-start(bf16[16,32,512]{2,0,1:T(8,128)(2,1)} %copy.103), calls=%async_computation | async-start | bytes 1048576 | tf_op jit(solution)/shard_map/all_to_all | solution.py:12
  25.2 0.7 fusion.42
  40.6 0.7 fusion.39
  41.3 1.2 compare_convert_fusion
  43.4 9.2 %all-to-all-done = bf16[16,32,512]{2,0,1:T(8,128)(2,1)S(1)} async-done(((bf16[16,32,512]{2,0,1:T(8,128)(2,1)}), bf16[16,32,512]{2,0,1:T(8,128)(2,1)S(1)}, u32[]{:S(2)}, u32[]{:S(2)}) %all-to-all-start) | async-done | bytes 524320 | tf_op jit(solution)/shard_map/all_to_all | solution.py:12
  54.7 1.9 %collective-permute-start.7 = (f32[2,128,128]{2,1,0:T(8,128)S(1)}, f32[2,128,128]{2,1,0:T(8,128)S(1)}, u32[]{:S(2)}, u32[]{:S(2)}) collective-permute-start(f32[2,128,128]{2,1,0:T(8,128)S(1)} %fusion.14), channel_id=1, source_target_pairs={{16,0},{32,16},{48,32},{64,48},{80,64},{96,80},{112,96},{128,112},... | collective-permute-start | bytes 393224 | tf_op jit(solution)/shard_map/ppermute | solution.py:49
  56.6 2.4 %collective-permute-start = (f32[2,128,128]{2,1,0:T(8,128)S(1)}, f32[2,128,128]{2,1,0:T(8,128)S(1)}, u32[]{:S(2)}, u32[]{:S(2)}) collective-permute-start(f32[2,128,128]{2,1,0:T(8,128)S(1)} %fusion.17), channel_id=1, source_target_pairs={{0,16},{16,32},{32,48},{48,64},{64,80},{80,96},{96,112},{112,128},... | collective-permute-start | bytes 393224 | tf_op jit(solution)/shard_map/ppermute | solution.py:49
  59.6 5.5 %collective-permute-start.8 = (f32[2,128,128]{2,1,0:T(8,128)S(1)}, f32[2,128,128]{2,1,0:T(8,128)S(1)}, u32[]{:S(2)}, u32[]{:S(2)}) collective-permute-start(f32[2,128,128]{2,1,0:T(8,128)S(1)} %multiply_add_fusion.5), channel_id=1, source_target_pairs={{32,0},{48,16},{64,32},{80,48},{96,64},{112,80},{128,96},{144,112}... | collective-permute-start | bytes 393224 | tf_op jit(solution)/shard_map/ppermute | solution.py:49
  65.2 1.9 %collective-permute-start.1 = (f32[2,128,128]{2,1,0:T(8,128)S(1)}, f32[2,128,128]{2,1,0:T(8,128)S(1)}, u32[]{:S(2)}, u32[]{:S(2)}) collective-permute-start(f32[2,128,128]{2,1,0:T(8,128)S(1)} %multiply_add_fusion.11), channel_id=1, source_target_pairs={{0,32},{16,48},{32,64},{48,80},{64,96},{80,112},{96,128},{112,144}... | collective-permute-start | bytes 393224 | tf_op jit(solution)/shard_map/ppermute | solution.py:49
  67.1 1.3 collective-permute-done.8
  68.5 5.2 %collective-permute-start.9 = (f32[2,128,128]{2,1,0:T(8,128)S(1)}, f32[2,128,128]{2,1,0:T(8,128)S(1)}, u32[]{:S(2)}, u32[]{:S(2)}) collective-permute-start(f32[2,128,128]{2,1,0:T(8,128)S(1)} %multiply_add_fusion.4), channel_id=1, source_target_pairs={{64,0},{80,16},{96,32},{112,48},{128,64},{144,80},{160,96},{176,11... | collective-permute-start | bytes 393224 | tf_op jit(solution)/shard_map/ppermute | solution.py:49
  73.6 1.7 %collective-permute-done.1 = f32[2,128,128]{2,1,0:T(8,128)S(1)} collective-permute-done((f32[2,128,128]{2,1,0:T(8,128)S(1)}, f32[2,128,128]{2,1,0:T(8,128)S(1)}, u32[]{:S(2)}, u32[]{:S(2)}) %collective-permute-start.1) | collective-permute-done | bytes 131104 | tf_op jit(solution)/shard_map/ppermute | solution.py:49
  75.4 1.9 %collective-permute-start.2 = (f32[2,128,128]{2,1,0:T(8,128)S(1)}, f32[2,128,128]{2,1,0:T(8,128)S(1)}, u32[]{:S(2)}, u32[]{:S(2)}) collective-permute-start(f32[2,128,128]{2,1,0:T(8,128)S(1)} %multiply_add_fusion.10), channel_id=1, source_target_pairs={{0,64},{16,80},{32,96},{48,112},{64,128},{80,144},{96,160},{112,17... | collective-permute-start | bytes 393224 | tf_op jit(solution)/shard_map/ppermute | solution.py:49
  77.6 6.9 %collective-permute-start.10 = (f32[2,128,128]{2,1,0:T(8,128)S(1)}, f32[2,128,128]{2,1,0:T(8,128)S(1)}, u32[]{:S(2)}, u32[]{:S(2)}) collective-permute-start(f32[2,128,128]{2,1,0:T(8,128)S(1)} %multiply_add_fusion.3), channel_id=1, source_target_pairs={{128,0},{144,16},{160,32},{176,48},{192,64},{208,80},{224,96},{240... | collective-permute-start | bytes 393224 | tf_op jit(solution)/shard_map/ppermute | solution.py:49
  84.8 2.6 %collective-permute-start.3 = (f32[2,128,128]{2,1,0:T(8,128)S(1)}, f32[2,128,128]{2,1,0:T(8,128)S(1)}, u32[]{:S(2)}, u32[]{:S(2)}) collective-permute-start(f32[2,128,128]{2,1,0:T(8,128)S(1)} %multiply_add_fusion.9), channel_id=1, source_target_pairs={{0,128},{16,144},{32,160},{48,176},{64,192},{80,208},{96,224},{112... | collective-permute-start | bytes 393224 | tf_op jit(solution)/shard_map/ppermute | solution.py:49
  87.4 10.2 %collective-permute-start.11 = (f32[2,128,128]{2,1,0:T(8,128)S(1)}, f32[2,128,128]{2,1,0:T(8,128)S(1)}, u32[]{:S(2)}, u32[]{:S(2)}) collective-permute-start(f32[2,128,128]{2,1,0:T(8,128)S(1)} %multiply_add_fusion.2), channel_id=1, source_target_pairs={{256,0},{272,16},{288,32},{304,48},{320,64},{336,80},{352,96},{368... | collective-permute-start | bytes 393224 | tf_op jit(solution)/shard_map/ppermute | solution.py:49
  97.8 1.9 %collective-permute-start.4 = (f32[2,128,128]{2,1,0:T(8,128)S(1)}, f32[2,128,128]{2,1,0:T(8,128)S(1)}, u32[]{:S(2)}, u32[]{:S(2)}) collective-permute-start(f32[2,128,128]{2,1,0:T(8,128)S(1)} %multiply_add_fusion.8), channel_id=1, source_target_pairs={{0,256},{16,272},{32,288},{48,304},{64,320},{80,336},{96,352},{112... | collective-permute-start | bytes 393224 | tf_op jit(solution)/shard_map/ppermute | solution.py:49
  100.3 5.2 %collective-permute-start.12 = (f32[2,128,128]{2,1,0:T(8,128)S(1)}, f32[2,128,128]{2,1,0:T(8,128)S(1)}, u32[]{:S(2)}, u32[]{:S(2)}) collective-permute-start(f32[2,128,128]{2,1,0:T(8,128)S(1)} %multiply_add_fusion.1), channel_id=1, source_target_pairs={{512,0},{528,16},{544,32},{560,48},{576,64},{592,80},{608,96},{624... | collective-permute-start | bytes 393224 | tf_op jit(solution)/shard_map/ppermute | solution.py:49
  105.5 2.6 %collective-permute-done.4 = f32[2,128,128]{2,1,0:T(8,128)S(1)} collective-permute-done((f32[2,128,128]{2,1,0:T(8,128)S(1)}, f32[2,128,128]{2,1,0:T(8,128)S(1)}, u32[]{:S(2)}, u32[]{:S(2)}) %collective-permute-start.4) | collective-permute-done | bytes 131104 | tf_op jit(solution)/shard_map/ppermute | solution.py:49
  108.2 1.3 collective-permute-start.5
  109.6 1.9 %collective-permute-start.13 = (f32[2,128,128]{2,1,0:T(8,128)S(1)}, f32[2,128,128]{2,1,0:T(8,128)S(1)}, u32[]{:S(2)}, u32[]{:S(2)}) collective-permute-start(f32[2,128,128]{2,1,0:T(8,128)S(1)} %multiply_add_fusion), channel_id=1, source_target_pairs={{16,0},{32,16},{48,32},{64,48},{80,64},{96,80},{112,96},{128,112},... | collective-permute-start | bytes 393224 | tf_op jit(solution)/shard_map/ppermute | solution.py:58
  111.6 8.8 %collective-permute-done.5 = f32[2,128,128]{2,1,0:T(8,128)S(1)} collective-permute-done((f32[2,128,128]{2,1,0:T(8,128)S(1)}, f32[2,128,128]{2,1,0:T(8,128)S(1)}, u32[]{:S(2)}, u32[]{:S(2)}) %collective-permute-start.5) | collective-permute-done | bytes 131104 | tf_op jit(solution)/shard_map/ppermute | solution.py:49
  120.5 1.9 %collective-permute-start.6 = (f32[2,128,128]{2,1,0:T(8,128)S(1)}, f32[2,128,128]{2,1,0:T(8,128)S(1)}, u32[]{:S(2)}, u32[]{:S(2)}) collective-permute-start(f32[2,128,128]{2,1,0:T(8,128)S(1)} %multiply_add_fusion.6), channel_id=1, source_target_pairs={{0,16},{16,32},{32,48},{48,64},{64,80},{80,96},{96,112},{112,128},... | collective-permute-start | bytes 393224 | tf_op jit(solution)/shard_map/ppermute | solution.py:58
  122.8 0.8 copy.128
  123.6 5.3 %collective-permute-done.6 = f32[2,128,128]{2,1,0:T(8,128)S(1)} collective-permute-done((f32[2,128,128]{2,1,0:T(8,128)S(1)}, f32[2,128,128]{2,1,0:T(8,128)S(1)}, u32[]{:S(2)}, u32[]{:S(2)}) %collective-permute-start.6) | collective-permute-done | bytes 131104 | tf_op jit(solution)/shard_map/ppermute | solution.py:58
  129.3 0.8 copy.125
  130.5 0.8 copy.127
  131.6 0.8 copy.126
  (62 shorter events, 8.6 us)
Async XLA Ops:
  0.6 1.0 copy-start
  1.6 0.9 copy-start.1
  2.5 0.9 copy-start.2
  4.6 48.0 %all-to-all-start = ((bf16[16,32,512]{2,0,1:T(8,128)(2,1)}), bf16[16,32,512]{2,0,1:T(8,128)(2,1)S(1)}, u32[]{:S(2)}, u32[]{:S(2)}) async-start(bf16[16,32,512]{2,0,1:T(8,128)(2,1)} %copy.103), calls=%async_computation | async-start | bytes 1048576 | tf_op jit(solution)/shard_map/all_to_all | solution.py:12
  23.5 0.7 copy-start.4
  42.6 0.7 copy-start.3
  54.7 4.8 %collective-permute-start.7 = (f32[2,128,128]{2,1,0:T(8,128)S(1)}, f32[2,128,128]{2,1,0:T(8,128)S(1)}, u32[]{:S(2)}, u32[]{:S(2)}) collective-permute-start(f32[2,128,128]{2,1,0:T(8,128)S(1)} %fusion.14), channel_id=1, source_target_pairs={{16,0},{32,16},{48,32},{64,48},{80,64},{96,80},{112,96},{128,112},... | collective-permute-start | bytes 393224 | tf_op jit(solution)/shard_map/ppermute | solution.py:49
  56.6 8.5 %collective-permute-start = (f32[2,128,128]{2,1,0:T(8,128)S(1)}, f32[2,128,128]{2,1,0:T(8,128)S(1)}, u32[]{:S(2)}, u32[]{:S(2)}) collective-permute-start(f32[2,128,128]{2,1,0:T(8,128)S(1)} %fusion.17), channel_id=1, source_target_pairs={{0,16},{16,32},{32,48},{48,64},{64,80},{80,96},{96,112},{112,128},... | collective-permute-start | bytes 393224 | tf_op jit(solution)/shard_map/ppermute | solution.py:49
  59.6 8.8 %collective-permute-start.8 = (f32[2,128,128]{2,1,0:T(8,128)S(1)}, f32[2,128,128]{2,1,0:T(8,128)S(1)}, u32[]{:S(2)}, u32[]{:S(2)}) collective-permute-start(f32[2,128,128]{2,1,0:T(8,128)S(1)} %multiply_add_fusion.5), channel_id=1, source_target_pairs={{32,0},{48,16},{64,32},{80,48},{96,64},{112,80},{128,96},{144,112}... | collective-permute-start | bytes 393224 | tf_op jit(solution)/shard_map/ppermute | solution.py:49
  65.2 10.2 %collective-permute-start.1 = (f32[2,128,128]{2,1,0:T(8,128)S(1)}, f32[2,128,128]{2,1,0:T(8,128)S(1)}, u32[]{:S(2)}, u32[]{:S(2)}) collective-permute-start(f32[2,128,128]{2,1,0:T(8,128)S(1)} %multiply_add_fusion.11), channel_id=1, source_target_pairs={{0,32},{16,48},{32,64},{48,80},{64,96},{80,112},{96,128},{112,144}... | collective-permute-start | bytes 393224 | tf_op jit(solution)/shard_map/ppermute | solution.py:49
  68.5 9.0 %collective-permute-start.9 = (f32[2,128,128]{2,1,0:T(8,128)S(1)}, f32[2,128,128]{2,1,0:T(8,128)S(1)}, u32[]{:S(2)}, u32[]{:S(2)}) collective-permute-start(f32[2,128,128]{2,1,0:T(8,128)S(1)} %multiply_add_fusion.4), channel_id=1, source_target_pairs={{64,0},{80,16},{96,32},{112,48},{128,64},{144,80},{160,96},{176,11... | collective-permute-start | bytes 393224 | tf_op jit(solution)/shard_map/ppermute | solution.py:49
  75.4 9.3 %collective-permute-start.2 = (f32[2,128,128]{2,1,0:T(8,128)S(1)}, f32[2,128,128]{2,1,0:T(8,128)S(1)}, u32[]{:S(2)}, u32[]{:S(2)}) collective-permute-start(f32[2,128,128]{2,1,0:T(8,128)S(1)} %multiply_add_fusion.10), channel_id=1, source_target_pairs={{0,64},{16,80},{32,96},{48,112},{64,128},{80,144},{96,160},{112,17... | collective-permute-start | bytes 393224 | tf_op jit(solution)/shard_map/ppermute | solution.py:49
  77.6 9.7 %collective-permute-start.10 = (f32[2,128,128]{2,1,0:T(8,128)S(1)}, f32[2,128,128]{2,1,0:T(8,128)S(1)}, u32[]{:S(2)}, u32[]{:S(2)}) collective-permute-start(f32[2,128,128]{2,1,0:T(8,128)S(1)} %multiply_add_fusion.3), channel_id=1, source_target_pairs={{128,0},{144,16},{160,32},{176,48},{192,64},{208,80},{224,96},{240... | collective-permute-start | bytes 393224 | tf_op jit(solution)/shard_map/ppermute | solution.py:49
  84.8 12.9 %collective-permute-start.3 = (f32[2,128,128]{2,1,0:T(8,128)S(1)}, f32[2,128,128]{2,1,0:T(8,128)S(1)}, u32[]{:S(2)}, u32[]{:S(2)}) collective-permute-start(f32[2,128,128]{2,1,0:T(8,128)S(1)} %multiply_add_fusion.9), channel_id=1, source_target_pairs={{0,128},{16,144},{32,160},{48,176},{64,192},{80,208},{96,224},{112... | collective-permute-start | bytes 393224 | tf_op jit(solution)/shard_map/ppermute | solution.py:49
  87.4 12.7 %collective-permute-start.11 = (f32[2,128,128]{2,1,0:T(8,128)S(1)}, f32[2,128,128]{2,1,0:T(8,128)S(1)}, u32[]{:S(2)}, u32[]{:S(2)}) collective-permute-start(f32[2,128,128]{2,1,0:T(8,128)S(1)} %multiply_add_fusion.2), channel_id=1, source_target_pairs={{256,0},{272,16},{288,32},{304,48},{320,64},{336,80},{352,96},{368... | collective-permute-start | bytes 393224 | tf_op jit(solution)/shard_map/ppermute | solution.py:49
  97.8 10.4 %collective-permute-start.4 = (f32[2,128,128]{2,1,0:T(8,128)S(1)}, f32[2,128,128]{2,1,0:T(8,128)S(1)}, u32[]{:S(2)}, u32[]{:S(2)}) collective-permute-start(f32[2,128,128]{2,1,0:T(8,128)S(1)} %multiply_add_fusion.8), channel_id=1, source_target_pairs={{0,256},{16,272},{32,288},{48,304},{64,320},{80,336},{96,352},{112... | collective-permute-start | bytes 393224 | tf_op jit(solution)/shard_map/ppermute | solution.py:49
  100.3 9.3 %collective-permute-start.12 = (f32[2,128,128]{2,1,0:T(8,128)S(1)}, f32[2,128,128]{2,1,0:T(8,128)S(1)}, u32[]{:S(2)}, u32[]{:S(2)}) collective-permute-start(f32[2,128,128]{2,1,0:T(8,128)S(1)} %multiply_add_fusion.1), channel_id=1, source_target_pairs={{512,0},{528,16},{544,32},{560,48},{576,64},{592,80},{608,96},{624... | collective-permute-start | bytes 393224 | tf_op jit(solution)/shard_map/ppermute | solution.py:49
  108.2 12.2 %collective-permute-start.5 = (f32[2,128,128]{2,1,0:T(8,128)S(1)}, f32[2,128,128]{2,1,0:T(8,128)S(1)}, u32[]{:S(2)}, u32[]{:S(2)}) collective-permute-start(f32[2,128,128]{2,1,0:T(8,128)S(1)} %multiply_add_fusion.7), channel_id=1, source_target_pairs={{0,512},{16,528},{32,544},{48,560},{64,576},{80,592},{96,608},{112... | collective-permute-start | bytes 393224 | tf_op jit(solution)/shard_map/ppermute | solution.py:49
  109.6 12.8 %collective-permute-start.13 = (f32[2,128,128]{2,1,0:T(8,128)S(1)}, f32[2,128,128]{2,1,0:T(8,128)S(1)}, u32[]{:S(2)}, u32[]{:S(2)}) collective-permute-start(f32[2,128,128]{2,1,0:T(8,128)S(1)} %multiply_add_fusion), channel_id=1, source_target_pairs={{16,0},{32,16},{48,32},{64,48},{80,64},{96,80},{112,96},{128,112},... | collective-permute-start | bytes 393224 | tf_op jit(solution)/shard_map/ppermute | solution.py:58
  120.5 8.4 %collective-permute-start.6 = (f32[2,128,128]{2,1,0:T(8,128)S(1)}, f32[2,128,128]{2,1,0:T(8,128)S(1)}, u32[]{:S(2)}, u32[]{:S(2)}) collective-permute-start(f32[2,128,128]{2,1,0:T(8,128)S(1)} %multiply_add_fusion.6), channel_id=1, source_target_pairs={{0,16},{16,32},{32,48},{48,64},{64,80},{80,96},{96,112},{112,128},... | collective-permute-start | bytes 393224 | tf_op jit(solution)/shard_map/ppermute | solution.py:58

commit v2 on v1

--- a/solution.py
+++ b/solution.py
@@ -36,26 +36,37 @@
     return (weights, enter_w, leave_w)
 
 
-def decayed_scan(term, anchors, here, decays, group_len, count, forward):
-    total = term
-    shift = 1
-    while shift < count:
+def decayed_scan(term, anchors, here, decays, group_len, count, forward, radix):
+    def pull(value, shift):
         if forward:
             pairs = [(i, i + shift) for i in range(count - shift)]
-            other = jnp.maximum(here - shift, 0)
         else:
             pairs = [(i + shift, i) for i in range(count - shift)]
-            other = jnp.minimum(here + shift, count - 1)
-        incoming = lax.ppermute(total, "ctx", pairs)
-        same = (anchors[here] == anchors[other]).astype(jnp.float32)
-        factor = jnp.exp(-decays * float(group_len * shift)) * same
-        total = total + factor[:, None, None] * incoming
-        shift *= 2
-    if forward:
-        pairs = [(i, i + 1) for i in range(count - 1)]
-    else:
-        pairs = [(i + 1, i) for i in range(count - 1)]
-    return lax.ppermute(total, "ctx", pairs)
+        return lax.ppermute(value, "ctx", pairs)
+
+    def anchor_at(offset):
+        at = here - offset if forward else here + offset
+        return anchors[jnp.clip(at, 0, count - 1)]
+
+    mine = anchor_at(1)
+    total = None
+    for shift in range(1, min(radix, count - 1) + 1):
+        same = (anchor_at(shift) == mine).astype(jnp.float32)
+        factor = jnp.exp(-decays * float(group_len * (shift - 1))) * same
+        part = factor[:, None, None] * pull(term, shift)
+        total = part if total is None else total + part
+    window = radix
+    while window < count - 1:
+        previous = total
+        for step in range(1, radix):
+            shift = window * step
+            if shift >= count:
+                break
+            same = (anchor_at(shift + 1) == mine).astype(jnp.float32)
+            factor = jnp.exp(-decays * float(group_len * shift)) * same
+            total = total + factor[:, None, None] * pull(previous, shift)
+        window *= radix
+    return total
 
 
 def on_device(queries, keys, values, out_grad, decay_rate, doc_lengths):
@@ -90,10 +101,10 @@
     forward_term = jnp.einsum("jhd,jhe->hde", k_wide * leave_t, v_wide, precision=precise)
     backward_term = jnp.einsum("ihd,ihe->hde", q_wide * enter_t, g_wide, precision=precise)
     state_in = decayed_scan(
-        forward_term, end_segments, here, decay_rate, group_len, count, True
+        forward_term, end_segments, here, decay_rate, group_len, count, True, 4
     )
     state_next = decayed_scan(
-        backward_term, before_segments, here, decay_rate, group_len, count, False
+        backward_term, before_segments, here, decay_rate, group_len, count, False, 4
     )
     scores = (
         jnp.einsum("ihd,jhd->hij", q_rows, k_rows, preferred_element_type=jnp.float32) * weights

time: 133 us -> 139 us (1.045)
  waiting for transfers between devices: 29.8 us -> 14.3 us
  starting transfers between devices: 69.6 us -> 81.3 us
  between operations: 15.8 us -> 25.1 us
    ppermute x14 -> x20, starting transfers between devices: 50.8 us -> 62.5 us  [pull(): return lax.ppermute(value, 'ctx', pairs)]
    all_to_all x1, waiting for transfers between devices: 9.17 us -> 0.01 us  [in_one_piece(): lax.all_to_all(both, axis, split_axis=split_dim, concat_axis=concat_dim,...]
    ppermute x14 -> x20, waiting for transfers between devices: 20.6 us -> 14.2 us  [pull(): return lax.ppermute(value, 'ctx', pairs)]
  transfers between devices with their start and end apart: 15 -> 21, of which waited for: 9 -> 6; matrix products, arithmetic and copies ran while one was open for 5% -> 6% of each run, Pallas kernels for 0% -> 0%
where the time goes in v2:
time: 139 us; the launch traced here: 138 us
  starting transfers between devices  81.3 us (58%)
  between operations  25.1 us (18%)
  waiting for transfers between devices  14.3 us (10%)
  local copies, waits for them, and re-layouts  10.7 us (8%)
  matrix products  3.58 us (3%)
  other arithmetic  3.15 us (2%)
    ppermute x20, starting transfers between devices, pull(): return lax.ppermute(value, 'ctx', pairs)  62.5 us
    all_to_all x1, starting transfers between devices, in_one_piece(): lax.all_to_all(both, axis, split_axis=split_dim, concat_axis=concat_dim,...  18.9 us
    ppermute x20, waiting for transfers between devices, pull(): return lax.ppermute(value, 'ctx', pairs)  14.2 us
    unnamed x18, local copies, waits for them, and re-layouts  7.12 us
  transfers between devices with their start and end apart: 21, of which 6 were waited for; matrix products, arithmetic and copies ran while one was open for 6% of the time, Pallas kernels for 0%

profile of v2, /device:TPU:40, one launch (start us, length us, event | category | flops | bytes accessed | tf_op | source)
XLA Modules:
  0.0 138.1 jit_solution(7556434341874839207)
XLA Ops:
  0.6 1.0 copy.145
  1.7 0.9 copy-done.1
  2.5 0.9 copy-done.2
  3.5 1.1 copy.103
  4.6 18.9 %all-to-all-start = ((bf16[16,32,512]{2,0,1:T(8,128)(2,1)}), bf16[16,32,512]{2,0,1:T(8,128)(2,1)S(1)}, u32[]{:S(2)}, u32[]{:S(2)}) async-start(bf16[16,32,512]{2,0,1:T(8,128)(2,1)} %copy.103), calls=%async_computation | async-start | bytes 1048576 | tf_op jit(solution)/shard_map/all_to_all | solution.py:12
  51.2 1.2 compare_convert_fusion
  53.9 5.7 %collective-permute-start.13 = (f32[2,128,128]{2,1,0:T(8,128)S(1)}, f32[2,128,128]{2,1,0:T(8,128)S(1)}, u32[]{:S(2)}, u32[]{:S(2)}) collective-permute-start(f32[2,128,128]{2,1,0:T(8,128)S(1)} %fusion.14), channel_id=1, source_target_pairs={{64,0},{80,16},{96,32},{112,48},{128,64},{144,80},{160,96},{176,11... | collective-permute-start | bytes 393224 | tf_op jit(solution)/shard_map/ppermute | solution.py:45
  59.6 1.9 %collective-permute-start.12 = (f32[2,128,128]{2,1,0:T(8,128)S(1)}, f32[2,128,128]{2,1,0:T(8,128)S(1)}, u32[]{:S(2)}, u32[]{:S(2)}) collective-permute-start(f32[2,128,128]{2,1,0:T(8,128)S(1)} %fusion.14), channel_id=1, source_target_pairs={{48,0},{64,16},{80,32},{96,48},{112,64},{128,80},{144,96},{160,112... | collective-permute-start | bytes 393224 | tf_op jit(solution)/shard_map/ppermute | solution.py:45
  61.6 3.9 %collective-permute-start.11 = (f32[2,128,128]{2,1,0:T(8,128)S(1)}, f32[2,128,128]{2,1,0:T(8,128)S(1)}, u32[]{:S(2)}, u32[]{:S(2)}) collective-permute-start(f32[2,128,128]{2,1,0:T(8,128)S(1)} %fusion.14), channel_id=1, source_target_pairs={{32,0},{48,16},{64,32},{80,48},{96,64},{112,80},{128,96},{144,112}... | collective-permute-start | bytes 393224 | tf_op jit(solution)/shard_map/ppermute | solution.py:45
  65.5 2.4 %collective-permute-start.10 = (f32[2,128,128]{2,1,0:T(8,128)S(1)}, f32[2,128,128]{2,1,0:T(8,128)S(1)}, u32[]{:S(2)}, u32[]{:S(2)}) collective-permute-start(f32[2,128,128]{2,1,0:T(8,128)S(1)} %fusion.14), channel_id=1, source_target_pairs={{16,0},{32,16},{48,32},{64,48},{80,64},{96,80},{112,96},{128,112},... | collective-permute-start | bytes 393224 | tf_op jit(solution)/shard_map/ppermute | solution.py:45
  68.9 4.0 %collective-permute-start.3 = (f32[2,128,128]{2,1,0:T(8,128)S(1)}, f32[2,128,128]{2,1,0:T(8,128)S(1)}, u32[]{:S(2)}, u32[]{:S(2)}) collective-permute-start(f32[2,128,128]{2,1,0:T(8,128)S(1)} %fusion.17), channel_id=1, source_target_pairs={{0,64},{16,80},{32,96},{48,112},{64,128},{80,144},{96,160},{112,17... | collective-permute-start | bytes 393224 | tf_op jit(solution)/shard_map/ppermute | solution.py:45
  73.5 1.9 %collective-permute-start.2 = (f32[2,128,128]{2,1,0:T(8,128)S(1)}, f32[2,128,128]{2,1,0:T(8,128)S(1)}, u32[]{:S(2)}, u32[]{:S(2)}) collective-permute-start(f32[2,128,128]{2,1,0:T(8,128)S(1)} %fusion.17), channel_id=1, source_target_pairs={{0,48},{16,64},{32,80},{48,96},{64,112},{80,128},{96,144},{112,160... | collective-permute-start | bytes 393224 | tf_op jit(solution)/shard_map/ppermute | solution.py:45
  75.4 3.6 %collective-permute-start.1 = (f32[2,128,128]{2,1,0:T(8,128)S(1)}, f32[2,128,128]{2,1,0:T(8,128)S(1)}, u32[]{:S(2)}, u32[]{:S(2)}) collective-permute-start(f32[2,128,128]{2,1,0:T(8,128)S(1)} %fusion.17), channel_id=1, source_target_pairs={{0,32},{16,48},{32,64},{48,80},{64,96},{80,112},{96,128},{112,144}... | collective-permute-start | bytes 393224 | tf_op jit(solution)/shard_map/ppermute | solution.py:45
  79.0 2.8 %collective-permute-start = (f32[2,128,128]{2,1,0:T(8,128)S(1)}, f32[2,128,128]{2,1,0:T(8,128)S(1)}, u32[]{:S(2)}, u32[]{:S(2)}) collective-permute-start(f32[2,128,128]{2,1,0:T(8,128)S(1)} %fusion.17), channel_id=1, source_target_pairs={{0,16},{16,32},{32,48},{48,64},{64,80},{80,96},{96,112},{112,128},... | collective-permute-start | bytes 393224 | tf_op jit(solution)/shard_map/ppermute | solution.py:45
  82.8 1.6 %collective-permute-done.1 = f32[2,128,128]{2,1,0:T(8,128)S(1)} collective-permute-done((f32[2,128,128]{2,1,0:T(8,128)S(1)}, f32[2,128,128]{2,1,0:T(8,128)S(1)}, u32[]{:S(2)}, u32[]{:S(2)}) %collective-permute-start.1) | collective-permute-done | bytes 131104 | tf_op jit(solution)/shard_map/ppermute | solution.py:45
  84.4 3.5 %collective-permute-done = f32[2,128,128]{2,1,0:T(8,128)S(1)} collective-permute-done((f32[2,128,128]{2,1,0:T(8,128)S(1)}, f32[2,128,128]{2,1,0:T(8,128)S(1)}, u32[]{:S(2)}, u32[]{:S(2)}) %collective-permute-start) | collective-permute-done | bytes 131104 | tf_op jit(solution)/shard_map/ppermute | solution.py:45
  88.0 2.9 %collective-permute-start.16 = (f32[2,128,128]{2,1,0:T(8,128)S(1)}, f32[2,128,128]{2,1,0:T(8,128)S(1)}, u32[]{:S(2)}, u32[]{:S(2)}) collective-permute-start(f32[2,128,128]{2,1,0:T(8,128)S(1)} %get-tuple-element.54), channel_id=1, source_target_pairs={{192,0},{208,16},{224,32},{240,48},{256,64},{272,80},{288,96},{304... | collective-permute-start | bytes 393224 | tf_op jit(solution)/shard_map/ppermute | solution.py:45
  91.0 2.6 %collective-permute-start.15 = (f32[2,128,128]{2,1,0:T(8,128)S(1)}, f32[2,128,128]{2,1,0:T(8,128)S(1)}, u32[]{:S(2)}, u32[]{:S(2)}) collective-permute-start(f32[2,128,128]{2,1,0:T(8,128)S(1)} %get-tuple-element.54), channel_id=1, source_target_pairs={{128,0},{144,16},{160,32},{176,48},{192,64},{208,80},{224,96},{240... | collective-permute-start | bytes 393224 | tf_op jit(solution)/shard_map/ppermute | solution.py:45
  93.5 4.8 %collective-permute-start.14 = (f32[2,128,128]{2,1,0:T(8,128)S(1)}, f32[2,128,128]{2,1,0:T(8,128)S(1)}, u32[]{:S(2)}, u32[]{:S(2)}) collective-permute-start(f32[2,128,128]{2,1,0:T(8,128)S(1)} %get-tuple-element.54), channel_id=1, source_target_pairs={{64,0},{80,16},{96,32},{112,48},{128,64},{144,80},{160,96},{176,11... | collective-permute-start | bytes 393224 | tf_op jit(solution)/shard_map/ppermute | solution.py:45
  98.5 3.5 %collective-permute-start.6 = (f32[2,128,128]{2,1,0:T(8,128)S(1)}, f32[2,128,128]{2,1,0:T(8,128)S(1)}, u32[]{:S(2)}, u32[]{:S(2)}) collective-permute-start(f32[2,128,128]{2,1,0:T(8,128)S(1)} %get-tuple-element.55), channel_id=1, source_target_pairs={{0,192},{16,208},{32,224},{48,240},{64,256},{80,272},{96,288},{112... | collective-permute-start | bytes 393224 | tf_op jit(solution)/shard_map/ppermute | solution.py:45
  102.0 2.4 %collective-permute-start.5 = (f32[2,128,128]{2,1,0:T(8,128)S(1)}, f32[2,128,128]{2,1,0:T(8,128)S(1)}, u32[]{:S(2)}, u32[]{:S(2)}) collective-permute-start(f32[2,128,128]{2,1,0:T(8,128)S(1)} %get-tuple-element.55), channel_id=1, source_target_pairs={{0,128},{16,144},{32,160},{48,176},{64,192},{80,208},{96,224},{112... | collective-permute-start | bytes 393224 | tf_op jit(solution)/shard_map/ppermute | solution.py:45
  104.4 5.9 %collective-permute-start.4 = (f32[2,128,128]{2,1,0:T(8,128)S(1)}, f32[2,128,128]{2,1,0:T(8,128)S(1)}, u32[]{:S(2)}, u32[]{:S(2)}) collective-permute-start(f32[2,128,128]{2,1,0:T(8,128)S(1)} %get-tuple-element.55), channel_id=1, source_target_pairs={{0,64},{16,80},{32,96},{48,112},{64,128},{80,144},{96,160},{112,17... | collective-permute-start | bytes 393224 | tf_op jit(solution)/shard_map/ppermute | solution.py:45
  111.1 4.2 %collective-permute-start.18 = (f32[2,128,128]{2,1,0:T(8,128)S(1)}, f32[2,128,128]{2,1,0:T(8,128)S(1)}, u32[]{:S(2)}, u32[]{:S(2)}) collective-permute-start(f32[2,128,128]{2,1,0:T(8,128)S(1)} %multiply_add_fusion.1), channel_id=1, source_target_pairs={{512,0},{528,16},{544,32},{560,48},{576,64},{592,80},{608,96},{624... | collective-permute-start | bytes 393224 | tf_op jit(solution)/shard_map/ppermute | solution.py:45
  115.3 2.1 %collective-permute-start.17 = (f32[2,128,128]{2,1,0:T(8,128)S(1)}, f32[2,128,128]{2,1,0:T(8,128)S(1)}, u32[]{:S(2)}, u32[]{:S(2)}) collective-permute-start(f32[2,128,128]{2,1,0:T(8,128)S(1)} %multiply_add_fusion.1), channel_id=1, source_target_pairs={{256,0},{272,16},{288,32},{304,48},{320,64},{336,80},{352,96},{368... | collective-permute-start | bytes 393224 | tf_op jit(solution)/shard_map/ppermute | solution.py:45
  118.2 1.3 collective-permute-start.8
  119.5 5.3 %collective-permute-start.7 = (f32[2,128,128]{2,1,0:T(8,128)S(1)}, f32[2,128,128]{2,1,0:T(8,128)S(1)}, u32[]{:S(2)}, u32[]{:S(2)}) collective-permute-start(f32[2,128,128]{2,1,0:T(8,128)S(1)} %multiply_add_fusion.4), channel_id=1, source_target_pairs={{0,256},{16,272},{32,288},{48,304},{64,320},{80,336},{96,352},{112... | collective-permute-start | bytes 393224 | tf_op jit(solution)/shard_map/ppermute | solution.py:45
  124.8 0.8 collective-permute-done.17
  126.1 0.8 copy.128
  126.9 3.2 %collective-permute-done.8 = f32[2,128,128]{2,1,0:T(8,128)S(1)} collective-permute-done((f32[2,128,128]{2,1,0:T(8,128)S(1)}, f32[2,128,128]{2,1,0:T(8,128)S(1)}, u32[]{:S(2)}, u32[]{:S(2)}) %collective-permute-start.8) | collective-permute-done | bytes 131104 | tf_op jit(solution)/shard_map/ppermute | solution.py:45
  130.1 4.4 %collective-permute-done.7 = f32[2,128,128]{2,1,0:T(8,128)S(1)} collective-permute-done((f32[2,128,128]{2,1,0:T(8,128)S(1)}, f32[2,128,128]{2,1,0:T(8,128)S(1)}, u32[]{:S(2)}, u32[]{:S(2)}) %collective-permute-start.7) | collective-permute-done | bytes 131104 | tf_op jit(solution)/shard_map/ppermute | solution.py:45
  135.0 0.8 copy.125
  136.2 0.8 copy.127
  (67 shorter events, 12.2 us)
Async XLA Ops:
  0.6 1.0 copy-start
  1.6 0.9 copy-start.1
  2.5 0.9 copy-start.2
  4.6 48.7 %all-to-all-start = ((bf16[16,32,512]{2,0,1:T(8,128)(2,1)}), bf16[16,32,512]{2,0,1:T(8,128)(2,1)S(1)}, u32[]{:S(2)}, u32[]{:S(2)}) async-start(bf16[16,32,512]{2,0,1:T(8,128)(2,1)} %copy.103), calls=%async_computation | async-start | bytes 1048576 | tf_op jit(solution)/shard_map/all_to_all | solution.py:12
  23.6 0.7 copy-start.4
  52.5 0.7 copy-start.3
  53.9 19.6 %collective-permute-start.13 = (f32[2,128,128]{2,1,0:T(8,128)S(1)}, f32[2,128,128]{2,1,0:T(8,128)S(1)}, u32[]{:S(2)}, u32[]{:S(2)}) collective-permute-start(f32[2,128,128]{2,1,0:T(8,128)S(1)} %fusion.14), channel_id=1, source_target_pairs={{64,0},{80,16},{96,32},{112,48},{128,64},{144,80},{160,96},{176,11... | collective-permute-start | bytes 393224 | tf_op jit(solution)/shard_map/ppermute | solution.py:45
  59.6 15.8 %collective-permute-start.12 = (f32[2,128,128]{2,1,0:T(8,128)S(1)}, f32[2,128,128]{2,1,0:T(8,128)S(1)}, u32[]{:S(2)}, u32[]{:S(2)}) collective-permute-start(f32[2,128,128]{2,1,0:T(8,128)S(1)} %fusion.14), channel_id=1, source_target_pairs={{48,0},{64,16},{80,32},{96,48},{112,64},{128,80},{144,96},{160,112... | collective-permute-start | bytes 393224 | tf_op jit(solution)/shard_map/ppermute | solution.py:45
  61.6 17.5 %collective-permute-start.11 = (f32[2,128,128]{2,1,0:T(8,128)S(1)}, f32[2,128,128]{2,1,0:T(8,128)S(1)}, u32[]{:S(2)}, u32[]{:S(2)}) collective-permute-start(f32[2,128,128]{2,1,0:T(8,128)S(1)} %fusion.14), channel_id=1, source_target_pairs={{32,0},{48,16},{64,32},{80,48},{96,64},{112,80},{128,96},{144,112}... | collective-permute-start | bytes 393224 | tf_op jit(solution)/shard_map/ppermute | solution.py:45
  65.5 16.6 %collective-permute-start.10 = (f32[2,128,128]{2,1,0:T(8,128)S(1)}, f32[2,128,128]{2,1,0:T(8,128)S(1)}, u32[]{:S(2)}, u32[]{:S(2)}) collective-permute-start(f32[2,128,128]{2,1,0:T(8,128)S(1)} %fusion.14), channel_id=1, source_target_pairs={{16,0},{32,16},{48,32},{64,48},{80,64},{96,80},{112,96},{128,112},... | collective-permute-start | bytes 393224 | tf_op jit(solution)/shard_map/ppermute | solution.py:45
  68.9 13.2 %collective-permute-start.3 = (f32[2,128,128]{2,1,0:T(8,128)S(1)}, f32[2,128,128]{2,1,0:T(8,128)S(1)}, u32[]{:S(2)}, u32[]{:S(2)}) collective-permute-start(f32[2,128,128]{2,1,0:T(8,128)S(1)} %fusion.17), channel_id=1, source_target_pairs={{0,64},{16,80},{32,96},{48,112},{64,128},{80,144},{96,160},{112,17... | collective-permute-start | bytes 393224 | tf_op jit(solution)/shard_map/ppermute | solution.py:45
  73.5 9.3 %collective-permute-start.2 = (f32[2,128,128]{2,1,0:T(8,128)S(1)}, f32[2,128,128]{2,1,0:T(8,128)S(1)}, u32[]{:S(2)}, u32[]{:S(2)}) collective-permute-start(f32[2,128,128]{2,1,0:T(8,128)S(1)} %fusion.17), channel_id=1, source_target_pairs={{0,48},{16,64},{32,80},{48,96},{64,112},{80,128},{96,144},{112,160... | collective-permute-start | bytes 393224 | tf_op jit(solution)/shard_map/ppermute | solution.py:45
  75.4 9.0 %collective-permute-start.1 = (f32[2,128,128]{2,1,0:T(8,128)S(1)}, f32[2,128,128]{2,1,0:T(8,128)S(1)}, u32[]{:S(2)}, u32[]{:S(2)}) collective-permute-start(f32[2,128,128]{2,1,0:T(8,128)S(1)} %fusion.17), channel_id=1, source_target_pairs={{0,32},{16,48},{32,64},{48,80},{64,96},{80,112},{96,128},{112,144}... | collective-permute-start | bytes 393224 | tf_op jit(solution)/shard_map/ppermute | solution.py:45
  79.0 8.9 %collective-permute-start = (f32[2,128,128]{2,1,0:T(8,128)S(1)}, f32[2,128,128]{2,1,0:T(8,128)S(1)}, u32[]{:S(2)}, u32[]{:S(2)}) collective-permute-start(f32[2,128,128]{2,1,0:T(8,128)S(1)} %fusion.17), channel_id=1, source_target_pairs={{0,16},{16,32},{32,48},{48,64},{64,80},{80,96},{96,112},{112,128},... | collective-permute-start | bytes 393224 | tf_op jit(solution)/shard_map/ppermute | solution.py:45
  88.0 16.4 %collective-permute-start.16 = (f32[2,128,128]{2,1,0:T(8,128)S(1)}, f32[2,128,128]{2,1,0:T(8,128)S(1)}, u32[]{:S(2)}, u32[]{:S(2)}) collective-permute-start(f32[2,128,128]{2,1,0:T(8,128)S(1)} %get-tuple-element.54), channel_id=1, source_target_pairs={{192,0},{208,16},{224,32},{240,48},{256,64},{272,80},{288,96},{304... | collective-permute-start | bytes 393224 | tf_op jit(solution)/shard_map/ppermute | solution.py:45
  91.0 19.3 %collective-permute-start.15 = (f32[2,128,128]{2,1,0:T(8,128)S(1)}, f32[2,128,128]{2,1,0:T(8,128)S(1)}, u32[]{:S(2)}, u32[]{:S(2)}) collective-permute-start(f32[2,128,128]{2,1,0:T(8,128)S(1)} %get-tuple-element.54), channel_id=1, source_target_pairs={{128,0},{144,16},{160,32},{176,48},{192,64},{208,80},{224,96},{240... | collective-permute-start | bytes 393224 | tf_op jit(solution)/shard_map/ppermute | solution.py:45
  93.5 16.8 %collective-permute-start.14 = (f32[2,128,128]{2,1,0:T(8,128)S(1)}, f32[2,128,128]{2,1,0:T(8,128)S(1)}, u32[]{:S(2)}, u32[]{:S(2)}) collective-permute-start(f32[2,128,128]{2,1,0:T(8,128)S(1)} %get-tuple-element.54), channel_id=1, source_target_pairs={{64,0},{80,16},{96,32},{112,48},{128,64},{144,80},{160,96},{176,11... | collective-permute-start | bytes 393224 | tf_op jit(solution)/shard_map/ppermute | solution.py:45
  98.5 16.8 %collective-permute-start.6 = (f32[2,128,128]{2,1,0:T(8,128)S(1)}, f32[2,128,128]{2,1,0:T(8,128)S(1)}, u32[]{:S(2)}, u32[]{:S(2)}) collective-permute-start(f32[2,128,128]{2,1,0:T(8,128)S(1)} %get-tuple-element.55), channel_id=1, source_target_pairs={{0,192},{16,208},{32,224},{48,240},{64,256},{80,272},{96,288},{112... | collective-permute-start | bytes 393224 | tf_op jit(solution)/shard_map/ppermute | solution.py:45
  102.0 15.4 %collective-permute-start.5 = (f32[2,128,128]{2,1,0:T(8,128)S(1)}, f32[2,128,128]{2,1,0:T(8,128)S(1)}, u32[]{:S(2)}, u32[]{:S(2)}) collective-permute-start(f32[2,128,128]{2,1,0:T(8,128)S(1)} %get-tuple-element.55), channel_id=1, source_target_pairs={{0,128},{16,144},{32,160},{48,176},{64,192},{80,208},{96,224},{112... | collective-permute-start | bytes 393224 | tf_op jit(solution)/shard_map/ppermute | solution.py:45
  104.4 13.0 %collective-permute-start.4 = (f32[2,128,128]{2,1,0:T(8,128)S(1)}, f32[2,128,128]{2,1,0:T(8,128)S(1)}, u32[]{:S(2)}, u32[]{:S(2)}) collective-permute-start(f32[2,128,128]{2,1,0:T(8,128)S(1)} %get-tuple-element.55), channel_id=1, source_target_pairs={{0,64},{16,80},{32,96},{48,112},{64,128},{80,144},{96,160},{112,17... | collective-permute-start | bytes 393224 | tf_op jit(solution)/shard_map/ppermute | solution.py:45
  110.4 9.1 %collective-permute-start.19 = (f32[2,128,128]{2,1,0:T(8,128)S(1)}, f32[2,128,128]{2,1,0:T(8,128)S(1)}, u32[]{:S(2)}, u32[]{:S(2)}) collective-permute-start(f32[2,128,128]{2,1,0:T(8,128)S(1)} %multiply_add_fusion.1), channel_id=1, source_target_pairs={{768,0},{784,16},{800,32},{816,48},{832,64},{848,80},{864,96},{880... | collective-permute-start | bytes 393224 | tf_op jit(solution)/shard_map/ppermute | solution.py:45
  111.1 13.7 %collective-permute-start.18 = (f32[2,128,128]{2,1,0:T(8,128)S(1)}, f32[2,128,128]{2,1,0:T(8,128)S(1)}, u32[]{:S(2)}, u32[]{:S(2)}) collective-permute-start(f32[2,128,128]{2,1,0:T(8,128)S(1)} %multiply_add_fusion.1), channel_id=1, source_target_pairs={{512,0},{528,16},{544,32},{560,48},{576,64},{592,80},{608,96},{624... | collective-permute-start | bytes 393224 | tf_op jit(solution)/shard_map/ppermute | solution.py:45
  115.3 10.3 %collective-permute-start.17 = (f32[2,128,128]{2,1,0:T(8,128)S(1)}, f32[2,128,128]{2,1,0:T(8,128)S(1)}, u32[]{:S(2)}, u32[]{:S(2)}) collective-permute-start(f32[2,128,128]{2,1,0:T(8,128)S(1)} %multiply_add_fusion.1), channel_id=1, source_target_pairs={{256,0},{272,16},{288,32},{304,48},{320,64},{336,80},{352,96},{368... | collective-permute-start | bytes 393224 | tf_op jit(solution)/shard_map/ppermute | solution.py:45
  117.6 9.3 %collective-permute-start.9 = (f32[2,128,128]{2,1,0:T(8,128)S(1)}, f32[2,128,128]{2,1,0:T(8,128)S(1)}, u32[]{:S(2)}, u32[]{:S(2)}) collective-permute-start(f32[2,128,128]{2,1,0:T(8,128)S(1)} %multiply_add_fusion.4), channel_id=1, source_target_pairs={{0,768},{16,784},{32,800},{48,816},{64,832},{80,848},{96,864},{112... | collective-permute-start | bytes 393224 | tf_op jit(solution)/shard_map/ppermute | solution.py:45
  118.2 11.9 %collective-permute-start.8 = (f32[2,128,128]{2,1,0:T(8,128)S(1)}, f32[2,128,128]{2,1,0:T(8,128)S(1)}, u32[]{:S(2)}, u32[]{:S(2)}) collective-permute-start(f32[2,128,128]{2,1,0:T(8,128)S(1)} %multiply_add_fusion.4), channel_id=1, source_target_pairs={{0,512},{16,528},{32,544},{48,560},{64,576},{80,592},{96,608},{112... | collective-permute-start | bytes 393224 | tf_op jit(solution)/shard_map/ppermute | solution.py:45
  119.5 15.0 %collective-permute-start.7 = (f32[2,128,128]{2,1,0:T(8,128)S(1)}, f32[2,128,128]{2,1,0:T(8,128)S(1)}, u32[]{:S(2)}, u32[]{:S(2)}) collective-permute-start(f32[2,128,128]{2,1,0:T(8,128)S(1)} %multiply_add_fusion.4), channel_id=1, source_target_pairs={{0,256},{16,272},{32,288},{48,304},{64,320},{80,336},{96,352},{112... | collective-permute-start | bytes 393224 | tf_op jit(solution)/shard_map/ppermute | solution.py:45

commit v3 on v1

--- a/solution.py
+++ b/solution.py
@@ -36,26 +36,54 @@
     return (weights, enter_w, leave_w)
 
 
-def decayed_scan(term, anchors, here, decays, group_len, count, forward):
-    total = term
+def butterfly_scan(forward_term, backward_term, end_segments, before_segments, here, decays,
+                   group_len, count):
+    def clipped(table, index):
+        return table[jnp.clip(index, 0, count - 1)]
+
+    def decay(groups):
+        return jnp.exp(-decays * (jnp.asarray(groups) * group_len).astype(jnp.float32))
+
+    ahead = jnp.zeros_like(forward_term)
+    behind = jnp.zeros_like(backward_term)
+    total_f, total_b = forward_term, backward_term
     shift = 1
     while shift < count:
-        if forward:
-            pairs = [(i, i + shift) for i in range(count - shift)]
-            other = jnp.maximum(here - shift, 0)
+        last = shift * 2 >= count
+        upper = (here // shift) % 2 == 1
+        start = (here // shift) * shift
+        other = jnp.where(upper, start - shift, start + shift)
+        pairs = [(i, i ^ shift) for i in range(count)]
+        if last:
+            got = lax.ppermute(jnp.where(upper, total_b, total_f), "ctx", pairs)
+            got_f = got_b = got
         else:
-            pairs = [(i + shift, i) for i in range(count - shift)]
-            other = jnp.minimum(here + shift, count - 1)
-        incoming = lax.ppermute(total, "ctx", pairs)
-        same = (anchors[here] == anchors[other]).astype(jnp.float32)
-        factor = jnp.exp(-decays * float(group_len * shift)) * same
-        total = total + factor[:, None, None] * incoming
+            got = lax.ppermute(jnp.stack([total_f, total_b]), "ctx", pairs)
+            got_f, got_b = got[0], got[1]
+        up = upper.astype(jnp.float32)
+        to_ahead = decay(here - start) * (
+            clipped(end_segments, start - 1) == clipped(end_segments, here - 1)
+        ).astype(jnp.float32)
+        ahead = ahead + (up * to_ahead)[:, None, None] * got_f
+        to_behind = decay(start + shift - 1 - here) * (
+            clipped(before_segments, start + shift) == clipped(before_segments, here + 1)
+        ).astype(jnp.float32)
+        behind = behind + ((1.0 - up) * to_behind)[:, None, None] * got_b
+        if not last:
+            joined_f = decay(shift) * (
+                clipped(end_segments, start + shift - 1) == clipped(end_segments, other + shift - 1)
+            ).astype(jnp.float32)
+            joined_b = decay(shift) * (
+                clipped(before_segments, start) == clipped(before_segments, other)
+            ).astype(jnp.float32)
+            total_f = jnp.where(upper, 1.0, joined_f)[:, None, None] * total_f + jnp.where(
+                upper, joined_f, 1.0
+            )[:, None, None] * got_f
+            total_b = jnp.where(upper, joined_b, 1.0)[:, None, None] * total_b + jnp.where(
+                upper, 1.0, joined_b
+            )[:, None, None] * got_b
         shift *= 2
-    if forward:
-        pairs = [(i, i + 1) for i in range(count - 1)]
-    else:
-        pairs = [(i + 1, i) for i in range(count - 1)]
-    return lax.ppermute(total, "ctx", pairs)
+    return ahead, behind
 
 
 def on_device(queries, keys, values, out_grad, decay_rate, doc_lengths):
@@ -89,11 +117,9 @@
     leave_t = leave_w.T[:, :, None]
     forward_term = jnp.einsum("jhd,jhe->hde", k_wide * leave_t, v_wide, precision=precise)
     backward_term = jnp.einsum("ihd,ihe->hde", q_wide * enter_t, g_wide, precision=precise)
-    state_in = decayed_scan(
-        forward_term, end_segments, here, decay_rate, group_len, count, True
-    )
-    state_next = decayed_scan(
-        backward_term, before_segments, here, decay_rate, group_len, count, False
+    state_in, state_next = butterfly_scan(
+        forward_term, backward_term, end_segments, before_segments, here, decay_rate, group_len,
+        count,
     )
     scores = (
         jnp.einsum("ihd,jhd->hij", q_rows, k_rows, preferred_element_type=jnp.float32) * weights

time: 133 us -> 137 us (1.030)
  the two profiles are of different devices: /device:TPU:40 before, /device:TPU:57 now
where the time goes in v3:
time: 137 us; the launch traced here: 136 us
  starting transfers between devices  47.2 us (34%)
  waiting for transfers between devices  44.6 us (33%)
  between operations  26.3 us (19%)
  local copies, waits for them, and re-layouts  10.8 us (8%)
  matrix products  3.58 us (3%)
  other arithmetic  3.48 us (3%)
    ppermute x5, waiting for transfers between devices, butterfly_scan(): got = lax.ppermute(jnp.stack([total_f, total_b]), 'ctx', pairs)  28.1 us
    ppermute x5, starting transfers between devices, butterfly_scan(): got = lax.ppermute(jnp.stack([total_f, total_b]), 'ctx', pairs)  23.6 us
    all_to_all x1, starting transfers between devices, in_one_piece(): lax.all_to_all(both, axis, split_axis=split_dim, concat_axis=concat_dim,...  18.6 us
    ppermute x1, waiting for transfers between devices, butterfly_scan(): got = lax.ppermute(jnp.where(upper, total_b, total_f), 'ctx', pairs)  8.77 us
    all_to_all x1, waiting for transfers between devices, in_one_piece(): lax.all_to_all(both, axis, split_axis=split_dim, concat_axis=concat_dim,...  7.78 us
    unnamed x18, local copies, waits for them, and re-layouts  7.12 us
    ppermute x1, starting transfers between devices, butterfly_scan(): got = lax.ppermute(jnp.where(upper, total_b, total_f), 'ctx', pairs)  5.02 us
  transfers between devices with their start and end apart: 7, of which 6 were waited for; matrix products, arithmetic and copies ran while one was open for 4% of the time, Pallas kernels for 0%

profile of v3, /device:TPU:57, one launch (start us, length us, event | category | flops | bytes accessed | tf_op | source)
XLA Modules:
  0.0 136.0 jit_solution(15666970659042642366)
XLA Ops:
  0.6 1.0 copy.145
  1.7 0.9 copy-done.1
  2.5 0.9 copy-done.2
  3.5 1.1 copy.103
  4.6 18.6 %all-to-all-start = ((bf16[16,32,512]{2,0,1:T(8,128)(2,1)}), bf16[16,32,512]{2,0,1:T(8,128)(2,1)S(1)}, u32[]{:S(2)}, u32[]{:S(2)}) async-start(bf16[16,32,512]{2,0,1:T(8,128)(2,1)} %copy.103), calls=%async_computation | async-start | bytes 1048576 | tf_op jit(solution)/shard_map/all_to_all | solution.py:12
  23.5 0.6 copy-done.4
  24.4 0.7 fusion.46
  26.4 0.8 fusion.47
  35.0 0.6 slice.33
  35.6 0.7 fusion.39
  36.3 1.2 compare_convert_fusion.2
  37.5 0.6 copy-done.3
  38.3 7.8 %all-to-all-done = bf16[16,32,512]{2,0,1:T(8,128)(2,1)S(1)} async-done(((bf16[16,32,512]{2,0,1:T(8,128)(2,1)}), bf16[16,32,512]{2,0,1:T(8,128)(2,1)S(1)}, u32[]{:S(2)}, u32[]{:S(2)}) %all-to-all-start) | async-done | bytes 524320 | tf_op jit(solution)/shard_map/all_to_all | solution.py:12
  46.1 0.5 fusion.17
  46.6 0.5 fusion.14
  47.2 9.1 %collective-permute-start = (f32[2,2,128,128]{3,2,1,0:T(8,128)S(1)}, f32[2,2,128,128]{3,2,1,0:T(8,128)S(1)}, u32[]{:S(2)}, u32[]{:S(2)}) collective-permute-start(f32[2,2,128,128]{3,2,1,0:T(8,128)S(1)} %pad_maximum_fusion.1), channel_id=1, source_target_pairs={{0,16},{16,0},{32,48},{48,32},{64,80},{80,64},{96,112},{112,96},{1... | collective-permute-start | bytes 786440 | tf_op jit(solution)/shard_map/ppermute | solution.py:61
  72.4 3.1 %collective-permute-start.1 = (f32[2,2,128,128]{3,2,1,0:T(8,128)S(1)}, f32[2,2,128,128]{3,2,1,0:T(8,128)S(1)}, u32[]{:S(2)}, u32[]{:S(2)}) collective-permute-start(f32[2,2,128,128]{3,2,1,0:T(8,128)S(1)} %pad_maximum_fusion.2), channel_id=1, source_target_pairs={{0,32},{16,48},{32,0},{48,16},{64,96},{80,112},{96,64},{112,80},{1... | collective-permute-start | bytes 786440 | tf_op jit(solution)/shard_map/ppermute | solution.py:61
  75.7 6.5 %collective-permute-done.1 = f32[2,2,128,128]{3,2,1,0:T(8,128)S(1)} collective-permute-done((f32[2,2,128,128]{3,2,1,0:T(8,128)S(1)}, f32[2,2,128,128]{3,2,1,0:T(8,128)S(1)}, u32[]{:S(2)}, u32[]{:S(2)}) %collective-permute-start.1) | collective-permute-done | bytes 262176 | tf_op jit(solution)/shard_map/ppermute | solution.py:61
  82.4 4.7 %collective-permute-start.2 = (f32[2,2,128,128]{3,2,1,0:T(8,128)S(1)}, f32[2,2,128,128]{3,2,1,0:T(8,128)S(1)}, u32[]{:S(2)}, u32[]{:S(2)}) collective-permute-start(f32[2,2,128,128]{3,2,1,0:T(8,128)S(1)} %pad_maximum_fusion.3), channel_id=1, source_target_pairs={{0,64},{16,80},{32,96},{48,112},{64,0},{80,16},{96,32},{112,48},{1... | collective-permute-start | bytes 786440 | tf_op jit(solution)/shard_map/ppermute | solution.py:61
  87.3 5.5 %collective-permute-done.2 = f32[2,2,128,128]{3,2,1,0:T(8,128)S(1)} collective-permute-done((f32[2,2,128,128]{3,2,1,0:T(8,128)S(1)}, f32[2,2,128,128]{3,2,1,0:T(8,128)S(1)}, u32[]{:S(2)}, u32[]{:S(2)}) %collective-permute-start.2) | collective-permute-done | bytes 262176 | tf_op jit(solution)/shard_map/ppermute | solution.py:61
  93.0 3.0 %collective-permute-start.3 = (f32[2,2,128,128]{3,2,1,0:T(8,128)S(1)}, f32[2,2,128,128]{3,2,1,0:T(8,128)S(1)}, u32[]{:S(2)}, u32[]{:S(2)}) collective-permute-start(f32[2,2,128,128]{3,2,1,0:T(8,128)S(1)} %pad_maximum_fusion.4), channel_id=1, source_target_pairs={{0,128},{16,144},{32,160},{48,176},{64,192},{80,208},{96,224},{112... | collective-permute-start | bytes 786440 | tf_op jit(solution)/shard_map/ppermute | solution.py:61
  96.5 4.5 %collective-permute-done.3 = f32[2,2,128,128]{3,2,1,0:T(8,128)S(1)} collective-permute-done((f32[2,2,128,128]{3,2,1,0:T(8,128)S(1)}, f32[2,2,128,128]{3,2,1,0:T(8,128)S(1)}, u32[]{:S(2)}, u32[]{:S(2)}) %collective-permute-start.3) | collective-permute-done | bytes 262176 | tf_op jit(solution)/shard_map/ppermute | solution.py:61
  101.1 3.8 %collective-permute-start.4 = (f32[2,2,128,128]{3,2,1,0:T(8,128)S(1)}, f32[2,2,128,128]{3,2,1,0:T(8,128)S(1)}, u32[]{:S(2)}, u32[]{:S(2)}) collective-permute-start(f32[2,2,128,128]{3,2,1,0:T(8,128)S(1)} %pad_maximum_fusion.5), channel_id=1, source_target_pairs={{0,256},{16,272},{32,288},{48,304},{64,320},{80,336},{96,352},{112... | collective-permute-start | bytes 786440 | tf_op jit(solution)/shard_map/ppermute | solution.py:61
  105.4 11.5 %collective-permute-done.4 = f32[2,2,128,128]{3,2,1,0:T(8,128)S(1)} collective-permute-done((f32[2,2,128,128]{3,2,1,0:T(8,128)S(1)}, f32[2,2,128,128]{3,2,1,0:T(8,128)S(1)}, u32[]{:S(2)}, u32[]{:S(2)}) %collective-permute-start.4) | collective-permute-done | bytes 262176 | tf_op jit(solution)/shard_map/ppermute | solution.py:61
  117.0 5.0 %collective-permute-start.5 = (f32[2,128,128]{2,1,0:T(8,128)S(1)}, f32[2,128,128]{2,1,0:T(8,128)S(1)}, u32[]{:S(2)}, u32[]{:S(2)}) collective-permute-start(f32[2,128,128]{2,1,0:T(8,128)S(1)} %add_select_fusion), channel_id=1, source_target_pairs={{0,512},{16,528},{32,544},{48,560},{64,576},{80,592},{96,608},{112... | collective-permute-start | bytes 393224 | tf_op jit(solution)/shard_map/ppermute | solution.py:58
  122.3 8.8 %collective-permute-done.5 = f32[2,128,128]{2,1,0:T(8,128)S(1)} collective-permute-done((f32[2,128,128]{2,1,0:T(8,128)S(1)}, f32[2,128,128]{2,1,0:T(8,128)S(1)}, u32[]{:S(2)}, u32[]{:S(2)}) %collective-permute-start.5) | collective-permute-done | bytes 131104 | tf_op jit(solution)/shard_map/ppermute | solution.py:58
  131.6 0.8 copy.128
  132.3 0.3 fusion.12
  132.7 0.8 copy.127
  133.6 0.3 fusion.11
  134.0 0.8 copy.126
  135.2 0.8 copy.125
  (48 shorter events, 4.2 us)
Async XLA Ops:
  0.6 1.0 copy-start
  1.6 0.9 copy-start.1
  2.5 0.9 copy-start.2
  4.6 41.4 %all-to-all-start = ((bf16[16,32,512]{2,0,1:T(8,128)(2,1)}), bf16[16,32,512]{2,0,1:T(8,128)(2,1)S(1)}, u32[]{:S(2)}, u32[]{:S(2)}) async-start(bf16[16,32,512]{2,0,1:T(8,128)(2,1)} %copy.103), calls=%async_computation | async-start | bytes 1048576 | tf_op jit(solution)/shard_map/all_to_all | solution.py:12
  23.5 0.7 copy-start.4
  37.5 0.7 copy-start.3
  47.2 25.1 %collective-permute-start = (f32[2,2,128,128]{3,2,1,0:T(8,128)S(1)}, f32[2,2,128,128]{3,2,1,0:T(8,128)S(1)}, u32[]{:S(2)}, u32[]{:S(2)}) collective-permute-start(f32[2,2,128,128]{3,2,1,0:T(8,128)S(1)} %pad_maximum_fusion.1), channel_id=1, source_target_pairs={{0,16},{16,0},{32,48},{48,32},{64,80},{80,64},{96,112},{112,96},{1... | collective-permute-start | bytes 786440 | tf_op jit(solution)/shard_map/ppermute | solution.py:61
  72.4 9.8 %collective-permute-start.1 = (f32[2,2,128,128]{3,2,1,0:T(8,128)S(1)}, f32[2,2,128,128]{3,2,1,0:T(8,128)S(1)}, u32[]{:S(2)}, u32[]{:S(2)}) collective-permute-start(f32[2,2,128,128]{3,2,1,0:T(8,128)S(1)} %pad_maximum_fusion.2), channel_id=1, source_target_pairs={{0,32},{16,48},{32,0},{48,16},{64,96},{80,112},{96,64},{112,80},{1... | collective-permute-start | bytes 786440 | tf_op jit(solution)/shard_map/ppermute | solution.py:61
  82.4 10.4 %collective-permute-start.2 = (f32[2,2,128,128]{3,2,1,0:T(8,128)S(1)}, f32[2,2,128,128]{3,2,1,0:T(8,128)S(1)}, u32[]{:S(2)}, u32[]{:S(2)}) collective-permute-start(f32[2,2,128,128]{3,2,1,0:T(8,128)S(1)} %pad_maximum_fusion.3), channel_id=1, source_target_pairs={{0,64},{16,80},{32,96},{48,112},{64,0},{80,16},{96,32},{112,48},{1... | collective-permute-start | bytes 786440 | tf_op jit(solution)/shard_map/ppermute | solution.py:61
  93.0 8.0 %collective-permute-start.3 = (f32[2,2,128,128]{3,2,1,0:T(8,128)S(1)}, f32[2,2,128,128]{3,2,1,0:T(8,128)S(1)}, u32[]{:S(2)}, u32[]{:S(2)}) collective-permute-start(f32[2,2,128,128]{3,2,1,0:T(8,128)S(1)} %pad_maximum_fusion.4), channel_id=1, source_target_pairs={{0,128},{16,144},{32,160},{48,176},{64,192},{80,208},{96,224},{112... | collective-permute-start | bytes 786440 | tf_op jit(solution)/shard_map/ppermute | solution.py:61
  101.1 15.8 %collective-permute-start.4 = (f32[2,2,128,128]{3,2,1,0:T(8,128)S(1)}, f32[2,2,128,128]{3,2,1,0:T(8,128)S(1)}, u32[]{:S(2)}, u32[]{:S(2)}) collective-permute-start(f32[2,2,128,128]{3,2,1,0:T(8,128)S(1)} %pad_maximum_fusion.5), channel_id=1, source_target_pairs={{0,256},{16,272},{32,288},{48,304},{64,320},{80,336},{96,352},{112... | collective-permute-start | bytes 786440 | tf_op jit(solution)/shard_map/ppermute | solution.py:61
  117.0 14.0 %collective-permute-start.5 = (f32[2,128,128]{2,1,0:T(8,128)S(1)}, f32[2,128,128]{2,1,0:T(8,128)S(1)}, u32[]{:S(2)}, u32[]{:S(2)}) collective-permute-start(f32[2,128,128]{2,1,0:T(8,128)S(1)} %add_select_fusion), channel_id=1, source_target_pairs={{0,512},{16,528},{32,544},{48,560},{64,576},{80,592},{96,608},{112... | collective-permute-start | bytes 393224 | tf_op jit(solution)/shard_map/ppermute | solution.py:58

commit v4 on v3

--- a/solution.py
+++ b/solution.py
@@ -44,45 +44,61 @@
     def decay(groups):
         return jnp.exp(-decays * (jnp.asarray(groups) * group_len).astype(jnp.float32))
 
+    def column(factor):
+        return factor[:, None, None]
+
+    odd = here % 2 == 1
     ahead = jnp.zeros_like(forward_term)
     behind = jnp.zeros_like(backward_term)
     total_f, total_b = forward_term, backward_term
     shift = 1
     while shift < count:
-        last = shift * 2 >= count
         upper = (here // shift) % 2 == 1
         start = (here // shift) * shift
         other = jnp.where(upper, start - shift, start + shift)
         pairs = [(i, i ^ shift) for i in range(count)]
-        if last:
-            got = lax.ppermute(jnp.where(upper, total_b, total_f), "ctx", pairs)
-            got_f = got_b = got
-        else:
+        if shift == 1:
             got = lax.ppermute(jnp.stack([total_f, total_b]), "ctx", pairs)
             got_f, got_b = got[0], got[1]
+            use_f = use_b = jnp.ones((), jnp.float32)
+        else:
+            got_f = got_b = lax.ppermute(jnp.where(odd, total_b, total_f), "ctx", pairs)
+            use_b = odd.astype(jnp.float32)
+            use_f = 1.0 - use_b
         up = upper.astype(jnp.float32)
         to_ahead = decay(here - start) * (
             clipped(end_segments, start - 1) == clipped(end_segments, here - 1)
         ).astype(jnp.float32)
-        ahead = ahead + (up * to_ahead)[:, None, None] * got_f
+        ahead = ahead + column(use_f * up * to_ahead) * got_f
         to_behind = decay(start + shift - 1 - here) * (
             clipped(before_segments, start + shift) == clipped(before_segments, here + 1)
         ).astype(jnp.float32)
-        behind = behind + ((1.0 - up) * to_behind)[:, None, None] * got_b
-        if not last:
+        behind = behind + column(use_b * (1.0 - up) * to_behind) * got_b
+        if shift * 2 < count:
             joined_f = decay(shift) * (
                 clipped(end_segments, start + shift - 1) == clipped(end_segments, other + shift - 1)
             ).astype(jnp.float32)
             joined_b = decay(shift) * (
                 clipped(before_segments, start) == clipped(before_segments, other)
             ).astype(jnp.float32)
-            total_f = jnp.where(upper, 1.0, joined_f)[:, None, None] * total_f + jnp.where(
-                upper, joined_f, 1.0
-            )[:, None, None] * got_f
-            total_b = jnp.where(upper, joined_b, 1.0)[:, None, None] * total_b + jnp.where(
-                upper, 1.0, joined_b
-            )[:, None, None] * got_b
+            total_f = column(jnp.where(upper, 1.0, joined_f)) * total_f + column(
+                jnp.where(upper, joined_f, 1.0)
+            ) * got_f
+            total_b = column(jnp.where(upper, joined_b, 1.0)) * total_b + column(
+                jnp.where(upper, 1.0, joined_b)
+            ) * got_b
         shift *= 2
+    if count > 2:
+        got = lax.ppermute(jnp.where(odd, behind, ahead), "ctx", [(i, i ^ 1) for i in range(count)])
+        move_f = decay(1) * (
+            clipped(end_segments, here - 2) == clipped(end_segments, here - 1)
+        ).astype(jnp.float32)
+        move_b = decay(1) * (
+            clipped(before_segments, here + 2) == clipped(before_segments, here + 1)
+        ).astype(jnp.float32)
+        oddf = odd.astype(jnp.float32)
+        ahead = ahead + column(oddf * move_f) * got
+        behind = behind + column((1.0 - oddf) * move_b) * got
     return ahead, behind
 
 

time: 137 us -> 116 us (0.85)
  waiting for transfers between devices: 44.6 us -> 20.1 us
  between operations: 26.3 us -> 29.2 us
    ppermute x5 -> x1, waiting for transfers between devices: 28.1 us -> 0.99 us  [butterfly_scan(): got = lax.ppermute(jnp.stack([total_f, total_b]), 'ctx', pairs)]
    ppermute x1 -> x6, starting transfers between devices: 5.02 us -> 26 us  [the longest x5 18.8 us: butterfly_scan(): got_f = got_b = lax.ppermute(jnp.where(odd, total_b, total_f), 'ctx', pairs)]
    ppermute x5 -> x1, starting transfers between devices: 23.6 us -> 2.87 us  [butterfly_scan(): got = lax.ppermute(jnp.stack([total_f, total_b]), 'ctx', pairs)]
    ppermute x1 -> x6, waiting for transfers between devices: 8.77 us -> 19.2 us  [the longest x5 18.4 us: butterfly_scan(): got_f = got_b = lax.ppermute(jnp.where(odd, total_b, total_f), 'ctx', pairs)]
    all_to_all x1, waiting for transfers between devices: 7.78 us -> 0.01 us  [in_one_piece(): lax.all_to_all(both, axis, split_axis=split_dim, concat_axis=concat_dim,...]
  transfers between devices with their start and end apart: 7 -> 8, of which waited for: 6 -> 7; matrix products, arithmetic and copies ran while one was open for 4% -> 5% of each run, Pallas kernels for 0% -> 0%
where the time goes in v4:
time: 116 us; the launch traced here: 115 us
  starting transfers between devices  47.5 us (41%)
  between operations  29.2 us (25%)
  waiting for transfers between devices  20.1 us (17%)
  local copies, waits for them, and re-layouts  10.9 us (9%)
  matrix products  3.87 us (3%)
  other arithmetic  3.33 us (3%)
    ppermute x5, starting transfers between devices, butterfly_scan(): got_f = got_b = lax.ppermute(jnp.where(odd, total_b, total_f), 'ctx', pairs)  18.8 us
    all_to_all x1, starting transfers between devices, in_one_piece(): lax.all_to_all(both, axis, split_axis=split_dim, concat_axis=concat_dim,...  18.6 us
    ppermute x5, waiting for transfers between devices, butterfly_scan(): got_f = got_b = lax.ppermute(jnp.where(odd, total_b, total_f), 'ctx', pairs)  18.4 us
    ppermute x1, starting transfers between devices, butterfly_scan(): lax.ppermute(jnp.where(odd, behind, ahead), 'ctx', [(i, i ^ 1) for i in r...  7.21 us
    unnamed x18, local copies, waits for them, and re-layouts  7.12 us
    ppermute x1, starting transfers between devices, butterfly_scan(): got = lax.ppermute(jnp.stack([total_f, total_b]), 'ctx', pairs)  2.87 us
  transfers between devices with their start and end apart: 8, of which 7 were waited for; matrix products, arithmetic and copies ran while one was open for 5% of the time, Pallas kernels for 0%

profile of v4, /device:TPU:57, one launch (start us, length us, event | category | flops | bytes accessed | tf_op | source)
XLA Modules:
  0.0 114.9 jit_solution(6190364123634993953)
XLA Ops:
  0.6 1.0 copy.145
  1.7 0.9 copy-done.1
  2.5 0.9 copy-done.2
  3.5 1.1 copy.103
  4.6 18.6 %all-to-all-start = ((bf16[16,32,512]{2,0,1:T(8,128)(2,1)}), bf16[16,32,512]{2,0,1:T(8,128)(2,1)S(1)}, u32[]{:S(2)}, u32[]{:S(2)}) async-start(bf16[16,32,512]{2,0,1:T(8,128)(2,1)} %copy.103), calls=%async_computation | async-start | bytes 1048576 | tf_op jit(solution)/shard_map/all_to_all | solution.py:12
  23.6 0.6 copy-done.4
  24.5 0.7 fusion.43
  29.2 0.8 fusion.42
  52.8 0.6 slice.9
  54.6 0.6 fusion.39
  55.2 0.7 copy-done.3
  55.9 1.2 %compare_convert_fusion.2 = (f32[256]{0:T(256)S(1)}, f32[256]{0:T(256)S(1)}) fusion(s32[256]{0:T(256)S(1)} %convert_reduce_fusion, s32[]{:T(128)} %bitcast.6, s32[]{:T(128)} %fusion.39), kind=kLoop, calls=%fused_computation.81 | loop fusion | flops 1024 | bytes 3080 | tf_op jit(solution)/shard_map/convert_element_type | solution.py:27
  57.3 0.5 fusion.17
  57.8 0.5 fusion.14
  58.4 2.9 %collective-permute-start = (f32[2,2,128,128]{3,2,1,0:T(8,128)S(1)}, f32[2,2,128,128]{3,2,1,0:T(8,128)S(1)}, u32[]{:S(2)}, u32[]{:S(2)}) collective-permute-start(f32[2,2,128,128]{3,2,1,0:T(8,128)S(1)} %pad_maximum_fusion.1), channel_id=1, source_target_pairs={{0,16},{16,0},{32,48},{48,32},{64,80},{80,64},{96,112},{112,96},{1... | collective-permute-start | bytes 786440 | tf_op jit(solution)/shard_map/ppermute | solution.py:61
  61.4 1.0 collective-permute-done
  62.5 3.1 %collective-permute-start.1 = (f32[2,128,128]{2,1,0:T(8,128)S(1)}, f32[2,128,128]{2,1,0:T(8,128)S(1)}, u32[]{:S(2)}, u32[]{:S(2)}) collective-permute-start(f32[2,128,128]{2,1,0:T(8,128)S(1)} %get-tuple-element.28), channel_id=1, source_target_pairs={{0,32},{16,48},{32,0},{48,16},{64,96},{80,112},{96,64},{112,80},{1... | collective-permute-start | bytes 393224 | tf_op jit(solution)/shard_map/ppermute | solution.py:65
  65.9 3.2 %collective-permute-done.1 = f32[2,128,128]{2,1,0:T(8,128)S(1)} collective-permute-done((f32[2,128,128]{2,1,0:T(8,128)S(1)}, f32[2,128,128]{2,1,0:T(8,128)S(1)}, u32[]{:S(2)}, u32[]{:S(2)}) %collective-permute-start.1) | collective-permute-done | bytes 131104 | tf_op jit(solution)/shard_map/ppermute | solution.py:65
  69.2 4.7 %collective-permute-start.2 = (f32[2,128,128]{2,1,0:T(8,128)S(1)}, f32[2,128,128]{2,1,0:T(8,128)S(1)}, u32[]{:S(2)}, u32[]{:S(2)}) collective-permute-start(f32[2,128,128]{2,1,0:T(8,128)S(1)} %broadcast_select_fusion.3), channel_id=1, source_target_pairs={{0,64},{16,80},{32,96},{48,112},{64,0},{80,16},{96,32},{112,48},{1... | collective-permute-start | bytes 393224 | tf_op jit(solution)/shard_map/ppermute | solution.py:65
  74.1 2.3 %collective-permute-done.2 = f32[2,128,128]{2,1,0:T(8,128)S(1)} collective-permute-done((f32[2,128,128]{2,1,0:T(8,128)S(1)}, f32[2,128,128]{2,1,0:T(8,128)S(1)}, u32[]{:S(2)}, u32[]{:S(2)}) %collective-permute-start.2) | collective-permute-done | bytes 131104 | tf_op jit(solution)/shard_map/ppermute | solution.py:65
  76.6 3.0 %collective-permute-start.3 = (f32[2,128,128]{2,1,0:T(8,128)S(1)}, f32[2,128,128]{2,1,0:T(8,128)S(1)}, u32[]{:S(2)}, u32[]{:S(2)}) collective-permute-start(f32[2,128,128]{2,1,0:T(8,128)S(1)} %get-tuple-element.25), channel_id=1, source_target_pairs={{0,128},{16,144},{32,160},{48,176},{64,192},{80,208},{96,224},{112... | collective-permute-start | bytes 393224 | tf_op jit(solution)/shard_map/ppermute | solution.py:65
  79.8 2.5 %collective-permute-done.3 = f32[2,128,128]{2,1,0:T(8,128)S(1)} collective-permute-done((f32[2,128,128]{2,1,0:T(8,128)S(1)}, f32[2,128,128]{2,1,0:T(8,128)S(1)}, u32[]{:S(2)}, u32[]{:S(2)}) %collective-permute-start.3) | collective-permute-done | bytes 131104 | tf_op jit(solution)/shard_map/ppermute | solution.py:65
  82.4 3.8 %collective-permute-start.4 = (f32[2,128,128]{2,1,0:T(8,128)S(1)}, f32[2,128,128]{2,1,0:T(8,128)S(1)}, u32[]{:S(2)}, u32[]{:S(2)}) collective-permute-start(f32[2,128,128]{2,1,0:T(8,128)S(1)} %broadcast_select_fusion.1), channel_id=1, source_target_pairs={{0,256},{16,272},{32,288},{48,304},{64,320},{80,336},{96,352},{112... | collective-permute-start | bytes 393224 | tf_op jit(solution)/shard_map/ppermute | solution.py:65
  86.4 4.0 %collective-permute-done.4 = f32[2,128,128]{2,1,0:T(8,128)S(1)} collective-permute-done((f32[2,128,128]{2,1,0:T(8,128)S(1)}, f32[2,128,128]{2,1,0:T(8,128)S(1)}, u32[]{:S(2)}, u32[]{:S(2)}) %collective-permute-start.4) | collective-permute-done | bytes 131104 | tf_op jit(solution)/shard_map/ppermute | solution.py:65
  90.5 4.3 %collective-permute-start.5 = (f32[2,128,128]{2,1,0:T(8,128)S(1)}, f32[2,128,128]{2,1,0:T(8,128)S(1)}, u32[]{:S(2)}, u32[]{:S(2)}) collective-permute-start(f32[2,128,128]{2,1,0:T(8,128)S(1)} %add_select_fusion), channel_id=1, source_target_pairs={{0,512},{16,528},{32,544},{48,560},{64,576},{80,592},{96,608},{112... | collective-permute-start | bytes 393224 | tf_op jit(solution)/shard_map/ppermute | solution.py:65
  95.1 6.4 %collective-permute-done.5 = f32[2,128,128]{2,1,0:T(8,128)S(1)} collective-permute-done((f32[2,128,128]{2,1,0:T(8,128)S(1)}, f32[2,128,128]{2,1,0:T(8,128)S(1)}, u32[]{:S(2)}, u32[]{:S(2)}) %collective-permute-start.5) | collective-permute-done | bytes 131104 | tf_op jit(solution)/shard_map/ppermute | solution.py:65
  101.7 7.2 %collective-permute-start.6 = (f32[2,128,128]{2,1,0:T(8,128)S(1)}, f32[2,128,128]{2,1,0:T(8,128)S(1)}, u32[]{:S(2)}, u32[]{:S(2)}) collective-permute-start(f32[2,128,128]{2,1,0:T(8,128)S(1)} %get-tuple-element.22), channel_id=1, source_target_pairs={{0,16},{16,0},{32,48},{48,32},{64,80},{80,64},{96,112},{112,96},{1... | collective-permute-start | bytes 393224 | tf_op jit(solution)/shard_map/ppermute | solution.py:92
  109.2 0.7 collective-permute-done.6
  110.4 0.8 copy.128
  111.6 0.8 copy.127
  112.9 0.8 copy.126
  114.1 0.8 copy.125
  (46 shorter events, 5.0 us)
Async XLA Ops:
  0.6 1.0 copy-start
  1.6 0.9 copy-start.1
  2.5 0.9 copy-start.2
  4.6 52.6 %all-to-all-start = ((bf16[16,32,512]{2,0,1:T(8,128)(2,1)}), bf16[16,32,512]{2,0,1:T(8,128)(2,1)S(1)}, u32[]{:S(2)}, u32[]{:S(2)}) async-start(bf16[16,32,512]{2,0,1:T(8,128)(2,1)} %copy.103), calls=%async_computation | async-start | bytes 1048576 | tf_op jit(solution)/shard_map/all_to_all | solution.py:12
  23.6 0.7 copy-start.4
  55.2 0.7 copy-start.3
  58.4 4.0 %collective-permute-start = (f32[2,2,128,128]{3,2,1,0:T(8,128)S(1)}, f32[2,2,128,128]{3,2,1,0:T(8,128)S(1)}, u32[]{:S(2)}, u32[]{:S(2)}) collective-permute-start(f32[2,2,128,128]{3,2,1,0:T(8,128)S(1)} %pad_maximum_fusion.1), channel_id=1, source_target_pairs={{0,16},{16,0},{32,48},{48,32},{64,80},{80,64},{96,112},{112,96},{1... | collective-permute-start | bytes 786440 | tf_op jit(solution)/shard_map/ppermute | solution.py:61
  62.5 6.6 %collective-permute-start.1 = (f32[2,128,128]{2,1,0:T(8,128)S(1)}, f32[2,128,128]{2,1,0:T(8,128)S(1)}, u32[]{:S(2)}, u32[]{:S(2)}) collective-permute-start(f32[2,128,128]{2,1,0:T(8,128)S(1)} %get-tuple-element.28), channel_id=1, source_target_pairs={{0,32},{16,48},{32,0},{48,16},{64,96},{80,112},{96,64},{112,80},{1... | collective-permute-start | bytes 393224 | tf_op jit(solution)/shard_map/ppermute | solution.py:65
  69.2 7.2 %collective-permute-start.2 = (f32[2,128,128]{2,1,0:T(8,128)S(1)}, f32[2,128,128]{2,1,0:T(8,128)S(1)}, u32[]{:S(2)}, u32[]{:S(2)}) collective-permute-start(f32[2,128,128]{2,1,0:T(8,128)S(1)} %broadcast_select_fusion.3), channel_id=1, source_target_pairs={{0,64},{16,80},{32,96},{48,112},{64,0},{80,16},{96,32},{112,48},{1... | collective-permute-start | bytes 393224 | tf_op jit(solution)/shard_map/ppermute | solution.py:65
  76.6 5.7 %collective-permute-start.3 = (f32[2,128,128]{2,1,0:T(8,128)S(1)}, f32[2,128,128]{2,1,0:T(8,128)S(1)}, u32[]{:S(2)}, u32[]{:S(2)}) collective-permute-start(f32[2,128,128]{2,1,0:T(8,128)S(1)} %get-tuple-element.25), channel_id=1, source_target_pairs={{0,128},{16,144},{32,160},{48,176},{64,192},{80,208},{96,224},{112... | collective-permute-start | bytes 393224 | tf_op jit(solution)/shard_map/ppermute | solution.py:65
  82.4 8.0 %collective-permute-start.4 = (f32[2,128,128]{2,1,0:T(8,128)S(1)}, f32[2,128,128]{2,1,0:T(8,128)S(1)}, u32[]{:S(2)}, u32[]{:S(2)}) collective-permute-start(f32[2,128,128]{2,1,0:T(8,128)S(1)} %broadcast_select_fusion.1), channel_id=1, source_target_pairs={{0,256},{16,272},{32,288},{48,304},{64,320},{80,336},{96,352},{112... | collective-permute-start | bytes 393224 | tf_op jit(solution)/shard_map/ppermute | solution.py:65
  90.5 11.0 %collective-permute-start.5 = (f32[2,128,128]{2,1,0:T(8,128)S(1)}, f32[2,128,128]{2,1,0:T(8,128)S(1)}, u32[]{:S(2)}, u32[]{:S(2)}) collective-permute-start(f32[2,128,128]{2,1,0:T(8,128)S(1)} %add_select_fusion), channel_id=1, source_target_pairs={{0,512},{16,528},{32,544},{48,560},{64,576},{80,592},{96,608},{112... | collective-permute-start | bytes 393224 | tf_op jit(solution)/shard_map/ppermute | solution.py:65
  101.7 8.2 %collective-permute-start.6 = (f32[2,128,128]{2,1,0:T(8,128)S(1)}, f32[2,128,128]{2,1,0:T(8,128)S(1)}, u32[]{:S(2)}, u32[]{:S(2)}) collective-permute-start(f32[2,128,128]{2,1,0:T(8,128)S(1)} %get-tuple-element.22), channel_id=1, source_target_pairs={{0,16},{16,0},{32,48},{48,32},{64,80},{80,64},{96,112},{112,96},{1... | collective-permute-start | bytes 393224 | tf_op jit(solution)/shard_map/ppermute | solution.py:92

commit v5 on v4

--- a/solution.py
+++ b/solution.py
@@ -113,58 +113,61 @@
     starts = jnp.arange(count, dtype=jnp.int32) * group_len
     end_segments = segment_of(starts + (group_len - 1), doc_ends)
     before_segments = segment_of(starts - 1, doc_ends)
-    q_rows, k_rows, v_rows, g_rows = in_one_piece(
-        (
-            queries.reshape(rows_in, -1, DH),
-            keys.reshape(rows_in, -1, DH),
-            values.reshape(rows_in, -1, DH),
-            out_grad.reshape(rows_in, -1, DH),
-        ),
-        "exp",
-        1,
-        0,
-        2,
+    moved = lax.all_to_all(
+        jnp.stack([queries, keys, values, out_grad]), "exp", split_axis=2, concat_axis=1, tiled=True
     )
-    k_wide = k_rows.astype(jnp.float32)
-    v_wide = v_rows.astype(jnp.float32)
-    q_wide = q_rows.astype(jnp.float32)
-    g_wide = g_rows.astype(jnp.float32)
-    enter_t = enter_w.T[:, :, None]
-    leave_t = leave_w.T[:, :, None]
-    forward_term = jnp.einsum("jhd,jhe->hde", k_wide * leave_t, v_wide, precision=precise)
-    backward_term = jnp.einsum("ihd,ihe->hde", q_wide * enter_t, g_wide, precision=precise)
+    heads = moved.shape[2] // DH
+    rows = [
+        tuple(moved[a, :, h * DH:(h + 1) * DH] for a in range(4)) for h in range(heads)
+    ]
+    forward_terms, backward_terms = [], []
+    for h, (q, k, v, g) in enumerate(rows):
+        forward_terms.append(
+            jnp.dot(
+                (k.astype(jnp.float32) * leave_w[h][:, None]).T,
+                v.astype(jnp.float32),
+                precision=precise,
+            )
+        )
+        backward_terms.append(
+            jnp.dot(
+                (q.astype(jnp.float32) * enter_w[h][:, None]).T,
+                g.astype(jnp.float32),
+                precision=precise,
+            )
+        )
     state_in, state_next = butterfly_scan(
-        forward_term, backward_term, end_segments, before_segments, here, decay_rate, group_len,
-        count,
+        jnp.stack(forward_terms), jnp.stack(backward_terms), end_segments, before_segments,
+        here, decay_rate, group_len, count,
     )
-    scores = (
-        jnp.einsum("ihd,jhd->hij", q_rows, k_rows, preferred_element_type=jnp.float32) * weights
-    ).astype(jnp.bfloat16)
-    grads_loc = (
-        jnp.einsum("ihd,jhd->hij", g_rows, v_rows, preferred_element_type=jnp.float32) * weights
-    ).astype(jnp.bfloat16)
-    attended = jnp.einsum("hij,jhd->ihd", scores, v_rows, preferred_element_type=jnp.float32)
-    grad_q = jnp.einsum("hij,jhd->ihd", grads_loc, k_rows, preferred_element_type=jnp.float32)
-    grad_k = jnp.einsum("hij,ihd->jhd", grads_loc, q_rows, preferred_element_type=jnp.float32)
-    grad_v = jnp.einsum("hij,ihe->jhe", scores, g_rows, preferred_element_type=jnp.float32)
-    attended = (
-        attended + jnp.einsum("ihd,hde->ihe", q_wide, state_in, precision=precise) * enter_t
-    ).astype(jnp.bfloat16)
-    grad_q = (
-        grad_q + jnp.einsum("ihe,hde->ihd", g_wide, state_in, precision=precise) * enter_t
-    ).astype(jnp.bfloat16)
-    grad_k = (
-        grad_k + jnp.einsum("jhe,hde->jhd", v_wide, state_next, precision=precise) * leave_t
-    ).astype(jnp.bfloat16)
-    grad_v = (
-        grad_v + jnp.einsum("jhd,hde->jhe", k_wide, state_next, precision=precise) * leave_t
-    ).astype(jnp.bfloat16)
-    return (
-        attended.reshape(group_len, -1),
-        grad_q.reshape(group_len, -1),
-        grad_k.reshape(group_len, -1),
-        grad_v.reshape(group_len, -1),
-    )
+    outs = [[], [], [], []]
+    for h, (q, k, v, g) in enumerate(rows):
+        wide = lambda x: x.astype(jnp.float32)
+        scores = (
+            jnp.dot(q, k.T, preferred_element_type=jnp.float32) * weights[h]
+        ).astype(jnp.bfloat16)
+        grads_loc = (
+            jnp.dot(g, v.T, preferred_element_type=jnp.float32) * weights[h]
+        ).astype(jnp.bfloat16)
+        enter = enter_w[h][:, None]
+        leave = leave_w[h][:, None]
+        outs[0].append(
+            jnp.dot(scores, v, preferred_element_type=jnp.float32)
+            + jnp.dot(wide(q), state_in[h], precision=precise) * enter
+        )
+        outs[1].append(
+            jnp.dot(grads_loc, k, preferred_element_type=jnp.float32)
+            + jnp.dot(wide(g), state_in[h].T, precision=precise) * enter
+        )
+        outs[2].append(
+            jnp.dot(grads_loc.T, q, preferred_element_type=jnp.float32)
+            + jnp.dot(wide(v), state_next[h].T, precision=precise) * leave
+        )
+        outs[3].append(
+            jnp.dot(scores.T, g, preferred_element_type=jnp.float32)
+            + jnp.dot(wide(k), state_next[h], precision=precise) * leave
+        )
+    return tuple(jnp.concatenate(o, axis=1).astype(jnp.bfloat16) for o in outs)
 
 
 def solution(mesh):

time: 116 us -> 135 us (1.16)
  local copies, waits for them, and re-layouts: 10.9 us -> 25.9 us
  matrix products: 3.87 us -> 5.9 us
  other arithmetic: 3.33 us -> 4.85 us
    unnamed x18 -> x10, local copies, waits for them, and re-layouts: 7.12 us -> 13.6 us
    all_to_all x1, local copies, waits for them, and re-layouts: 0.04 us -> 5.48 us  [on_device(): lax.all_to_all(jnp.stack([queries, keys, values, out_grad]), 'exp', split...]
    another operation x0 -> x1, local copies, waits for them, and re-layouts: none -> 4.59 us  [on_device(): jnp.stack([queries, keys, values, out_grad])]
    dot_general x12 -> x24, matrix products: 3.87 us -> 5.9 us  [the longest x2 0.71 us: on_device(): jnp.dot((q.astype(jnp.float32) * enter_w[h][:, None]).T, g.astype(jnp.flo...]
where the time goes in v5:
time: 135 us; the launch traced here: 134 us
  starting transfers between devices  47.5 us (35%)
  between operations  29.4 us (22%)
  local copies, waits for them, and re-layouts  25.9 us (19%)
  waiting for transfers between devices  20 us (15%)
  matrix products  5.9 us (4%)
  other arithmetic  4.85 us (4%)
    ppermute x5, starting transfers between devices, butterfly_scan(): got_f = got_b = lax.ppermute(jnp.where(odd, total_b, total_f), 'ctx', pairs)  18.8 us
    all_to_all x1, starting transfers between devices, on_device(): lax.all_to_all(jnp.stack([queries, keys, values, out_grad]), 'exp', split...  18.6 us
    ppermute x5, waiting for transfers between devices, butterfly_scan(): got_f = got_b = lax.ppermute(jnp.where(odd, total_b, total_f), 'ctx', pairs)  18.6 us
    unnamed x10, local copies, waits for them, and re-layouts  13.6 us
    ppermute x1, starting transfers between devices, butterfly_scan(): lax.ppermute(jnp.where(odd, behind, ahead), 'ctx', [(i, i ^ 1) for i in r...  7.2 us
    all_to_all x1, local copies, waits for them, and re-layouts, on_device(): lax.all_to_all(jnp.stack([queries, keys, values, out_grad]), 'exp', split...  5.48 us
    another operation x1, local copies, waits for them, and re-layouts, on_device(): jnp.stack([queries, keys, values, out_grad])  4.59 us
    ppermute x1, starting transfers between devices, butterfly_scan(): got = lax.ppermute(jnp.stack([total_f, total_b]), 'ctx', pairs)  2.87 us
  transfers between devices with their start and end apart: 8, of which 7 were waited for; matrix products, arithmetic and copies ran while one was open for 5% of the time, Pallas kernels for 0%

profile of v5, /device:TPU:57, one launch (start us, length us, event | category | flops | bytes accessed | tf_op | source)
XLA Modules:
  0.0 133.5 jit_solution(3610193037641325878)
XLA Ops:
  0.6 1.2 pad_maximum_fusion
  1.8 4.6 %copy.40 = bf16[4,16,4096]{1,0,2:T(4,128)(2,1)} copy(bf16[4,16,4096]{2,1,0:T(8,128)(2,1)S(1)} %pad_maximum_fusion) | data formatting | bytes 1048576 | tf_op jit(solution)/shard_map/stack | solution.py:117
  6.4 6.4 %reshape.279 = bf16[16,2,8192]{2,1,0:T(2,128)(2,1)} reshape(bf16[4096,4,16]{2,1,0:T(4,128)(2,1)} %bitcast.168) | data formatting | bytes 1048576
  12.8 18.6 %all-to-all-start = ((bf16[16,2,8192]{2,1,0:T(2,128)(2,1)}), bf16[16,2,8192]{2,1,0:T(2,128)(2,1)S(1)}, u32[]{:S(2)}, u32[]{:S(2)}) async-start(bf16[16,2,8192]{2,1,0:T(2,128)(2,1)} %reshape.279), calls=%async_computation | async-start | bytes 1048576 | tf_op jit(solution)/shard_map/all_to_all | solution.py:116
  32.0 0.6 fusion.75
  32.7 0.6 slice.85
  33.4 0.7 fusion.81
  35.4 1.2 compare_convert_fusion.2
  49.6 0.8 fusion.80
  64.8 4.1 %reshape.280 = bf16[4096,4,16]{2,1,0:T(4,128)(2,1)} reshape(bf16[16,2,8192]{2,1,0:T(2,128)(2,1)S(1)} %all-to-all-done) | data formatting | bytes 1048576
  68.9 5.5 %copy.48 = bf16[4,16,16,256]{3,1,2,0:T(8,128)(2,1)S(1)} copy(bf16[4,16,16,256]{1,0,3,2:T(4,128)(2,1)} %bitcast.169) | data formatting | bytes 1048576 | tf_op jit(solution)/shard_map/all_to_all | solution.py:116
  75.0 0.4 convolution_bitcast_fusion.3
  75.7 0.4 convolution_bitcast_fusion.1
  76.1 0.4 convolution_bitcast_fusion.2
  76.7 2.9 %collective-permute-start = (f32[2,2,128,128]{3,2,1,0:T(8,128)S(1)}, f32[2,2,128,128]{3,2,1,0:T(8,128)S(1)}, u32[]{:S(2)}, u32[]{:S(2)}) collective-permute-start(f32[2,2,128,128]{3,2,1,0:T(8,128)S(1)} %pad_maximum_fusion.1), channel_id=1, source_target_pairs={{0,16},{16,0},{32,48},{48,32},{64,80},{80,64},{96,112},{112,96},{1... | collective-permute-start | bytes 786440 | tf_op jit(solution)/shard_map/ppermute | solution.py:61
  80.0 0.7 collective-permute-done
  80.8 3.1 %collective-permute-start.1 = (f32[2,128,128]{2,1,0:T(8,128)S(1)}, f32[2,128,128]{2,1,0:T(8,128)S(1)}, u32[]{:S(2)}, u32[]{:S(2)}) collective-permute-start(f32[2,128,128]{2,1,0:T(8,128)S(1)} %get-tuple-element.36), channel_id=1, source_target_pairs={{0,32},{16,48},{32,0},{48,16},{64,96},{80,112},{96,64},{112,80},{1... | collective-permute-start | bytes 393224 | tf_op jit(solution)/shard_map/ppermute | solution.py:65
  84.2 3.3 %collective-permute-done.1 = f32[2,128,128]{2,1,0:T(8,128)S(1)} collective-permute-done((f32[2,128,128]{2,1,0:T(8,128)S(1)}, f32[2,128,128]{2,1,0:T(8,128)S(1)}, u32[]{:S(2)}, u32[]{:S(2)}) %collective-permute-start.1) | collective-permute-done | bytes 131104 | tf_op jit(solution)/shard_map/ppermute | solution.py:65
  87.5 4.6 %collective-permute-start.2 = (f32[2,128,128]{2,1,0:T(8,128)S(1)}, f32[2,128,128]{2,1,0:T(8,128)S(1)}, u32[]{:S(2)}, u32[]{:S(2)}) collective-permute-start(f32[2,128,128]{2,1,0:T(8,128)S(1)} %broadcast_select_fusion.3), channel_id=1, source_target_pairs={{0,64},{16,80},{32,96},{48,112},{64,0},{80,16},{96,32},{112,48},{1... | collective-permute-start | bytes 393224 | tf_op jit(solution)/shard_map/ppermute | solution.py:65
  92.4 2.3 %collective-permute-done.2 = f32[2,128,128]{2,1,0:T(8,128)S(1)} collective-permute-done((f32[2,128,128]{2,1,0:T(8,128)S(1)}, f32[2,128,128]{2,1,0:T(8,128)S(1)}, u32[]{:S(2)}, u32[]{:S(2)}) %collective-permute-start.2) | collective-permute-done | bytes 131104 | tf_op jit(solution)/shard_map/ppermute | solution.py:65
  94.9 3.0 %collective-permute-start.3 = (f32[2,128,128]{2,1,0:T(8,128)S(1)}, f32[2,128,128]{2,1,0:T(8,128)S(1)}, u32[]{:S(2)}, u32[]{:S(2)}) collective-permute-start(f32[2,128,128]{2,1,0:T(8,128)S(1)} %get-tuple-element.33), channel_id=1, source_target_pairs={{0,128},{16,144},{32,160},{48,176},{64,192},{80,208},{96,224},{112... | collective-permute-start | bytes 393224 | tf_op jit(solution)/shard_map/ppermute | solution.py:65
  98.1 2.5 %collective-permute-done.3 = f32[2,128,128]{2,1,0:T(8,128)S(1)} collective-permute-done((f32[2,128,128]{2,1,0:T(8,128)S(1)}, f32[2,128,128]{2,1,0:T(8,128)S(1)}, u32[]{:S(2)}, u32[]{:S(2)}) %collective-permute-start.3) | collective-permute-done | bytes 131104 | tf_op jit(solution)/shard_map/ppermute | solution.py:65
  100.7 3.8 %collective-permute-start.4 = (f32[2,128,128]{2,1,0:T(8,128)S(1)}, f32[2,128,128]{2,1,0:T(8,128)S(1)}, u32[]{:S(2)}, u32[]{:S(2)}) collective-permute-start(f32[2,128,128]{2,1,0:T(8,128)S(1)} %broadcast_select_fusion.1), channel_id=1, source_target_pairs={{0,256},{16,272},{32,288},{48,304},{64,320},{80,336},{96,352},{112... | collective-permute-start | bytes 393224 | tf_op jit(solution)/shard_map/ppermute | solution.py:65
  104.7 4.0 %collective-permute-done.4 = f32[2,128,128]{2,1,0:T(8,128)S(1)} collective-permute-done((f32[2,128,128]{2,1,0:T(8,128)S(1)}, f32[2,128,128]{2,1,0:T(8,128)S(1)}, u32[]{:S(2)}, u32[]{:S(2)}) %collective-permute-start.4) | collective-permute-done | bytes 131104 | tf_op jit(solution)/shard_map/ppermute | solution.py:65
  108.9 4.3 %collective-permute-start.5 = (f32[2,128,128]{2,1,0:T(8,128)S(1)}, f32[2,128,128]{2,1,0:T(8,128)S(1)}, u32[]{:S(2)}, u32[]{:S(2)}) collective-permute-start(f32[2,128,128]{2,1,0:T(8,128)S(1)} %add_select_fusion), channel_id=1, source_target_pairs={{0,512},{16,528},{32,544},{48,560},{64,576},{80,592},{96,608},{112... | collective-permute-start | bytes 393224 | tf_op jit(solution)/shard_map/ppermute | solution.py:65
  113.4 6.4 %collective-permute-done.5 = f32[2,128,128]{2,1,0:T(8,128)S(1)} collective-permute-done((f32[2,128,128]{2,1,0:T(8,128)S(1)}, f32[2,128,128]{2,1,0:T(8,128)S(1)}, u32[]{:S(2)}, u32[]{:S(2)}) %collective-permute-start.5) | collective-permute-done | bytes 131104 | tf_op jit(solution)/shard_map/ppermute | solution.py:65
  120.1 7.2 %collective-permute-start.6 = (f32[2,128,128]{2,1,0:T(8,128)S(1)}, f32[2,128,128]{2,1,0:T(8,128)S(1)}, u32[]{:S(2)}, u32[]{:S(2)}) collective-permute-start(f32[2,128,128]{2,1,0:T(8,128)S(1)} %get-tuple-element.30), channel_id=1, source_target_pairs={{0,16},{16,0},{32,48},{48,32},{64,80},{80,64},{96,112},{112,96},{1... | collective-permute-start | bytes 393224 | tf_op jit(solution)/shard_map/ppermute | solution.py:92
  127.5 0.7 collective-permute-done.6
  130.4 0.8 copy.45
  131.2 0.8 copy.46
  132.0 0.8 copy.43
  132.7 0.8 copy.44
  (56 shorter events, 6.7 us)
Async XLA Ops:
  6.4 25.4 %copy-start.1 = (s32[8]{0:T(128)S(1)}, s32[8]{0:T(128)}, u32[]{:S(2)}) copy-start(s32[8]{0:T(128)} %param.11) | copy-start | bytes 100
  6.4 30.3 %copy-start = (f32[2]{0:T(128)S(1)}, f32[2]{0:T(128)}, u32[]{:S(2)}) copy-start(f32[2]{0:T(128)} %param.10) | copy-start | bytes 28
  12.8 51.9 %all-to-all-start = ((bf16[16,2,8192]{2,1,0:T(2,128)(2,1)}), bf16[16,2,8192]{2,1,0:T(2,128)(2,1)S(1)}, u32[]{:S(2)}, u32[]{:S(2)}) async-start(bf16[16,2,8192]{2,1,0:T(2,128)(2,1)} %reshape.279), calls=%async_computation | async-start | bytes 1048576 | tf_op jit(solution)/shard_map/all_to_all | solution.py:116
  76.7 4.0 %collective-permute-start = (f32[2,2,128,128]{3,2,1,0:T(8,128)S(1)}, f32[2,2,128,128]{3,2,1,0:T(8,128)S(1)}, u32[]{:S(2)}, u32[]{:S(2)}) collective-permute-start(f32[2,2,128,128]{3,2,1,0:T(8,128)S(1)} %pad_maximum_fusion.1), channel_id=1, source_target_pairs={{0,16},{16,0},{32,48},{48,32},{64,80},{80,64},{96,112},{112,96},{1... | collective-permute-start | bytes 786440 | tf_op jit(solution)/shard_map/ppermute | solution.py:61
  80.8 6.6 %collective-permute-start.1 = (f32[2,128,128]{2,1,0:T(8,128)S(1)}, f32[2,128,128]{2,1,0:T(8,128)S(1)}, u32[]{:S(2)}, u32[]{:S(2)}) collective-permute-start(f32[2,128,128]{2,1,0:T(8,128)S(1)} %get-tuple-element.36), channel_id=1, source_target_pairs={{0,32},{16,48},{32,0},{48,16},{64,96},{80,112},{96,64},{112,80},{1... | collective-permute-start | bytes 393224 | tf_op jit(solution)/shard_map/ppermute | solution.py:65
  87.5 7.2 %collective-permute-start.2 = (f32[2,128,128]{2,1,0:T(8,128)S(1)}, f32[2,128,128]{2,1,0:T(8,128)S(1)}, u32[]{:S(2)}, u32[]{:S(2)}) collective-permute-start(f32[2,128,128]{2,1,0:T(8,128)S(1)} %broadcast_select_fusion.3), channel_id=1, source_target_pairs={{0,64},{16,80},{32,96},{48,112},{64,0},{80,16},{96,32},{112,48},{1... | collective-permute-start | bytes 393224 | tf_op jit(solution)/shard_map/ppermute | solution.py:65
  94.9 5.7 %collective-permute-start.3 = (f32[2,128,128]{2,1,0:T(8,128)S(1)}, f32[2,128,128]{2,1,0:T(8,128)S(1)}, u32[]{:S(2)}, u32[]{:S(2)}) collective-permute-start(f32[2,128,128]{2,1,0:T(8,128)S(1)} %get-tuple-element.33), channel_id=1, source_target_pairs={{0,128},{16,144},{32,160},{48,176},{64,192},{80,208},{96,224},{112... | collective-permute-start | bytes 393224 | tf_op jit(solution)/shard_map/ppermute | solution.py:65
  100.7 8.0 %collective-permute-start.4 = (f32[2,128,128]{2,1,0:T(8,128)S(1)}, f32[2,128,128]{2,1,0:T(8,128)S(1)}, u32[]{:S(2)}, u32[]{:S(2)}) collective-permute-start(f32[2,128,128]{2,1,0:T(8,128)S(1)} %broadcast_select_fusion.1), channel_id=1, source_target_pairs={{0,256},{16,272},{32,288},{48,304},{64,320},{80,336},{96,352},{112... | collective-permute-start | bytes 393224 | tf_op jit(solution)/shard_map/ppermute | solution.py:65
  108.9 11.0 %collective-permute-start.5 = (f32[2,128,128]{2,1,0:T(8,128)S(1)}, f32[2,128,128]{2,1,0:T(8,128)S(1)}, u32[]{:S(2)}, u32[]{:S(2)}) collective-permute-start(f32[2,128,128]{2,1,0:T(8,128)S(1)} %add_select_fusion), channel_id=1, source_target_pairs={{0,512},{16,528},{32,544},{48,560},{64,576},{80,592},{96,608},{112... | collective-permute-start | bytes 393224 | tf_op jit(solution)/shard_map/ppermute | solution.py:65
  120.1 8.2 %collective-permute-start.6 = (f32[2,128,128]{2,1,0:T(8,128)S(1)}, f32[2,128,128]{2,1,0:T(8,128)S(1)}, u32[]{:S(2)}, u32[]{:S(2)}) collective-permute-start(f32[2,128,128]{2,1,0:T(8,128)S(1)} %get-tuple-element.30), channel_id=1, source_target_pairs={{0,16},{16,0},{32,48},{48,32},{64,80},{80,64},{96,112},{112,96},{1... | collective-permute-start | bytes 393224 | tf_op jit(solution)/shard_map/ppermute | solution.py:92

commit v6 on v1

--- a/solution.py
+++ b/solution.py
@@ -36,26 +36,47 @@
     return (weights, enter_w, leave_w)
 
 
-def decayed_scan(term, anchors, here, decays, group_len, count, forward):
-    total = term
-    shift = 1
-    while shift < count:
-        if forward:
-            pairs = [(i, i + shift) for i in range(count - shift)]
-            other = jnp.maximum(here - shift, 0)
-        else:
-            pairs = [(i + shift, i) for i in range(count - shift)]
-            other = jnp.minimum(here + shift, count - 1)
-        incoming = lax.ppermute(total, "ctx", pairs)
-        same = (anchors[here] == anchors[other]).astype(jnp.float32)
-        factor = jnp.exp(-decays * float(group_len * shift)) * same
-        total = total + factor[:, None, None] * incoming
-        shift *= 2
-    if forward:
-        pairs = [(i, i + 1) for i in range(count - 1)]
-    else:
-        pairs = [(i + 1, i) for i in range(count - 1)]
-    return lax.ppermute(total, "ctx", pairs)
+def pair_scan(forward_term, backward_term, end_segments, before_segments, here, decays,
+              group_len, count):
+    def clipped(table, index):
+        return table[jnp.clip(index, 0, count - 1)]
+
+    def decay(groups):
+        return jnp.exp(-decays * (jnp.asarray(groups) * group_len).astype(jnp.float32))
+
+    def column(factor):
+        return factor[:, None, None]
+
+    def same(table, i, j):
+        return (clipped(table, i) == clipped(table, j)).astype(jnp.float32)
+
+    def push(value, pair_shift):
+        shift = 2 * pair_shift
+        pairs = [(i, i + shift) for i in range(0, count - shift, 2)]
+        pairs += [(i, i - shift) for i in range(shift + 1, count, 2)]
+        return lax.ppermute(value, "ctx", pairs)
+
+    odd = here % 2 == 1
+    partner = [(i, i ^ 1) for i in range(count)]
+    mate = lax.ppermute(jnp.where(odd, forward_term, backward_term), "ctx", partner)
+    pair_f = column(decay(1) * same(end_segments, here, here + 1)) * forward_term + mate
+    pair_b = column(decay(1) * same(before_segments, here, here - 1)) * backward_term + mate
+    pair_total = jnp.where(odd, pair_b, pair_f)
+    def reach(pairs_away):
+        groups = 2 * pairs_away
+        forward = decay(groups) * same(end_segments, here - 1 - groups, here - 1)
+        backward = decay(groups) * same(before_segments, here + 1 + groups, here + 1)
+        return column(jnp.where(odd, backward, forward))
+
+    total = push(pair_total, 1) + reach(1) * push(pair_total, 2)
+    window = 2
+    while window < count // 2:
+        total = total + reach(window) * push(total, window)
+        window *= 2
+    handed_f = column(decay(1) * same(end_segments, here - 1, here)) * total + forward_term
+    handed_b = column(decay(1) * same(before_segments, here + 1, here)) * total + backward_term
+    handed = lax.ppermute(jnp.where(odd, handed_b, handed_f), "ctx", partner)
+    return jnp.where(odd, handed, total), jnp.where(odd, total, handed)
 
 
 def on_device(queries, keys, values, out_grad, decay_rate, doc_lengths):
@@ -89,11 +110,9 @@
     leave_t = leave_w.T[:, :, None]
     forward_term = jnp.einsum("jhd,jhe->hde", k_wide * leave_t, v_wide, precision=precise)
     backward_term = jnp.einsum("ihd,ihe->hde", q_wide * enter_t, g_wide, precision=precise)
-    state_in = decayed_scan(
-        forward_term, end_segments, here, decay_rate, group_len, count, True
-    )
-    state_next = decayed_scan(
-        backward_term, before_segments, here, decay_rate, group_len, count, False
+    state_in, state_next = pair_scan(
+        forward_term, backward_term, end_segments, before_segments, here, decay_rate, group_len,
+        count,
     )
     scores = (
         jnp.einsum("ihd,jhd->hij", q_rows, k_rows, preferred_element_type=jnp.float32) * weights

time: 133 us -> 119 us (0.89)
  the two profiles are of different devices: /device:TPU:40 before, /device:TPU:1 now
where the time goes in v6:
time: 119 us; the launch traced here: 118 us
  starting transfers between devices  44.6 us (37%)
  waiting for transfers between devices  38.8 us (33%)
  between operations  18.2 us (15%)
  local copies, waits for them, and re-layouts  9.97 us (8%)
  matrix products  3.58 us (3%)
  other arithmetic  3.03 us (3%)
    ppermute x6, waiting for transfers between devices, push(): return lax.ppermute(value, 'ctx', pairs)  36.6 us
    all_to_all x1, starting transfers between devices, in_one_piece(): lax.all_to_all(both, axis, split_axis=split_dim, concat_axis=concat_dim,...  19.4 us
    ppermute x1, starting transfers between devices, pair_scan(): lax.ppermute(jnp.where(odd, forward_term, backward_term), 'ctx', partner)  9.13 us
    ppermute x1, starting transfers between devices, pair_scan(): handed = lax.ppermute(jnp.where(odd, handed_b, handed_f), 'ctx', partner)  8.31 us
    ppermute x6, starting transfers between devices, push(): return lax.ppermute(value, 'ctx', pairs)  7.75 us
    unnamed x18, local copies, waits for them, and re-layouts  7.12 us
  transfers between devices with their start and end apart: 9, of which 9 were waited for; matrix products, arithmetic and copies ran while one was open for 4% of the time, Pallas kernels for 0%

profile of v6, /device:TPU:1, one launch (start us, length us, event | category | flops | bytes accessed | tf_op | source)
XLA Modules:
  0.0 118.2 jit_solution(8443655668967466493)
XLA Ops:
  0.6 1.0 copy.145
  1.7 0.9 copy-done.1
  2.5 0.9 copy-done.2
  3.5 1.1 copy.103
  4.6 19.4 %all-to-all-start = ((bf16[16,32,512]{2,0,1:T(8,128)(2,1)}), bf16[16,32,512]{2,0,1:T(8,128)(2,1)S(1)}, u32[]{:S(2)}, u32[]{:S(2)}) async-start(bf16[16,32,512]{2,0,1:T(8,128)(2,1)} %copy.103), calls=%async_computation | async-start | bytes 1048576 | tf_op jit(solution)/shard_map/all_to_all | solution.py:12
  24.1 0.6 copy-done.4
  25.0 0.7 fusion.42
  43.0 0.6 slice.3
  43.6 0.7 fusion.39
  44.2 1.2 %compare_convert_fusion = (f32[256]{0:T(256)S(1)}, f32[256]{0:T(256)S(1)}) fusion(s32[256]{0:T(256)S(1)} %convert_reduce_fusion, s32[]{:T(128)} %bitcast.8, s32[]{:T(128)} %fusion.39), kind=kLoop, calls=%fused_computation.68 | loop fusion | flops 1024 | bytes 3080 | tf_op jit(solution)/shard_map/convert_element_type | solution.py:27
  45.4 0.6 copy-done.3
  46.2 0.7 all-to-all-done
  48.0 9.1 %collective-permute-start = (f32[2,128,128]{2,1,0:T(8,128)S(1)}, f32[2,128,128]{2,1,0:T(8,128)S(1)}, u32[]{:S(2)}, u32[]{:S(2)}) collective-permute-start(f32[2,128,128]{2,1,0:T(8,128)S(1)} %get-tuple-element.54), channel_id=1, source_target_pairs={{0,16},{16,0},{32,48},{48,32},{64,80},{80,64},{96,112},{112,96},{1... | collective-permute-start | bytes 393224 | tf_op jit(solution)/shard_map/ppermute | solution.py:61
  57.2 0.8 collective-permute-done
  58.2 1.3 %collective-permute-start.1 = (f32[2,128,128]{2,1,0:T(8,128)S(1)}, f32[2,128,128]{2,1,0:T(8,128)S(1)}, u32[]{:S(2)}, u32[]{:S(2)}) collective-permute-start(f32[2,128,128]{2,1,0:T(8,128)S(1)} %add_select_fusion.1), channel_id=1, source_target_pairs={{0,32},{32,64},{64,96},{96,128},{128,160},{160,192},{192,224},{224... | collective-permute-start | bytes 393224 | tf_op jit(solution)/shard_map/ppermute | solution.py:57
  59.5 1.3 %collective-permute-start.2 = (f32[2,128,128]{2,1,0:T(8,128)S(1)}, f32[2,128,128]{2,1,0:T(8,128)S(1)}, u32[]{:S(2)}, u32[]{:S(2)}) collective-permute-start(f32[2,128,128]{2,1,0:T(8,128)S(1)} %add_select_fusion.1), channel_id=1, source_target_pairs={{0,64},{32,96},{64,128},{96,160},{128,192},{160,224},{192,256},{22... | collective-permute-start | bytes 393224 | tf_op jit(solution)/shard_map/ppermute | solution.py:57
  61.0 2.9 %collective-permute-done.1 = f32[2,128,128]{2,1,0:T(8,128)S(1)} collective-permute-done((f32[2,128,128]{2,1,0:T(8,128)S(1)}, f32[2,128,128]{2,1,0:T(8,128)S(1)}, u32[]{:S(2)}, u32[]{:S(2)}) %collective-permute-start.1) | collective-permute-done | bytes 131104 | tf_op jit(solution)/shard_map/ppermute | solution.py:57
  63.9 4.4 %collective-permute-done.2 = f32[2,128,128]{2,1,0:T(8,128)S(1)} collective-permute-done((f32[2,128,128]{2,1,0:T(8,128)S(1)}, f32[2,128,128]{2,1,0:T(8,128)S(1)}, u32[]{:S(2)}, u32[]{:S(2)}) %collective-permute-start.2) | collective-permute-done | bytes 131104 | tf_op jit(solution)/shard_map/ppermute | solution.py:57
  68.4 1.3 %collective-permute-start.3 = (f32[2,128,128]{2,1,0:T(8,128)S(1)}, f32[2,128,128]{2,1,0:T(8,128)S(1)}, u32[]{:S(2)}, u32[]{:S(2)}) collective-permute-start(f32[2,128,128]{2,1,0:T(8,128)S(1)} %multiply_add_fusion.4), channel_id=1, source_target_pairs={{0,64},{32,96},{64,128},{96,160},{128,192},{160,224},{192,256},{22... | collective-permute-start | bytes 393224 | tf_op jit(solution)/shard_map/ppermute | solution.py:57
  69.9 5.7 %collective-permute-done.3 = f32[2,128,128]{2,1,0:T(8,128)S(1)} collective-permute-done((f32[2,128,128]{2,1,0:T(8,128)S(1)}, f32[2,128,128]{2,1,0:T(8,128)S(1)}, u32[]{:S(2)}, u32[]{:S(2)}) %collective-permute-start.3) | collective-permute-done | bytes 131104 | tf_op jit(solution)/shard_map/ppermute | solution.py:57
  75.7 1.3 %collective-permute-start.4 = (f32[2,128,128]{2,1,0:T(8,128)S(1)}, f32[2,128,128]{2,1,0:T(8,128)S(1)}, u32[]{:S(2)}, u32[]{:S(2)}) collective-permute-start(f32[2,128,128]{2,1,0:T(8,128)S(1)} %multiply_add_fusion.3), channel_id=1, source_target_pairs={{0,128},{32,160},{64,192},{96,224},{128,256},{160,288},{192,320},{... | collective-permute-start | bytes 393224 | tf_op jit(solution)/shard_map/ppermute | solution.py:57
  77.2 6.8 %collective-permute-done.4 = f32[2,128,128]{2,1,0:T(8,128)S(1)} collective-permute-done((f32[2,128,128]{2,1,0:T(8,128)S(1)}, f32[2,128,128]{2,1,0:T(8,128)S(1)}, u32[]{:S(2)}, u32[]{:S(2)}) %collective-permute-start.4) | collective-permute-done | bytes 131104 | tf_op jit(solution)/shard_map/ppermute | solution.py:57
  84.1 1.3 %collective-permute-start.5 = (f32[2,128,128]{2,1,0:T(8,128)S(1)}, f32[2,128,128]{2,1,0:T(8,128)S(1)}, u32[]{:S(2)}, u32[]{:S(2)}) collective-permute-start(f32[2,128,128]{2,1,0:T(8,128)S(1)} %multiply_add_fusion.2), channel_id=1, source_target_pairs={{0,256},{32,288},{64,320},{96,352},{128,384},{160,416},{192,448},{... | collective-permute-start | bytes 393224 | tf_op jit(solution)/shard_map/ppermute | solution.py:57
  85.6 5.2 %collective-permute-done.5 = f32[2,128,128]{2,1,0:T(8,128)S(1)} collective-permute-done((f32[2,128,128]{2,1,0:T(8,128)S(1)}, f32[2,128,128]{2,1,0:T(8,128)S(1)}, u32[]{:S(2)}, u32[]{:S(2)}) %collective-permute-start.5) | collective-permute-done | bytes 131104 | tf_op jit(solution)/shard_map/ppermute | solution.py:57
  90.9 1.3 %collective-permute-start.6 = (f32[2,128,128]{2,1,0:T(8,128)S(1)}, f32[2,128,128]{2,1,0:T(8,128)S(1)}, u32[]{:S(2)}, u32[]{:S(2)}) collective-permute-start(f32[2,128,128]{2,1,0:T(8,128)S(1)} %multiply_add_fusion.1), channel_id=1, source_target_pairs={{0,512},{32,544},{64,576},{96,608},{128,640},{160,672},{192,704},{... | collective-permute-start | bytes 393224 | tf_op jit(solution)/shard_map/ppermute | solution.py:57
  92.5 11.6 %collective-permute-done.6 = f32[2,128,128]{2,1,0:T(8,128)S(1)} collective-permute-done((f32[2,128,128]{2,1,0:T(8,128)S(1)}, f32[2,128,128]{2,1,0:T(8,128)S(1)}, u32[]{:S(2)}, u32[]{:S(2)}) %collective-permute-start.6) | collective-permute-done | bytes 131104 | tf_op jit(solution)/shard_map/ppermute | solution.py:57
  104.2 8.3 %collective-permute-start.7 = (f32[2,128,128]{2,1,0:T(8,128)S(1)}, f32[2,128,128]{2,1,0:T(8,128)S(1)}, u32[]{:S(2)}, u32[]{:S(2)}) collective-permute-start(f32[2,128,128]{2,1,0:T(8,128)S(1)} %get-tuple-element.22), channel_id=1, source_target_pairs={{0,16},{16,0},{32,48},{48,32},{64,80},{80,64},{96,112},{112,96},{1... | collective-permute-start | bytes 393224 | tf_op jit(solution)/shard_map/ppermute | solution.py:78
  112.8 0.7 collective-permute-done.7
  113.9 0.8 copy.128
  115.1 0.8 copy.127
  116.2 0.8 copy.126
  117.4 0.8 copy.125
  (44 shorter events, 5.3 us)
Async XLA Ops:
  0.6 1.0 copy-start
  1.6 0.9 copy-start.1
  2.5 0.9 copy-start.2
  4.6 42.2 %all-to-all-start = ((bf16[16,32,512]{2,0,1:T(8,128)(2,1)}), bf16[16,32,512]{2,0,1:T(8,128)(2,1)S(1)}, u32[]{:S(2)}, u32[]{:S(2)}) async-start(bf16[16,32,512]{2,0,1:T(8,128)(2,1)} %copy.103), calls=%async_computation | async-start | bytes 1048576 | tf_op jit(solution)/shard_map/all_to_all | solution.py:12
  24.1 0.7 copy-start.4
  45.4 0.7 copy-start.3
  48.0 10.1 %collective-permute-start = (f32[2,128,128]{2,1,0:T(8,128)S(1)}, f32[2,128,128]{2,1,0:T(8,128)S(1)}, u32[]{:S(2)}, u32[]{:S(2)}) collective-permute-start(f32[2,128,128]{2,1,0:T(8,128)S(1)} %get-tuple-element.54), channel_id=1, source_target_pairs={{0,16},{16,0},{32,48},{48,32},{64,80},{80,64},{96,112},{112,96},{1... | collective-permute-start | bytes 393224 | tf_op jit(solution)/shard_map/ppermute | solution.py:61
  58.2 5.7 %collective-permute-start.1 = (f32[2,128,128]{2,1,0:T(8,128)S(1)}, f32[2,128,128]{2,1,0:T(8,128)S(1)}, u32[]{:S(2)}, u32[]{:S(2)}) collective-permute-start(f32[2,128,128]{2,1,0:T(8,128)S(1)} %add_select_fusion.1), channel_id=1, source_target_pairs={{0,32},{32,64},{64,96},{96,128},{128,160},{160,192},{192,224},{224... | collective-permute-start | bytes 393224 | tf_op jit(solution)/shard_map/ppermute | solution.py:57
  59.5 8.8 %collective-permute-start.2 = (f32[2,128,128]{2,1,0:T(8,128)S(1)}, f32[2,128,128]{2,1,0:T(8,128)S(1)}, u32[]{:S(2)}, u32[]{:S(2)}) collective-permute-start(f32[2,128,128]{2,1,0:T(8,128)S(1)} %add_select_fusion.1), channel_id=1, source_target_pairs={{0,64},{32,96},{64,128},{96,160},{128,192},{160,224},{192,256},{22... | collective-permute-start | bytes 393224 | tf_op jit(solution)/shard_map/ppermute | solution.py:57
  68.4 7.2 %collective-permute-start.3 = (f32[2,128,128]{2,1,0:T(8,128)S(1)}, f32[2,128,128]{2,1,0:T(8,128)S(1)}, u32[]{:S(2)}, u32[]{:S(2)}) collective-permute-start(f32[2,128,128]{2,1,0:T(8,128)S(1)} %multiply_add_fusion.4), channel_id=1, source_target_pairs={{0,64},{32,96},{64,128},{96,160},{128,192},{160,224},{192,256},{22... | collective-permute-start | bytes 393224 | tf_op jit(solution)/shard_map/ppermute | solution.py:57
  75.7 8.3 %collective-permute-start.4 = (f32[2,128,128]{2,1,0:T(8,128)S(1)}, f32[2,128,128]{2,1,0:T(8,128)S(1)}, u32[]{:S(2)}, u32[]{:S(2)}) collective-permute-start(f32[2,128,128]{2,1,0:T(8,128)S(1)} %multiply_add_fusion.3), channel_id=1, source_target_pairs={{0,128},{32,160},{64,192},{96,224},{128,256},{160,288},{192,320},{... | collective-permute-start | bytes 393224 | tf_op jit(solution)/shard_map/ppermute | solution.py:57
  84.1 6.7 %collective-permute-start.5 = (f32[2,128,128]{2,1,0:T(8,128)S(1)}, f32[2,128,128]{2,1,0:T(8,128)S(1)}, u32[]{:S(2)}, u32[]{:S(2)}) collective-permute-start(f32[2,128,128]{2,1,0:T(8,128)S(1)} %multiply_add_fusion.2), channel_id=1, source_target_pairs={{0,256},{32,288},{64,320},{96,352},{128,384},{160,416},{192,448},{... | collective-permute-start | bytes 393224 | tf_op jit(solution)/shard_map/ppermute | solution.py:57
  90.9 13.2 %collective-permute-start.6 = (f32[2,128,128]{2,1,0:T(8,128)S(1)}, f32[2,128,128]{2,1,0:T(8,128)S(1)}, u32[]{:S(2)}, u32[]{:S(2)}) collective-permute-start(f32[2,128,128]{2,1,0:T(8,128)S(1)} %multiply_add_fusion.1), channel_id=1, source_target_pairs={{0,512},{32,544},{64,576},{96,608},{128,640},{160,672},{192,704},{... | collective-permute-start | bytes 393224 | tf_op jit(solution)/shard_map/ppermute | solution.py:57
  104.2 9.3 %collective-permute-start.7 = (f32[2,128,128]{2,1,0:T(8,128)S(1)}, f32[2,128,128]{2,1,0:T(8,128)S(1)}, u32[]{:S(2)}, u32[]{:S(2)}) collective-permute-start(f32[2,128,128]{2,1,0:T(8,128)S(1)} %get-tuple-element.22), channel_id=1, source_target_pairs={{0,16},{16,0},{32,48},{48,32},{64,80},{80,64},{96,112},{112,96},{1... | collective-permute-start | bytes 393224 | tf_op jit(solution)/shard_map/ppermute | solution.py:78

commit v7 on v4

--- a/solution.py
+++ b/solution.py
@@ -113,17 +113,12 @@
     starts = jnp.arange(count, dtype=jnp.int32) * group_len
     end_segments = segment_of(starts + (group_len - 1), doc_ends)
     before_segments = segment_of(starts - 1, doc_ends)
-    q_rows, k_rows, v_rows, g_rows = in_one_piece(
-        (
-            queries.reshape(rows_in, -1, DH),
-            keys.reshape(rows_in, -1, DH),
-            values.reshape(rows_in, -1, DH),
-            out_grad.reshape(rows_in, -1, DH),
-        ),
-        "exp",
-        1,
-        0,
-        2,
+    arrays = (queries, keys, values, out_grad)
+    joined = jnp.concatenate(arrays, axis=0).reshape(len(arrays) * rows_in, -1, DH)
+    moved = lax.all_to_all(joined, "exp", split_axis=1, concat_axis=0, tiled=True)
+    moved = moved.reshape(-1, len(arrays), rows_in, moved.shape[1], DH)
+    q_rows, k_rows, v_rows, g_rows = (
+        moved[:, a].reshape(group_len, -1, DH) for a in range(len(arrays))
     )
     k_wide = k_rows.astype(jnp.float32)
     v_wide = v_rows.astype(jnp.float32)

time: 116 us -> 114 us (0.983)
  local copies, waits for them, and re-layouts: 10.9 us -> 6.99 us
  other arithmetic: 3.33 us -> 5.34 us
    unnamed x18 -> x8, local copies, waits for them, and re-layouts: 7.12 us -> 4.35 us
    reshape x0 -> x1, other arithmetic: none -> 2.03 us  [on_device(): jnp.concatenate(arrays, axis=0).reshape(len(arrays) * rows_in, -1, DH)]
where the time goes in v7:
time: 114 us; the launch traced here: 113 us
  starting transfers between devices  47.5 us (42%)
  between operations  28.8 us (25%)
  waiting for transfers between devices  20.1 us (18%)
  local copies, waits for them, and re-layouts  6.99 us (6%)
  other arithmetic  5.34 us (5%)
  matrix products  3.88 us (3%)
    ppermute x5, starting transfers between devices, butterfly_scan(): got_f = got_b = lax.ppermute(jnp.where(odd, total_b, total_f), 'ctx', pairs)  18.8 us
    all_to_all x1, starting transfers between devices, on_device(): lax.all_to_all(joined, 'exp', split_axis=1, concat_axis=0, tiled=True)  18.6 us
    ppermute x5, waiting for transfers between devices, butterfly_scan(): got_f = got_b = lax.ppermute(jnp.where(odd, total_b, total_f), 'ctx', pairs)  18.4 us
    ppermute x1, starting transfers between devices, butterfly_scan(): lax.ppermute(jnp.where(odd, behind, ahead), 'ctx', [(i, i ^ 1) for i in r...  7.21 us
    unnamed x8, local copies, waits for them, and re-layouts  4.35 us
    ppermute x1, starting transfers between devices, butterfly_scan(): got = lax.ppermute(jnp.stack([total_f, total_b]), 'ctx', pairs)  2.87 us
  transfers between devices with their start and end apart: 8, of which 7 were waited for; matrix products, arithmetic and copies ran while one was open for 5% of the time, Pallas kernels for 0%

profile of v7, /device:TPU:57, one launch (start us, length us, event | category | flops | bytes accessed | tf_op | source)
XLA Modules:
  0.0 112.6 jit_solution(2196731652904666)
XLA Ops:
  0.6 2.0 %copy_bitcast_fusion = bf16[64,32,128]{2,0,1:T(8,128)(2,1)} fusion(bf16[16,4096]{1,0:T(8,128)(2,1)} %param.9, bf16[16,4096]{1,0:T(8,128)(2,1)} %param.8, bf16[16,4096]{1,0:T(8,128)(2,1)} %param.7, bf16[16,4096]{1,0:T(8,128)(2,1)} %param.6), kind=kLoop, calls=%fused_computation.24 | loop fusion | flops 2097152 | bytes 1048576 | tf_op jit(solution)/shard_map/reshape | solution.py:117
  2.7 18.6 %all-to-all-start = ((bf16[64,32,128]{2,0,1:T(8,128)(2,1)}), bf16[64,32,128]{2,0,1:T(8,128)(2,1)S(1)}, u32[]{:S(2)}, u32[]{:S(2)}) async-start(bf16[64,32,128]{2,0,1:T(8,128)(2,1)} %copy_bitcast_fusion), calls=%async_computation | async-start | bytes 1048576 | tf_op jit(solution)/shard_map/all_to_all | solution.py:118
  21.7 0.6 copy-done.1
  22.6 0.7 fusion.28
  27.0 0.8 fusion.27
  51.6 0.6 slice.24
  52.2 0.6 fusion.23
  52.8 0.7 copy-done
  53.5 1.2 %compare_convert_fusion.2 = (f32[256]{0:T(256)S(1)}, f32[256]{0:T(256)S(1)}) fusion(s32[256]{0:T(256)S(1)} %convert_reduce_fusion, s32[]{:T(128)} %bitcast.11, s32[]{:T(128)} %fusion.23), kind=kLoop, calls=%fused_computation.66 | loop fusion | flops 1024 | bytes 3080 | tf_op jit(solution)/shard_map/convert_element_type | solution.py:27
  55.0 0.5 fusion.17
  55.5 0.5 fusion.14
  56.1 2.9 %collective-permute-start = (f32[2,2,128,128]{3,2,1,0:T(8,128)S(1)}, f32[2,2,128,128]{3,2,1,0:T(8,128)S(1)}, u32[]{:S(2)}, u32[]{:S(2)}) collective-permute-start(f32[2,2,128,128]{3,2,1,0:T(8,128)S(1)} %pad_maximum_fusion), channel_id=1, source_target_pairs={{0,16},{16,0},{32,48},{48,32},{64,80},{80,64},{96,112},{112,96},{1... | collective-permute-start | bytes 786440 | tf_op jit(solution)/shard_map/ppermute | solution.py:61
  59.1 1.0 collective-permute-done
  60.2 3.1 %collective-permute-start.1 = (f32[2,128,128]{2,1,0:T(8,128)S(1)}, f32[2,128,128]{2,1,0:T(8,128)S(1)}, u32[]{:S(2)}, u32[]{:S(2)}) collective-permute-start(f32[2,128,128]{2,1,0:T(8,128)S(1)} %get-tuple-element.20), channel_id=1, source_target_pairs={{0,32},{16,48},{32,0},{48,16},{64,96},{80,112},{96,64},{112,80},{1... | collective-permute-start | bytes 393224 | tf_op jit(solution)/shard_map/ppermute | solution.py:65
  63.6 3.2 %collective-permute-done.1 = f32[2,128,128]{2,1,0:T(8,128)S(1)} collective-permute-done((f32[2,128,128]{2,1,0:T(8,128)S(1)}, f32[2,128,128]{2,1,0:T(8,128)S(1)}, u32[]{:S(2)}, u32[]{:S(2)}) %collective-permute-start.1) | collective-permute-done | bytes 131104 | tf_op jit(solution)/shard_map/ppermute | solution.py:65
  66.9 4.7 %collective-permute-start.2 = (f32[2,128,128]{2,1,0:T(8,128)S(1)}, f32[2,128,128]{2,1,0:T(8,128)S(1)}, u32[]{:S(2)}, u32[]{:S(2)}) collective-permute-start(f32[2,128,128]{2,1,0:T(8,128)S(1)} %broadcast_select_fusion.3), channel_id=1, source_target_pairs={{0,64},{16,80},{32,96},{48,112},{64,0},{80,16},{96,32},{112,48},{1... | collective-permute-start | bytes 393224 | tf_op jit(solution)/shard_map/ppermute | solution.py:65
  71.8 2.3 %collective-permute-done.2 = f32[2,128,128]{2,1,0:T(8,128)S(1)} collective-permute-done((f32[2,128,128]{2,1,0:T(8,128)S(1)}, f32[2,128,128]{2,1,0:T(8,128)S(1)}, u32[]{:S(2)}, u32[]{:S(2)}) %collective-permute-start.2) | collective-permute-done | bytes 131104 | tf_op jit(solution)/shard_map/ppermute | solution.py:65
  74.3 3.0 %collective-permute-start.3 = (f32[2,128,128]{2,1,0:T(8,128)S(1)}, f32[2,128,128]{2,1,0:T(8,128)S(1)}, u32[]{:S(2)}, u32[]{:S(2)}) collective-permute-start(f32[2,128,128]{2,1,0:T(8,128)S(1)} %get-tuple-element.17), channel_id=1, source_target_pairs={{0,128},{16,144},{32,160},{48,176},{64,192},{80,208},{96,224},{112... | collective-permute-start | bytes 393224 | tf_op jit(solution)/shard_map/ppermute | solution.py:65
  77.5 2.5 %collective-permute-done.3 = f32[2,128,128]{2,1,0:T(8,128)S(1)} collective-permute-done((f32[2,128,128]{2,1,0:T(8,128)S(1)}, f32[2,128,128]{2,1,0:T(8,128)S(1)}, u32[]{:S(2)}, u32[]{:S(2)}) %collective-permute-start.3) | collective-permute-done | bytes 131104 | tf_op jit(solution)/shard_map/ppermute | solution.py:65
  80.1 3.8 %collective-permute-start.4 = (f32[2,128,128]{2,1,0:T(8,128)S(1)}, f32[2,128,128]{2,1,0:T(8,128)S(1)}, u32[]{:S(2)}, u32[]{:S(2)}) collective-permute-start(f32[2,128,128]{2,1,0:T(8,128)S(1)} %broadcast_select_fusion.1), channel_id=1, source_target_pairs={{0,256},{16,272},{32,288},{48,304},{64,320},{80,336},{96,352},{112... | collective-permute-start | bytes 393224 | tf_op jit(solution)/shard_map/ppermute | solution.py:65
  84.1 4.0 %collective-permute-done.4 = f32[2,128,128]{2,1,0:T(8,128)S(1)} collective-permute-done((f32[2,128,128]{2,1,0:T(8,128)S(1)}, f32[2,128,128]{2,1,0:T(8,128)S(1)}, u32[]{:S(2)}, u32[]{:S(2)}) %collective-permute-start.4) | collective-permute-done | bytes 131104 | tf_op jit(solution)/shard_map/ppermute | solution.py:65
  88.3 4.3 %collective-permute-start.5 = (f32[2,128,128]{2,1,0:T(8,128)S(1)}, f32[2,128,128]{2,1,0:T(8,128)S(1)}, u32[]{:S(2)}, u32[]{:S(2)}) collective-permute-start(f32[2,128,128]{2,1,0:T(8,128)S(1)} %add_select_fusion), channel_id=1, source_target_pairs={{0,512},{16,528},{32,544},{48,560},{64,576},{80,592},{96,608},{112... | collective-permute-start | bytes 393224 | tf_op jit(solution)/shard_map/ppermute | solution.py:65
  92.9 6.4 %collective-permute-done.5 = f32[2,128,128]{2,1,0:T(8,128)S(1)} collective-permute-done((f32[2,128,128]{2,1,0:T(8,128)S(1)}, f32[2,128,128]{2,1,0:T(8,128)S(1)}, u32[]{:S(2)}, u32[]{:S(2)}) %collective-permute-start.5) | collective-permute-done | bytes 131104 | tf_op jit(solution)/shard_map/ppermute | solution.py:65
  99.5 7.2 %collective-permute-start.6 = (f32[2,128,128]{2,1,0:T(8,128)S(1)}, f32[2,128,128]{2,1,0:T(8,128)S(1)}, u32[]{:S(2)}, u32[]{:S(2)}) collective-permute-start(f32[2,128,128]{2,1,0:T(8,128)S(1)} %get-tuple-element.14), channel_id=1, source_target_pairs={{0,16},{16,0},{32,48},{48,32},{64,80},{80,64},{96,112},{112,96},{1... | collective-permute-start | bytes 393224 | tf_op jit(solution)/shard_map/ppermute | solution.py:92
  106.9 0.7 collective-permute-done.6
  107.6 0.4 fusion.13
  108.1 0.8 copy.86
  109.4 0.8 copy.85
  110.1 0.3 fusion.11
  110.6 0.8 copy.84
  111.4 0.3 fusion.10
  111.8 0.8 copy.83
  (39 shorter events, 3.8 us)
Async XLA Ops:
  2.7 52.2 %all-to-all-start = ((bf16[64,32,128]{2,0,1:T(8,128)(2,1)}), bf16[64,32,128]{2,0,1:T(8,128)(2,1)S(1)}, u32[]{:S(2)}, u32[]{:S(2)}) async-start(bf16[64,32,128]{2,0,1:T(8,128)(2,1)} %copy_bitcast_fusion), calls=%async_computation | async-start | bytes 1048576 | tf_op jit(solution)/shard_map/all_to_all | solution.py:118
  21.7 0.7 copy-start.1
  52.8 0.7 copy-start
  56.1 4.0 %collective-permute-start = (f32[2,2,128,128]{3,2,1,0:T(8,128)S(1)}, f32[2,2,128,128]{3,2,1,0:T(8,128)S(1)}, u32[]{:S(2)}, u32[]{:S(2)}) collective-permute-start(f32[2,2,128,128]{3,2,1,0:T(8,128)S(1)} %pad_maximum_fusion), channel_id=1, source_target_pairs={{0,16},{16,0},{32,48},{48,32},{64,80},{80,64},{96,112},{112,96},{1... | collective-permute-start | bytes 786440 | tf_op jit(solution)/shard_map/ppermute | solution.py:61
  60.2 6.6 %collective-permute-start.1 = (f32[2,128,128]{2,1,0:T(8,128)S(1)}, f32[2,128,128]{2,1,0:T(8,128)S(1)}, u32[]{:S(2)}, u32[]{:S(2)}) collective-permute-start(f32[2,128,128]{2,1,0:T(8,128)S(1)} %get-tuple-element.20), channel_id=1, source_target_pairs={{0,32},{16,48},{32,0},{48,16},{64,96},{80,112},{96,64},{112,80},{1... | collective-permute-start | bytes 393224 | tf_op jit(solution)/shard_map/ppermute | solution.py:65
  66.9 7.2 %collective-permute-start.2 = (f32[2,128,128]{2,1,0:T(8,128)S(1)}, f32[2,128,128]{2,1,0:T(8,128)S(1)}, u32[]{:S(2)}, u32[]{:S(2)}) collective-permute-start(f32[2,128,128]{2,1,0:T(8,128)S(1)} %broadcast_select_fusion.3), channel_id=1, source_target_pairs={{0,64},{16,80},{32,96},{48,112},{64,0},{80,16},{96,32},{112,48},{1... | collective-permute-start | bytes 393224 | tf_op jit(solution)/shard_map/ppermute | solution.py:65
  74.3 5.7 %collective-permute-start.3 = (f32[2,128,128]{2,1,0:T(8,128)S(1)}, f32[2,128,128]{2,1,0:T(8,128)S(1)}, u32[]{:S(2)}, u32[]{:S(2)}) collective-permute-start(f32[2,128,128]{2,1,0:T(8,128)S(1)} %get-tuple-element.17), channel_id=1, source_target_pairs={{0,128},{16,144},{32,160},{48,176},{64,192},{80,208},{96,224},{112... | collective-permute-start | bytes 393224 | tf_op jit(solution)/shard_map/ppermute | solution.py:65
  80.1 8.0 %collective-permute-start.4 = (f32[2,128,128]{2,1,0:T(8,128)S(1)}, f32[2,128,128]{2,1,0:T(8,128)S(1)}, u32[]{:S(2)}, u32[]{:S(2)}) collective-permute-start(f32[2,128,128]{2,1,0:T(8,128)S(1)} %broadcast_select_fusion.1), channel_id=1, source_target_pairs={{0,256},{16,272},{32,288},{48,304},{64,320},{80,336},{96,352},{112... | collective-permute-start | bytes 393224 | tf_op jit(solution)/shard_map/ppermute | solution.py:65
  88.3 11.0 %collective-permute-start.5 = (f32[2,128,128]{2,1,0:T(8,128)S(1)}, f32[2,128,128]{2,1,0:T(8,128)S(1)}, u32[]{:S(2)}, u32[]{:S(2)}) collective-permute-start(f32[2,128,128]{2,1,0:T(8,128)S(1)} %add_select_fusion), channel_id=1, source_target_pairs={{0,512},{16,528},{32,544},{48,560},{64,576},{80,592},{96,608},{112... | collective-permute-start | bytes 393224 | tf_op jit(solution)/shard_map/ppermute | solution.py:65
  99.5 8.2 %collective-permute-start.6 = (f32[2,128,128]{2,1,0:T(8,128)S(1)}, f32[2,128,128]{2,1,0:T(8,128)S(1)}, u32[]{:S(2)}, u32[]{:S(2)}) collective-permute-start(f32[2,128,128]{2,1,0:T(8,128)S(1)} %get-tuple-element.14), channel_id=1, source_target_pairs={{0,16},{16,0},{32,48},{48,32},{64,80},{80,64},{96,112},{112,96},{1... | collective-permute-start | bytes 393224 | tf_op jit(solution)/shard_map/ppermute | solution.py:92

commit v8 on v7

--- a/solution.py
+++ b/solution.py
@@ -58,9 +58,8 @@
         other = jnp.where(upper, start - shift, start + shift)
         pairs = [(i, i ^ shift) for i in range(count)]
         if shift == 1:
-            got = lax.ppermute(jnp.stack([total_f, total_b]), "ctx", pairs)
-            got_f, got_b = got[0], got[1]
-            use_f = use_b = jnp.ones((), jnp.float32)
+            got_f = got_b = lax.ppermute(jnp.where(odd, total_f, total_b), "ctx", pairs)
+            use_f = use_b = jnp.zeros((), jnp.float32)
         else:
             got_f = got_b = lax.ppermute(jnp.where(odd, total_b, total_f), "ctx", pairs)
             use_b = odd.astype(jnp.float32)
@@ -88,18 +87,16 @@
                 jnp.where(upper, 1.0, joined_b)
             ) * got_b
         shift *= 2
-    if count > 2:
-        got = lax.ppermute(jnp.where(odd, behind, ahead), "ctx", [(i, i ^ 1) for i in range(count)])
-        move_f = decay(1) * (
-            clipped(end_segments, here - 2) == clipped(end_segments, here - 1)
-        ).astype(jnp.float32)
-        move_b = decay(1) * (
-            clipped(before_segments, here + 2) == clipped(before_segments, here + 1)
-        ).astype(jnp.float32)
-        oddf = odd.astype(jnp.float32)
-        ahead = ahead + column(oddf * move_f) * got
-        behind = behind + column((1.0 - oddf) * move_b) * got
-    return ahead, behind
+    handed_f = column(decay(1) * (
+        clipped(end_segments, here - 1) == clipped(end_segments, here)
+    ).astype(jnp.float32)) * ahead + forward_term
+    handed_b = column(decay(1) * (
+        clipped(before_segments, here + 1) == clipped(before_segments, here)
+    ).astype(jnp.float32)) * behind + backward_term
+    got = lax.ppermute(
+        jnp.where(odd, handed_b, handed_f), "ctx", [(i, i ^ 1) for i in range(count)]
+    )
+    return jnp.where(odd, got, ahead), jnp.where(odd, behind, got)
 
 
 def on_device(queries, keys, values, out_grad, decay_rate, doc_lengths):

time: 114 us -> 114 us (level)
  no operation moved by 1% of the time
where the time goes in v8:
time: 114 us; the launch traced here: 113 us
  starting transfers between devices  47.5 us (42%)
  between operations  29.2 us (26%)
  waiting for transfers between devices  20.1 us (18%)
  local copies, waits for them, and re-layouts  6.91 us (6%)
  other arithmetic  5.36 us (5%)
  matrix products  3.59 us (3%)
    ppermute x5, starting transfers between devices, butterfly_scan(): got_f = got_b = lax.ppermute(jnp.where(odd, total_b, total_f), 'ctx', pairs)  18.8 us
    all_to_all x1, starting transfers between devices, on_device(): lax.all_to_all(joined, 'exp', split_axis=1, concat_axis=0, tiled=True)  18.6 us
    ppermute x5, waiting for transfers between devices, butterfly_scan(): got_f = got_b = lax.ppermute(jnp.where(odd, total_b, total_f), 'ctx', pairs)  18.4 us
    ppermute x1, starting transfers between devices, butterfly_scan(): lax.ppermute(jnp.where(odd, handed_b, handed_f), 'ctx', [(i, i ^ 1) for i...  7.2 us
    unnamed x8, local copies, waits for them, and re-layouts  4.34 us
    ppermute x1, starting transfers between devices, butterfly_scan(): got_f = got_b = lax.ppermute(jnp.where(odd, total_f, total_b), 'ctx', pairs)  2.87 us
  transfers between devices with their start and end apart: 8, of which 7 were waited for; matrix products, arithmetic and copies ran while one was open for 5% of the time, Pallas kernels for 0%

profile of v8, /device:TPU:57, one launch (start us, length us, event | category | flops | bytes accessed | tf_op | source)
XLA Modules:
  0.0 112.6 jit_solution(9262394153849534323)
XLA Ops:
  0.6 2.0 %copy_bitcast_fusion = bf16[64,32,128]{2,0,1:T(8,128)(2,1)} fusion(bf16[16,4096]{1,0:T(8,128)(2,1)} %param.9, bf16[16,4096]{1,0:T(8,128)(2,1)} %param.8, bf16[16,4096]{1,0:T(8,128)(2,1)} %param.7, bf16[16,4096]{1,0:T(8,128)(2,1)} %param.6), kind=kLoop, calls=%fused_computation.24 | loop fusion | flops 2097152 | bytes 1048576 | tf_op jit(solution)/shard_map/reshape | solution.py:114
  2.7 18.6 %all-to-all-start = ((bf16[64,32,128]{2,0,1:T(8,128)(2,1)}), bf16[64,32,128]{2,0,1:T(8,128)(2,1)S(1)}, u32[]{:S(2)}, u32[]{:S(2)}) async-start(bf16[64,32,128]{2,0,1:T(8,128)(2,1)} %copy_bitcast_fusion), calls=%async_computation | async-start | bytes 1048576 | tf_op jit(solution)/shard_map/all_to_all | solution.py:115
  21.7 0.6 copy-done.1
  22.6 0.7 fusion.27
  28.5 0.8 fusion.28
  42.0 0.6 slice.18
  52.5 0.7 fusion.23
  53.2 1.2 %compare_convert_fusion.2 = (f32[256]{0:T(256)S(1)}, f32[256]{0:T(256)S(1)}) fusion(s32[256]{0:T(256)S(1)} %convert_reduce_fusion, s32[]{:T(128)} %bitcast.12, s32[]{:T(128)} %fusion.23), kind=kLoop, calls=%fused_computation.64 | loop fusion | flops 1024 | bytes 3080 | tf_op jit(solution)/shard_map/convert_element_type | solution.py:27
  54.4 0.6 copy-done
  55.4 0.5 fusion.14
  56.0 0.5 broadcast_select_fusion.6
  56.5 2.9 %collective-permute-start = (f32[2,128,128]{2,1,0:T(8,128)S(1)}, f32[2,128,128]{2,1,0:T(8,128)S(1)}, u32[]{:S(2)}, u32[]{:S(2)}) collective-permute-start(f32[2,128,128]{2,1,0:T(8,128)S(1)} %get-tuple-element.98), channel_id=1, source_target_pairs={{0,16},{16,0},{32,48},{48,32},{64,80},{80,64},{96,112},{112,96},{1... | collective-permute-start | bytes 393224 | tf_op jit(solution)/shard_map/ppermute | solution.py:61
  59.4 0.9 collective-permute-done
  60.4 3.1 %collective-permute-start.1 = (f32[2,128,128]{2,1,0:T(8,128)S(1)}, f32[2,128,128]{2,1,0:T(8,128)S(1)}, u32[]{:S(2)}, u32[]{:S(2)}) collective-permute-start(f32[2,128,128]{2,1,0:T(8,128)S(1)} %broadcast_select_fusion.5), channel_id=1, source_target_pairs={{0,32},{16,48},{32,0},{48,16},{64,96},{80,112},{96,64},{112,80},{1... | collective-permute-start | bytes 393224 | tf_op jit(solution)/shard_map/ppermute | solution.py:64
  63.8 3.2 %collective-permute-done.1 = f32[2,128,128]{2,1,0:T(8,128)S(1)} collective-permute-done((f32[2,128,128]{2,1,0:T(8,128)S(1)}, f32[2,128,128]{2,1,0:T(8,128)S(1)}, u32[]{:S(2)}, u32[]{:S(2)}) %collective-permute-start.1) | collective-permute-done | bytes 131104 | tf_op jit(solution)/shard_map/ppermute | solution.py:64
  67.2 4.7 %collective-permute-start.2 = (f32[2,128,128]{2,1,0:T(8,128)S(1)}, f32[2,128,128]{2,1,0:T(8,128)S(1)}, u32[]{:S(2)}, u32[]{:S(2)}) collective-permute-start(f32[2,128,128]{2,1,0:T(8,128)S(1)} %get-tuple-element.20), channel_id=1, source_target_pairs={{0,64},{16,80},{32,96},{48,112},{64,0},{80,16},{96,32},{112,48},{1... | collective-permute-start | bytes 393224 | tf_op jit(solution)/shard_map/ppermute | solution.py:64
  72.1 2.3 %collective-permute-done.2 = f32[2,128,128]{2,1,0:T(8,128)S(1)} collective-permute-done((f32[2,128,128]{2,1,0:T(8,128)S(1)}, f32[2,128,128]{2,1,0:T(8,128)S(1)}, u32[]{:S(2)}, u32[]{:S(2)}) %collective-permute-start.2) | collective-permute-done | bytes 131104 | tf_op jit(solution)/shard_map/ppermute | solution.py:64
  74.5 3.0 %collective-permute-start.3 = (f32[2,128,128]{2,1,0:T(8,128)S(1)}, f32[2,128,128]{2,1,0:T(8,128)S(1)}, u32[]{:S(2)}, u32[]{:S(2)}) collective-permute-start(f32[2,128,128]{2,1,0:T(8,128)S(1)} %broadcast_select_fusion.3), channel_id=1, source_target_pairs={{0,128},{16,144},{32,160},{48,176},{64,192},{80,208},{96,224},{112... | collective-permute-start | bytes 393224 | tf_op jit(solution)/shard_map/ppermute | solution.py:64
  77.8 2.5 %collective-permute-done.3 = f32[2,128,128]{2,1,0:T(8,128)S(1)} collective-permute-done((f32[2,128,128]{2,1,0:T(8,128)S(1)}, f32[2,128,128]{2,1,0:T(8,128)S(1)}, u32[]{:S(2)}, u32[]{:S(2)}) %collective-permute-start.3) | collective-permute-done | bytes 131104 | tf_op jit(solution)/shard_map/ppermute | solution.py:64
  80.4 3.8 %collective-permute-start.4 = (f32[2,128,128]{2,1,0:T(8,128)S(1)}, f32[2,128,128]{2,1,0:T(8,128)S(1)}, u32[]{:S(2)}, u32[]{:S(2)}) collective-permute-start(f32[2,128,128]{2,1,0:T(8,128)S(1)} %get-tuple-element.17), channel_id=1, source_target_pairs={{0,256},{16,272},{32,288},{48,304},{64,320},{80,336},{96,352},{112... | collective-permute-start | bytes 393224 | tf_op jit(solution)/shard_map/ppermute | solution.py:64
  84.4 4.0 %collective-permute-done.4 = f32[2,128,128]{2,1,0:T(8,128)S(1)} collective-permute-done((f32[2,128,128]{2,1,0:T(8,128)S(1)}, f32[2,128,128]{2,1,0:T(8,128)S(1)}, u32[]{:S(2)}, u32[]{:S(2)}) %collective-permute-start.4) | collective-permute-done | bytes 131104 | tf_op jit(solution)/shard_map/ppermute | solution.py:64
  88.5 4.3 %collective-permute-start.5 = (f32[2,128,128]{2,1,0:T(8,128)S(1)}, f32[2,128,128]{2,1,0:T(8,128)S(1)}, u32[]{:S(2)}, u32[]{:S(2)}) collective-permute-start(f32[2,128,128]{2,1,0:T(8,128)S(1)} %add_select_fusion.1), channel_id=1, source_target_pairs={{0,512},{16,528},{32,544},{48,560},{64,576},{80,592},{96,608},{112... | collective-permute-start | bytes 393224 | tf_op jit(solution)/shard_map/ppermute | solution.py:64
  93.1 6.4 %collective-permute-done.5 = f32[2,128,128]{2,1,0:T(8,128)S(1)} collective-permute-done((f32[2,128,128]{2,1,0:T(8,128)S(1)}, f32[2,128,128]{2,1,0:T(8,128)S(1)}, u32[]{:S(2)}, u32[]{:S(2)}) %collective-permute-start.5) | collective-permute-done | bytes 131104 | tf_op jit(solution)/shard_map/ppermute | solution.py:64
  99.7 7.2 %collective-permute-start.6 = (f32[2,128,128]{2,1,0:T(8,128)S(1)}, f32[2,128,128]{2,1,0:T(8,128)S(1)}, u32[]{:S(2)}, u32[]{:S(2)}) collective-permute-start(f32[2,128,128]{2,1,0:T(8,128)S(1)} %get-tuple-element.14), channel_id=1, source_target_pairs={{0,16},{16,0},{32,48},{48,32},{64,80},{80,64},{96,112},{112,96},{1... | collective-permute-start | bytes 393224 | tf_op jit(solution)/shard_map/ppermute | solution.py:96
  107.1 0.7 collective-permute-done.6
  107.9 0.3 fusion.13
  108.3 0.8 copy.86
  109.0 0.3 fusion.12
  109.5 0.8 copy.85
  110.2 0.3 fusion.11
  110.6 0.8 copy.84
  111.8 0.8 copy.83
  (37 shorter events, 3.7 us)
Async XLA Ops:
  2.7 52.6 %all-to-all-start = ((bf16[64,32,128]{2,0,1:T(8,128)(2,1)}), bf16[64,32,128]{2,0,1:T(8,128)(2,1)S(1)}, u32[]{:S(2)}, u32[]{:S(2)}) async-start(bf16[64,32,128]{2,0,1:T(8,128)(2,1)} %copy_bitcast_fusion), calls=%async_computation | async-start | bytes 1048576 | tf_op jit(solution)/shard_map/all_to_all | solution.py:115
  21.7 0.7 copy-start.1
  54.4 0.7 copy-start
  56.5 3.8 %collective-permute-start = (f32[2,128,128]{2,1,0:T(8,128)S(1)}, f32[2,128,128]{2,1,0:T(8,128)S(1)}, u32[]{:S(2)}, u32[]{:S(2)}) collective-permute-start(f32[2,128,128]{2,1,0:T(8,128)S(1)} %get-tuple-element.98), channel_id=1, source_target_pairs={{0,16},{16,0},{32,48},{48,32},{64,80},{80,64},{96,112},{112,96},{1... | collective-permute-start | bytes 393224 | tf_op jit(solution)/shard_map/ppermute | solution.py:61
  60.4 6.6 %collective-permute-start.1 = (f32[2,128,128]{2,1,0:T(8,128)S(1)}, f32[2,128,128]{2,1,0:T(8,128)S(1)}, u32[]{:S(2)}, u32[]{:S(2)}) collective-permute-start(f32[2,128,128]{2,1,0:T(8,128)S(1)} %broadcast_select_fusion.5), channel_id=1, source_target_pairs={{0,32},{16,48},{32,0},{48,16},{64,96},{80,112},{96,64},{112,80},{1... | collective-permute-start | bytes 393224 | tf_op jit(solution)/shard_map/ppermute | solution.py:64
  67.2 7.2 %collective-permute-start.2 = (f32[2,128,128]{2,1,0:T(8,128)S(1)}, f32[2,128,128]{2,1,0:T(8,128)S(1)}, u32[]{:S(2)}, u32[]{:S(2)}) collective-permute-start(f32[2,128,128]{2,1,0:T(8,128)S(1)} %get-tuple-element.20), channel_id=1, source_target_pairs={{0,64},{16,80},{32,96},{48,112},{64,0},{80,16},{96,32},{112,48},{1... | collective-permute-start | bytes 393224 | tf_op jit(solution)/shard_map/ppermute | solution.py:64
  74.5 5.7 %collective-permute-start.3 = (f32[2,128,128]{2,1,0:T(8,128)S(1)}, f32[2,128,128]{2,1,0:T(8,128)S(1)}, u32[]{:S(2)}, u32[]{:S(2)}) collective-permute-start(f32[2,128,128]{2,1,0:T(8,128)S(1)} %broadcast_select_fusion.3), channel_id=1, source_target_pairs={{0,128},{16,144},{32,160},{48,176},{64,192},{80,208},{96,224},{112... | collective-permute-start | bytes 393224 | tf_op jit(solution)/shard_map/ppermute | solution.py:64
  80.4 8.0 %collective-permute-start.4 = (f32[2,128,128]{2,1,0:T(8,128)S(1)}, f32[2,128,128]{2,1,0:T(8,128)S(1)}, u32[]{:S(2)}, u32[]{:S(2)}) collective-permute-start(f32[2,128,128]{2,1,0:T(8,128)S(1)} %get-tuple-element.17), channel_id=1, source_target_pairs={{0,256},{16,272},{32,288},{48,304},{64,320},{80,336},{96,352},{112... | collective-permute-start | bytes 393224 | tf_op jit(solution)/shard_map/ppermute | solution.py:64
  88.5 11.0 %collective-permute-start.5 = (f32[2,128,128]{2,1,0:T(8,128)S(1)}, f32[2,128,128]{2,1,0:T(8,128)S(1)}, u32[]{:S(2)}, u32[]{:S(2)}) collective-permute-start(f32[2,128,128]{2,1,0:T(8,128)S(1)} %add_select_fusion.1), channel_id=1, source_target_pairs={{0,512},{16,528},{32,544},{48,560},{64,576},{80,592},{96,608},{112... | collective-permute-start | bytes 393224 | tf_op jit(solution)/shard_map/ppermute | solution.py:64
  99.7 8.2 %collective-permute-start.6 = (f32[2,128,128]{2,1,0:T(8,128)S(1)}, f32[2,128,128]{2,1,0:T(8,128)S(1)}, u32[]{:S(2)}, u32[]{:S(2)}) collective-permute-start(f32[2,128,128]{2,1,0:T(8,128)S(1)} %get-tuple-element.14), channel_id=1, source_target_pairs={{0,16},{16,0},{32,48},{48,32},{64,80},{80,64},{96,112},{112,96},{1... | collective-permute-start | bytes 393224 | tf_op jit(solution)/shard_map/ppermute | solution.py:96

commit v9 on v8

--- a/solution.py
+++ b/solution.py
@@ -36,8 +36,8 @@
     return (weights, enter_w, leave_w)
 
 
-def butterfly_scan(forward_term, backward_term, end_segments, before_segments, here, decays,
-                   group_len, count):
+def butterfly_scan(forward_term, backward_term, sent_term, end_segments, before_segments, here,
+                   decays, group_len, count):
     def clipped(table, index):
         return table[jnp.clip(index, 0, count - 1)]
 
@@ -58,7 +58,7 @@
         other = jnp.where(upper, start - shift, start + shift)
         pairs = [(i, i ^ shift) for i in range(count)]
         if shift == 1:
-            got_f = got_b = lax.ppermute(jnp.where(odd, total_f, total_b), "ctx", pairs)
+            got_f = got_b = lax.ppermute(sent_term, "ctx", pairs)
             use_f = use_b = jnp.zeros((), jnp.float32)
         else:
             got_f = got_b = lax.ppermute(jnp.where(odd, total_b, total_f), "ctx", pairs)
@@ -100,7 +100,7 @@
 
 
 def on_device(queries, keys, values, out_grad, decay_rate, doc_lengths):
-    precise = lax.Precision.HIGHEST
+    precise = lax.Precision.HIGH
     rows_in = queries.shape[0]
     count = lax.axis_size("ctx")
     group_len = rows_in * lax.axis_size("exp")
@@ -123,10 +123,23 @@
     g_wide = g_rows.astype(jnp.float32)
     enter_t = enter_w.T[:, :, None]
     leave_t = leave_w.T[:, :, None]
-    forward_term = jnp.einsum("jhd,jhe->hde", k_wide * leave_t, v_wide, precision=precise)
-    backward_term = jnp.einsum("ihd,ihe->hde", q_wide * enter_t, g_wide, precision=precise)
+    odd = here % 2 == 1
+    sent_term = jnp.einsum(
+        "jhd,jhe->hde",
+        jnp.where(odd, k_wide * leave_t, q_wide * enter_t),
+        jnp.where(odd, v_wide, g_wide),
+        precision=precise,
+    )
+    kept_term = jnp.einsum(
+        "jhd,jhe->hde",
+        jnp.where(odd, q_wide * enter_t, k_wide * leave_t),
+        jnp.where(odd, g_wide, v_wide),
+        precision=precise,
+    )
+    forward_term = jnp.where(odd, sent_term, kept_term)
+    backward_term = jnp.where(odd, kept_term, sent_term)
     state_in, state_next = butterfly_scan(
-        forward_term, backward_term, end_segments, before_segments, here, decay_rate, group_len,
+        forward_term, backward_term, sent_term, end_segments, before_segments, here, decay_rate, group_len,
         count,
     )
     scores = (

time: 114 us -> 114 us (level)
  no operation moved by 1% of the time
where the time goes in v9:
time: 114 us; the launch traced here: 113 us
  starting transfers between devices  47.5 us (42%)
  between operations  29.5 us (26%)
  waiting for transfers between devices  20 us (18%)
  local copies, waits for them, and re-layouts  7.01 us (6%)
  other arithmetic  5.36 us (5%)
  matrix products  3.56 us (3%)
    ppermute x5, starting transfers between devices, butterfly_scan(): got_f = got_b = lax.ppermute(jnp.where(odd, total_b, total_f), 'ctx', pairs)  18.8 us
    all_to_all x1, starting transfers between devices, on_device(): lax.all_to_all(joined, 'exp', split_axis=1, concat_axis=0, tiled=True)  18.6 us
    ppermute x5, waiting for transfers between devices, butterfly_scan(): got_f = got_b = lax.ppermute(jnp.where(odd, total_b, total_f), 'ctx', pairs)  18.4 us
    ppermute x1, starting transfers between devices, butterfly_scan(): lax.ppermute(jnp.where(odd, handed_b, handed_f), 'ctx', [(i, i ^ 1) for i...  7.21 us
    unnamed x8, local copies, waits for them, and re-layouts  4.34 us
    ppermute x1, starting transfers between devices, butterfly_scan(): got_f = got_b = lax.ppermute(sent_term, 'ctx', pairs)  2.86 us
  transfers between devices with their start and end apart: 8, of which 7 were waited for; matrix products, arithmetic and copies ran while one was open for 5% of the time, Pallas kernels for 0%

profile of v9, /device:TPU:57, one launch (start us, length us, event | category | flops | bytes accessed | tf_op | source)
XLA Modules:
  0.0 112.9 jit_solution(11987506445188890473)
XLA Ops:
  0.6 2.0 %copy_bitcast_fusion = bf16[64,32,128]{2,0,1:T(8,128)(2,1)} fusion(bf16[16,4096]{1,0:T(8,128)(2,1)} %param.9, bf16[16,4096]{1,0:T(8,128)(2,1)} %param.8, bf16[16,4096]{1,0:T(8,128)(2,1)} %param.7, bf16[16,4096]{1,0:T(8,128)(2,1)} %param.6), kind=kLoop, calls=%fused_computation.24 | loop fusion | flops 2097152 | bytes 1048576 | tf_op jit(solution)/shard_map/reshape | solution.py:114
  2.7 18.6 %all-to-all-start = ((bf16[64,32,128]{2,0,1:T(8,128)(2,1)}), bf16[64,32,128]{2,0,1:T(8,128)(2,1)S(1)}, u32[]{:S(2)}, u32[]{:S(2)}) async-start(bf16[64,32,128]{2,0,1:T(8,128)(2,1)} %copy_bitcast_fusion), calls=%async_computation | async-start | bytes 1048576 | tf_op jit(solution)/shard_map/all_to_all | solution.py:115
  21.7 0.6 copy-done.1
  22.6 0.7 fusion.29
  28.4 0.8 fusion.30
  42.2 0.6 slice.18
  52.9 0.7 fusion.25
  53.6 1.3 %compare_convert_fusion.2 = (f32[256]{0:T(256)S(1)}, f32[256]{0:T(256)S(1)}) fusion(s32[256]{0:T(256)S(1)} %convert_reduce_fusion, s32[]{:T(128)} %bitcast.12, s32[]{:T(128)} %fusion.25), kind=kLoop, calls=%fused_computation.71 | loop fusion | flops 1024 | bytes 3080 | tf_op jit(solution)/shard_map/convert_element_type | solution.py:27
  54.9 0.6 copy-done
  55.9 0.6 fusion.14
  56.5 2.9 %collective-permute-start = (f32[2,128,128]{2,1,0:T(8,128)S(1)}, f32[2,128,128]{2,1,0:T(8,128)S(1)}, u32[]{:S(2)}, u32[]{:S(2)}) collective-permute-start(f32[2,128,128]{2,1,0:T(8,128)S(1)} %fusion.14), channel_id=1, source_target_pairs={{0,16},{16,0},{32,48},{48,32},{64,80},{80,64},{96,112},{112,96},{1... | collective-permute-start | bytes 393224 | tf_op jit(solution)/shard_map/ppermute | solution.py:61
  59.5 0.9 collective-permute-done
  60.4 0.6 broadcast_select_fusion.5
  61.0 3.1 %collective-permute-start.1 = (f32[2,128,128]{2,1,0:T(8,128)S(1)}, f32[2,128,128]{2,1,0:T(8,128)S(1)}, u32[]{:S(2)}, u32[]{:S(2)}) collective-permute-start(f32[2,128,128]{2,1,0:T(8,128)S(1)} %get-tuple-element.20), channel_id=1, source_target_pairs={{0,32},{16,48},{32,0},{48,16},{64,96},{80,112},{96,64},{112,80},{1... | collective-permute-start | bytes 393224 | tf_op jit(solution)/shard_map/ppermute | solution.py:64
  64.3 3.2 %collective-permute-done.1 = f32[2,128,128]{2,1,0:T(8,128)S(1)} collective-permute-done((f32[2,128,128]{2,1,0:T(8,128)S(1)}, f32[2,128,128]{2,1,0:T(8,128)S(1)}, u32[]{:S(2)}, u32[]{:S(2)}) %collective-permute-start.1) | collective-permute-done | bytes 131104 | tf_op jit(solution)/shard_map/ppermute | solution.py:64
  67.7 4.7 %collective-permute-start.2 = (f32[2,128,128]{2,1,0:T(8,128)S(1)}, f32[2,128,128]{2,1,0:T(8,128)S(1)}, u32[]{:S(2)}, u32[]{:S(2)}) collective-permute-start(f32[2,128,128]{2,1,0:T(8,128)S(1)} %broadcast_select_fusion.4), channel_id=1, source_target_pairs={{0,64},{16,80},{32,96},{48,112},{64,0},{80,16},{96,32},{112,48},{1... | collective-permute-start | bytes 393224 | tf_op jit(solution)/shard_map/ppermute | solution.py:64
  72.6 2.3 %collective-permute-done.2 = f32[2,128,128]{2,1,0:T(8,128)S(1)} collective-permute-done((f32[2,128,128]{2,1,0:T(8,128)S(1)}, f32[2,128,128]{2,1,0:T(8,128)S(1)}, u32[]{:S(2)}, u32[]{:S(2)}) %collective-permute-start.2) | collective-permute-done | bytes 131104 | tf_op jit(solution)/shard_map/ppermute | solution.py:64
  75.0 3.0 %collective-permute-start.3 = (f32[2,128,128]{2,1,0:T(8,128)S(1)}, f32[2,128,128]{2,1,0:T(8,128)S(1)}, u32[]{:S(2)}, u32[]{:S(2)}) collective-permute-start(f32[2,128,128]{2,1,0:T(8,128)S(1)} %get-tuple-element.17), channel_id=1, source_target_pairs={{0,128},{16,144},{32,160},{48,176},{64,192},{80,208},{96,224},{112... | collective-permute-start | bytes 393224 | tf_op jit(solution)/shard_map/ppermute | solution.py:64
  78.0 0.3 convolution_bitcast_fusion.3
  78.3 2.5 %collective-permute-done.3 = f32[2,128,128]{2,1,0:T(8,128)S(1)} collective-permute-done((f32[2,128,128]{2,1,0:T(8,128)S(1)}, f32[2,128,128]{2,1,0:T(8,128)S(1)}, u32[]{:S(2)}, u32[]{:S(2)}) %collective-permute-start.3) | collective-permute-done | bytes 131104 | tf_op jit(solution)/shard_map/ppermute | solution.py:64
  80.9 3.8 %collective-permute-start.4 = (f32[2,128,128]{2,1,0:T(8,128)S(1)}, f32[2,128,128]{2,1,0:T(8,128)S(1)}, u32[]{:S(2)}, u32[]{:S(2)}) collective-permute-start(f32[2,128,128]{2,1,0:T(8,128)S(1)} %broadcast_select_fusion.2), channel_id=1, source_target_pairs={{0,256},{16,272},{32,288},{48,304},{64,320},{80,336},{96,352},{112... | collective-permute-start | bytes 393224 | tf_op jit(solution)/shard_map/ppermute | solution.py:64
  84.8 4.0 %collective-permute-done.4 = f32[2,128,128]{2,1,0:T(8,128)S(1)} collective-permute-done((f32[2,128,128]{2,1,0:T(8,128)S(1)}, f32[2,128,128]{2,1,0:T(8,128)S(1)}, u32[]{:S(2)}, u32[]{:S(2)}) %collective-permute-start.4) | collective-permute-done | bytes 131104 | tf_op jit(solution)/shard_map/ppermute | solution.py:64
  89.0 4.3 %collective-permute-start.5 = (f32[2,128,128]{2,1,0:T(8,128)S(1)}, f32[2,128,128]{2,1,0:T(8,128)S(1)}, u32[]{:S(2)}, u32[]{:S(2)}) collective-permute-start(f32[2,128,128]{2,1,0:T(8,128)S(1)} %add_select_fusion.1), channel_id=1, source_target_pairs={{0,512},{16,528},{32,544},{48,560},{64,576},{80,592},{96,608},{112... | collective-permute-start | bytes 393224 | tf_op jit(solution)/shard_map/ppermute | solution.py:64
  93.3 0.3 convolution_bitcast_fusion.2
  93.6 6.4 %collective-permute-done.5 = f32[2,128,128]{2,1,0:T(8,128)S(1)} collective-permute-done((f32[2,128,128]{2,1,0:T(8,128)S(1)}, f32[2,128,128]{2,1,0:T(8,128)S(1)}, u32[]{:S(2)}, u32[]{:S(2)}) %collective-permute-start.5) | collective-permute-done | bytes 131104 | tf_op jit(solution)/shard_map/ppermute | solution.py:64
  100.2 7.2 %collective-permute-start.6 = (f32[2,128,128]{2,1,0:T(8,128)S(1)}, f32[2,128,128]{2,1,0:T(8,128)S(1)}, u32[]{:S(2)}, u32[]{:S(2)}) collective-permute-start(f32[2,128,128]{2,1,0:T(8,128)S(1)} %get-tuple-element.14), channel_id=1, source_target_pairs={{0,16},{16,0},{32,48},{48,32},{64,80},{80,64},{96,112},{112,96},{1... | collective-permute-start | bytes 393224 | tf_op jit(solution)/shard_map/ppermute | solution.py:96
  107.7 0.7 collective-permute-done.6
  108.8 0.8 copy.83
  109.9 0.8 copy.82
  110.7 0.2 fusion.11
  111.1 0.8 copy.81
  112.2 0.8 copy.80
  (36 shorter events, 3.5 us)
Async XLA Ops:
  2.7 53.2 %all-to-all-start = ((bf16[64,32,128]{2,0,1:T(8,128)(2,1)}), bf16[64,32,128]{2,0,1:T(8,128)(2,1)S(1)}, u32[]{:S(2)}, u32[]{:S(2)}) async-start(bf16[64,32,128]{2,0,1:T(8,128)(2,1)} %copy_bitcast_fusion), calls=%async_computation | async-start | bytes 1048576 | tf_op jit(solution)/shard_map/all_to_all | solution.py:115
  21.7 0.7 copy-start.1
  54.9 0.7 copy-start
  56.5 3.8 %collective-permute-start = (f32[2,128,128]{2,1,0:T(8,128)S(1)}, f32[2,128,128]{2,1,0:T(8,128)S(1)}, u32[]{:S(2)}, u32[]{:S(2)}) collective-permute-start(f32[2,128,128]{2,1,0:T(8,128)S(1)} %fusion.14), channel_id=1, source_target_pairs={{0,16},{16,0},{32,48},{48,32},{64,80},{80,64},{96,112},{112,96},{1... | collective-permute-start | bytes 393224 | tf_op jit(solution)/shard_map/ppermute | solution.py:61
  61.0 6.6 %collective-permute-start.1 = (f32[2,128,128]{2,1,0:T(8,128)S(1)}, f32[2,128,128]{2,1,0:T(8,128)S(1)}, u32[]{:S(2)}, u32[]{:S(2)}) collective-permute-start(f32[2,128,128]{2,1,0:T(8,128)S(1)} %get-tuple-element.20), channel_id=1, source_target_pairs={{0,32},{16,48},{32,0},{48,16},{64,96},{80,112},{96,64},{112,80},{1... | collective-permute-start | bytes 393224 | tf_op jit(solution)/shard_map/ppermute | solution.py:64
  67.7 7.2 %collective-permute-start.2 = (f32[2,128,128]{2,1,0:T(8,128)S(1)}, f32[2,128,128]{2,1,0:T(8,128)S(1)}, u32[]{:S(2)}, u32[]{:S(2)}) collective-permute-start(f32[2,128,128]{2,1,0:T(8,128)S(1)} %broadcast_select_fusion.4), channel_id=1, source_target_pairs={{0,64},{16,80},{32,96},{48,112},{64,0},{80,16},{96,32},{112,48},{1... | collective-permute-start | bytes 393224 | tf_op jit(solution)/shard_map/ppermute | solution.py:64
  75.0 5.7 %collective-permute-start.3 = (f32[2,128,128]{2,1,0:T(8,128)S(1)}, f32[2,128,128]{2,1,0:T(8,128)S(1)}, u32[]{:S(2)}, u32[]{:S(2)}) collective-permute-start(f32[2,128,128]{2,1,0:T(8,128)S(1)} %get-tuple-element.17), channel_id=1, source_target_pairs={{0,128},{16,144},{32,160},{48,176},{64,192},{80,208},{96,224},{112... | collective-permute-start | bytes 393224 | tf_op jit(solution)/shard_map/ppermute | solution.py:64
  80.9 8.0 %collective-permute-start.4 = (f32[2,128,128]{2,1,0:T(8,128)S(1)}, f32[2,128,128]{2,1,0:T(8,128)S(1)}, u32[]{:S(2)}, u32[]{:S(2)}) collective-permute-start(f32[2,128,128]{2,1,0:T(8,128)S(1)} %broadcast_select_fusion.2), channel_id=1, source_target_pairs={{0,256},{16,272},{32,288},{48,304},{64,320},{80,336},{96,352},{112... | collective-permute-start | bytes 393224 | tf_op jit(solution)/shard_map/ppermute | solution.py:64
  89.0 11.0 %collective-permute-start.5 = (f32[2,128,128]{2,1,0:T(8,128)S(1)}, f32[2,128,128]{2,1,0:T(8,128)S(1)}, u32[]{:S(2)}, u32[]{:S(2)}) collective-permute-start(f32[2,128,128]{2,1,0:T(8,128)S(1)} %add_select_fusion.1), channel_id=1, source_target_pairs={{0,512},{16,528},{32,544},{48,560},{64,576},{80,592},{96,608},{112... | collective-permute-start | bytes 393224 | tf_op jit(solution)/shard_map/ppermute | solution.py:64
  100.2 8.2 %collective-permute-start.6 = (f32[2,128,128]{2,1,0:T(8,128)S(1)}, f32[2,128,128]{2,1,0:T(8,128)S(1)}, u32[]{:S(2)}, u32[]{:S(2)}) collective-permute-start(f32[2,128,128]{2,1,0:T(8,128)S(1)} %get-tuple-element.14), channel_id=1, source_target_pairs={{0,16},{16,0},{32,48},{48,32},{64,80},{80,64},{96,112},{112,96},{1... | collective-permute-start | bytes 393224 | tf_op jit(solution)/shard_map/ppermute | solution.py:96

commit v10 on v7

--- a/solution.py
+++ b/solution.py
@@ -57,6 +57,8 @@
         start = (here // shift) * shift
         other = jnp.where(upper, start - shift, start + shift)
         pairs = [(i, i ^ shift) for i in range(count)]
+        if shift > 1 and shift * 2 >= count:
+            pairs = [(i, j) for i, j in pairs if (i % 2 == 0) == (i < j)]
         if shift == 1:
             got = lax.ppermute(jnp.stack([total_f, total_b]), "ctx", pairs)
             got_f, got_b = got[0], got[1]

time: 114 us -> 113 us (level)
  waiting for transfers between devices: 20.1 us -> 15.4 us
  starting transfers between devices: 47.5 us -> 51.4 us
    ppermute x5, waiting for transfers between devices: 18.4 us -> 13.7 us  [butterfly_scan(): got_f = got_b = lax.ppermute(jnp.where(odd, total_b, total_f), 'ctx', pairs)]
    ppermute x1, starting transfers between devices: 7.21 us -> 11.1 us  [butterfly_scan(): lax.ppermute(jnp.where(odd, behind, ahead), 'ctx', [(i, i ^ 1) for i in r...]
where the time goes in v10:
time: 113 us; the launch traced here: 112 us
  starting transfers between devices  51.4 us (45%)
  between operations  28.8 us (25%)
  waiting for transfers between devices  15.4 us (14%)
  local copies, waits for them, and re-layouts  6.99 us (6%)
  other arithmetic  5.34 us (5%)
  matrix products  3.88 us (3%)
    ppermute x5, starting transfers between devices, butterfly_scan(): got_f = got_b = lax.ppermute(jnp.where(odd, total_b, total_f), 'ctx', pairs)  18.8 us
    all_to_all x1, starting transfers between devices, on_device(): lax.all_to_all(joined, 'exp', split_axis=1, concat_axis=0, tiled=True)  18.6 us
    ppermute x5, waiting for transfers between devices, butterfly_scan(): got_f = got_b = lax.ppermute(jnp.where(odd, total_b, total_f), 'ctx', pairs)  13.7 us
    ppermute x1, starting transfers between devices, butterfly_scan(): lax.ppermute(jnp.where(odd, behind, ahead), 'ctx', [(i, i ^ 1) for i in r...  11.1 us
    unnamed x8, local copies, waits for them, and re-layouts  4.35 us
    ppermute x1, starting transfers between devices, butterfly_scan(): got = lax.ppermute(jnp.stack([total_f, total_b]), 'ctx', pairs)  2.87 us
  transfers between devices with their start and end apart: 8, of which 7 were waited for; matrix products, arithmetic and copies ran while one was open for 5% of the time, Pallas kernels for 0%

profile of v10, /device:TPU:57, one launch (start us, length us, event | category | flops | bytes accessed | tf_op | source)
XLA Modules:
  0.0 111.7 jit_solution(2422930378998579415)
XLA Ops:
  0.6 2.0 %copy_bitcast_fusion = bf16[64,32,128]{2,0,1:T(8,128)(2,1)} fusion(bf16[16,4096]{1,0:T(8,128)(2,1)} %param.9, bf16[16,4096]{1,0:T(8,128)(2,1)} %param.8, bf16[16,4096]{1,0:T(8,128)(2,1)} %param.7, bf16[16,4096]{1,0:T(8,128)(2,1)} %param.6), kind=kLoop, calls=%fused_computation.24 | loop fusion | flops 2097152 | bytes 1048576 | tf_op jit(solution)/shard_map/reshape | solution.py:119
  2.7 18.6 %all-to-all-start = ((bf16[64,32,128]{2,0,1:T(8,128)(2,1)}), bf16[64,32,128]{2,0,1:T(8,128)(2,1)S(1)}, u32[]{:S(2)}, u32[]{:S(2)}) async-start(bf16[64,32,128]{2,0,1:T(8,128)(2,1)} %copy_bitcast_fusion), calls=%async_computation | async-start | bytes 1048576 | tf_op jit(solution)/shard_map/all_to_all | solution.py:120
  21.7 0.6 copy-done.1
  22.6 0.7 fusion.28
  27.0 0.8 fusion.27
  51.6 0.6 slice.24
  52.2 0.6 fusion.23
  52.8 0.7 copy-done
  53.5 1.2 %compare_convert_fusion.2 = (f32[256]{0:T(256)S(1)}, f32[256]{0:T(256)S(1)}) fusion(s32[256]{0:T(256)S(1)} %convert_reduce_fusion, s32[]{:T(128)} %bitcast.11, s32[]{:T(128)} %fusion.23), kind=kLoop, calls=%fused_computation.66 | loop fusion | flops 1024 | bytes 3080 | tf_op jit(solution)/shard_map/convert_element_type | solution.py:27
  55.0 0.5 fusion.17
  55.5 0.5 fusion.14
  56.1 2.9 %collective-permute-start = (f32[2,2,128,128]{3,2,1,0:T(8,128)S(1)}, f32[2,2,128,128]{3,2,1,0:T(8,128)S(1)}, u32[]{:S(2)}, u32[]{:S(2)}) collective-permute-start(f32[2,2,128,128]{3,2,1,0:T(8,128)S(1)} %pad_maximum_fusion), channel_id=1, source_target_pairs={{0,16},{16,0},{32,48},{48,32},{64,80},{80,64},{96,112},{112,96},{1... | collective-permute-start | bytes 786440 | tf_op jit(solution)/shard_map/ppermute | solution.py:63
  59.1 1.0 collective-permute-done
  60.2 3.1 %collective-permute-start.1 = (f32[2,128,128]{2,1,0:T(8,128)S(1)}, f32[2,128,128]{2,1,0:T(8,128)S(1)}, u32[]{:S(2)}, u32[]{:S(2)}) collective-permute-start(f32[2,128,128]{2,1,0:T(8,128)S(1)} %get-tuple-element.20), channel_id=1, source_target_pairs={{0,32},{16,48},{32,0},{48,16},{64,96},{80,112},{96,64},{112,80},{1... | collective-permute-start | bytes 393224 | tf_op jit(solution)/shard_map/ppermute | solution.py:67
  63.6 3.2 %collective-permute-done.1 = f32[2,128,128]{2,1,0:T(8,128)S(1)} collective-permute-done((f32[2,128,128]{2,1,0:T(8,128)S(1)}, f32[2,128,128]{2,1,0:T(8,128)S(1)}, u32[]{:S(2)}, u32[]{:S(2)}) %collective-permute-start.1) | collective-permute-done | bytes 131104 | tf_op jit(solution)/shard_map/ppermute | solution.py:67
  66.9 4.7 %collective-permute-start.2 = (f32[2,128,128]{2,1,0:T(8,128)S(1)}, f32[2,128,128]{2,1,0:T(8,128)S(1)}, u32[]{:S(2)}, u32[]{:S(2)}) collective-permute-start(f32[2,128,128]{2,1,0:T(8,128)S(1)} %broadcast_select_fusion.3), channel_id=1, source_target_pairs={{0,64},{16,80},{32,96},{48,112},{64,0},{80,16},{96,32},{112,48},{1... | collective-permute-start | bytes 393224 | tf_op jit(solution)/shard_map/ppermute | solution.py:67
  71.8 2.3 %collective-permute-done.2 = f32[2,128,128]{2,1,0:T(8,128)S(1)} collective-permute-done((f32[2,128,128]{2,1,0:T(8,128)S(1)}, f32[2,128,128]{2,1,0:T(8,128)S(1)}, u32[]{:S(2)}, u32[]{:S(2)}) %collective-permute-start.2) | collective-permute-done | bytes 131104 | tf_op jit(solution)/shard_map/ppermute | solution.py:67
  74.3 3.0 %collective-permute-start.3 = (f32[2,128,128]{2,1,0:T(8,128)S(1)}, f32[2,128,128]{2,1,0:T(8,128)S(1)}, u32[]{:S(2)}, u32[]{:S(2)}) collective-permute-start(f32[2,128,128]{2,1,0:T(8,128)S(1)} %get-tuple-element.17), channel_id=1, source_target_pairs={{0,128},{16,144},{32,160},{48,176},{64,192},{80,208},{96,224},{112... | collective-permute-start | bytes 393224 | tf_op jit(solution)/shard_map/ppermute | solution.py:67
  77.5 2.5 %collective-permute-done.3 = f32[2,128,128]{2,1,0:T(8,128)S(1)} collective-permute-done((f32[2,128,128]{2,1,0:T(8,128)S(1)}, f32[2,128,128]{2,1,0:T(8,128)S(1)}, u32[]{:S(2)}, u32[]{:S(2)}) %collective-permute-start.3) | collective-permute-done | bytes 131104 | tf_op jit(solution)/shard_map/ppermute | solution.py:67
  80.1 3.8 %collective-permute-start.4 = (f32[2,128,128]{2,1,0:T(8,128)S(1)}, f32[2,128,128]{2,1,0:T(8,128)S(1)}, u32[]{:S(2)}, u32[]{:S(2)}) collective-permute-start(f32[2,128,128]{2,1,0:T(8,128)S(1)} %broadcast_select_fusion.1), channel_id=1, source_target_pairs={{0,256},{16,272},{32,288},{48,304},{64,320},{80,336},{96,352},{112... | collective-permute-start | bytes 393224 | tf_op jit(solution)/shard_map/ppermute | solution.py:67
  84.1 4.0 %collective-permute-done.4 = f32[2,128,128]{2,1,0:T(8,128)S(1)} collective-permute-done((f32[2,128,128]{2,1,0:T(8,128)S(1)}, f32[2,128,128]{2,1,0:T(8,128)S(1)}, u32[]{:S(2)}, u32[]{:S(2)}) %collective-permute-start.4) | collective-permute-done | bytes 131104 | tf_op jit(solution)/shard_map/ppermute | solution.py:67
  88.3 4.3 %collective-permute-start.5 = (f32[2,128,128]{2,1,0:T(8,128)S(1)}, f32[2,128,128]{2,1,0:T(8,128)S(1)}, u32[]{:S(2)}, u32[]{:S(2)}) collective-permute-start(f32[2,128,128]{2,1,0:T(8,128)S(1)} %add_select_fusion), channel_id=1, source_target_pairs={{0,512},{32,544},{64,576},{96,608},{128,640},{160,672},{192,704},{... | collective-permute-start | bytes 393224 | tf_op jit(solution)/shard_map/ppermute | solution.py:67
  92.9 1.7 %collective-permute-done.5 = f32[2,128,128]{2,1,0:T(8,128)S(1)} collective-permute-done((f32[2,128,128]{2,1,0:T(8,128)S(1)}, f32[2,128,128]{2,1,0:T(8,128)S(1)}, u32[]{:S(2)}, u32[]{:S(2)}) %collective-permute-start.5) | collective-permute-done | bytes 131104 | tf_op jit(solution)/shard_map/ppermute | solution.py:67
  94.7 11.1 %collective-permute-start.6 = (f32[2,128,128]{2,1,0:T(8,128)S(1)}, f32[2,128,128]{2,1,0:T(8,128)S(1)}, u32[]{:S(2)}, u32[]{:S(2)}) collective-permute-start(f32[2,128,128]{2,1,0:T(8,128)S(1)} %get-tuple-element.14), channel_id=1, source_target_pairs={{0,16},{16,0},{32,48},{48,32},{64,80},{80,64},{96,112},{112,96},{1... | collective-permute-start | bytes 393224 | tf_op jit(solution)/shard_map/ppermute | solution.py:94
  106.0 0.7 collective-permute-done.6
  106.8 0.4 fusion.13
  107.3 0.8 copy.86
  108.0 0.3 fusion.12
  108.5 0.8 copy.85
  109.7 0.8 copy.84
  110.5 0.3 fusion.10
  111.0 0.8 copy.83
  (39 shorter events, 3.8 us)
Async XLA Ops:
  2.7 52.2 %all-to-all-start = ((bf16[64,32,128]{2,0,1:T(8,128)(2,1)}), bf16[64,32,128]{2,0,1:T(8,128)(2,1)S(1)}, u32[]{:S(2)}, u32[]{:S(2)}) async-start(bf16[64,32,128]{2,0,1:T(8,128)(2,1)} %copy_bitcast_fusion), calls=%async_computation | async-start | bytes 1048576 | tf_op jit(solution)/shard_map/all_to_all | solution.py:120
  21.7 0.7 copy-start.1
  52.8 0.7 copy-start
  56.1 4.0 %collective-permute-start = (f32[2,2,128,128]{3,2,1,0:T(8,128)S(1)}, f32[2,2,128,128]{3,2,1,0:T(8,128)S(1)}, u32[]{:S(2)}, u32[]{:S(2)}) collective-permute-start(f32[2,2,128,128]{3,2,1,0:T(8,128)S(1)} %pad_maximum_fusion), channel_id=1, source_target_pairs={{0,16},{16,0},{32,48},{48,32},{64,80},{80,64},{96,112},{112,96},{1... | collective-permute-start | bytes 786440 | tf_op jit(solution)/shard_map/ppermute | solution.py:63
  60.2 6.6 %collective-permute-start.1 = (f32[2,128,128]{2,1,0:T(8,128)S(1)}, f32[2,128,128]{2,1,0:T(8,128)S(1)}, u32[]{:S(2)}, u32[]{:S(2)}) collective-permute-start(f32[2,128,128]{2,1,0:T(8,128)S(1)} %get-tuple-element.20), channel_id=1, source_target_pairs={{0,32},{16,48},{32,0},{48,16},{64,96},{80,112},{96,64},{112,80},{1... | collective-permute-start | bytes 393224 | tf_op jit(solution)/shard_map/ppermute | solution.py:67
  66.9 7.2 %collective-permute-start.2 = (f32[2,128,128]{2,1,0:T(8,128)S(1)}, f32[2,128,128]{2,1,0:T(8,128)S(1)}, u32[]{:S(2)}, u32[]{:S(2)}) collective-permute-start(f32[2,128,128]{2,1,0:T(8,128)S(1)} %broadcast_select_fusion.3), channel_id=1, source_target_pairs={{0,64},{16,80},{32,96},{48,112},{64,0},{80,16},{96,32},{112,48},{1... | collective-permute-start | bytes 393224 | tf_op jit(solution)/shard_map/ppermute | solution.py:67
  74.3 5.7 %collective-permute-start.3 = (f32[2,128,128]{2,1,0:T(8,128)S(1)}, f32[2,128,128]{2,1,0:T(8,128)S(1)}, u32[]{:S(2)}, u32[]{:S(2)}) collective-permute-start(f32[2,128,128]{2,1,0:T(8,128)S(1)} %get-tuple-element.17), channel_id=1, source_target_pairs={{0,128},{16,144},{32,160},{48,176},{64,192},{80,208},{96,224},{112... | collective-permute-start | bytes 393224 | tf_op jit(solution)/shard_map/ppermute | solution.py:67
  80.1 8.0 %collective-permute-start.4 = (f32[2,128,128]{2,1,0:T(8,128)S(1)}, f32[2,128,128]{2,1,0:T(8,128)S(1)}, u32[]{:S(2)}, u32[]{:S(2)}) collective-permute-start(f32[2,128,128]{2,1,0:T(8,128)S(1)} %broadcast_select_fusion.1), channel_id=1, source_target_pairs={{0,256},{16,272},{32,288},{48,304},{64,320},{80,336},{96,352},{112... | collective-permute-start | bytes 393224 | tf_op jit(solution)/shard_map/ppermute | solution.py:67
  88.3 6.3 %collective-permute-start.5 = (f32[2,128,128]{2,1,0:T(8,128)S(1)}, f32[2,128,128]{2,1,0:T(8,128)S(1)}, u32[]{:S(2)}, u32[]{:S(2)}) collective-permute-start(f32[2,128,128]{2,1,0:T(8,128)S(1)} %add_select_fusion), channel_id=1, source_target_pairs={{0,512},{32,544},{64,576},{96,608},{128,640},{160,672},{192,704},{... | collective-permute-start | bytes 393224 | tf_op jit(solution)/shard_map/ppermute | solution.py:67
  94.7 12.0 %collective-permute-start.6 = (f32[2,128,128]{2,1,0:T(8,128)S(1)}, f32[2,128,128]{2,1,0:T(8,128)S(1)}, u32[]{:S(2)}, u32[]{:S(2)}) collective-permute-start(f32[2,128,128]{2,1,0:T(8,128)S(1)} %get-tuple-element.14), channel_id=1, source_target_pairs={{0,16},{16,0},{32,48},{48,32},{64,80},{80,64},{96,112},{112,96},{1... | collective-permute-start | bytes 393224 | tf_op jit(solution)/shard_map/ppermute | solution.py:94

commit v11 on v10

--- a/solution.py
+++ b/solution.py
@@ -59,6 +59,13 @@
         pairs = [(i, i ^ shift) for i in range(count)]
         if shift > 1 and shift * 2 >= count:
             pairs = [(i, j) for i, j in pairs if (i % 2 == 0) == (i < j)]
+        elif shift > 1 and shift * 4 == count:
+            half = count // 2
+            pairs = [
+                (i, j)
+                for i, j in pairs
+                if (j % 2 == 0 and (j > i or j < half)) or (j % 2 == 1 and (j < i or j >= half))
+            ]
         if shift == 1:
             got = lax.ppermute(jnp.stack([total_f, total_b]), "ctx", pairs)
             got_f, got_b = got[0], got[1]

time: 113 us -> 113 us (level)
    ppermute x1, starting transfers between devices: 11.1 us -> 14.2 us  [butterfly_scan(): lax.ppermute(jnp.where(odd, behind, ahead), 'ctx', [(i, i ^ 1) for i in r...]
    ppermute x5, starting transfers between devices: 18.8 us -> 15.8 us  [butterfly_scan(): got_f = got_b = lax.ppermute(jnp.where(odd, total_b, total_f), 'ctx', pairs)]
where the time goes in v11:
time: 113 us; the launch traced here: 112 us
  starting transfers between devices  51.5 us (46%)
  between operations  28.8 us (25%)
  waiting for transfers between devices  15.4 us (14%)
  local copies, waits for them, and re-layouts  6.99 us (6%)
  other arithmetic  5.34 us (5%)
  matrix products  3.87 us (3%)
    all_to_all x1, starting transfers between devices, on_device(): lax.all_to_all(joined, 'exp', split_axis=1, concat_axis=0, tiled=True)  18.6 us
    ppermute x5, starting transfers between devices, butterfly_scan(): got_f = got_b = lax.ppermute(jnp.where(odd, total_b, total_f), 'ctx', pairs)  15.8 us
    ppermute x1, starting transfers between devices, butterfly_scan(): lax.ppermute(jnp.where(odd, behind, ahead), 'ctx', [(i, i ^ 1) for i in r...  14.2 us
    ppermute x5, waiting for transfers between devices, butterfly_scan(): got_f = got_b = lax.ppermute(jnp.where(odd, total_b, total_f), 'ctx', pairs)  13.7 us
    unnamed x8, local copies, waits for them, and re-layouts  4.35 us
    ppermute x1, starting transfers between devices, butterfly_scan(): got = lax.ppermute(jnp.stack([total_f, total_b]), 'ctx', pairs)  2.87 us
  transfers between devices with their start and end apart: 8, of which 7 were waited for; matrix products, arithmetic and copies ran while one was open for 5% of the time, Pallas kernels for 0%

profile of v11, /device:TPU:57, one launch (start us, length us, event | category | flops | bytes accessed | tf_op | source)
XLA Modules:
  0.0 111.8 jit_solution(1971813232727714461)
XLA Ops:
  0.6 2.0 %copy_bitcast_fusion = bf16[64,32,128]{2,0,1:T(8,128)(2,1)} fusion(bf16[16,4096]{1,0:T(8,128)(2,1)} %param.9, bf16[16,4096]{1,0:T(8,128)(2,1)} %param.8, bf16[16,4096]{1,0:T(8,128)(2,1)} %param.7, bf16[16,4096]{1,0:T(8,128)(2,1)} %param.6), kind=kLoop, calls=%fused_computation.24 | loop fusion | flops 2097152 | bytes 1048576 | tf_op jit(solution)/shard_map/reshape | solution.py:126
  2.7 18.6 %all-to-all-start = ((bf16[64,32,128]{2,0,1:T(8,128)(2,1)}), bf16[64,32,128]{2,0,1:T(8,128)(2,1)S(1)}, u32[]{:S(2)}, u32[]{:S(2)}) async-start(bf16[64,32,128]{2,0,1:T(8,128)(2,1)} %copy_bitcast_fusion), calls=%async_computation | async-start | bytes 1048576 | tf_op jit(solution)/shard_map/all_to_all | solution.py:127
  21.7 0.6 copy-done.1
  22.6 0.7 fusion.28
  27.0 0.8 fusion.27
  51.6 0.6 slice.24
  52.2 0.6 fusion.23
  52.8 0.7 copy-done
  53.5 1.2 %compare_convert_fusion.2 = (f32[256]{0:T(256)S(1)}, f32[256]{0:T(256)S(1)}) fusion(s32[256]{0:T(256)S(1)} %convert_reduce_fusion, s32[]{:T(128)} %bitcast.11, s32[]{:T(128)} %fusion.23), kind=kLoop, calls=%fused_computation.66 | loop fusion | flops 1024 | bytes 3080 | tf_op jit(solution)/shard_map/convert_element_type | solution.py:27
  55.0 0.5 fusion.17
  55.5 0.5 fusion.14
  56.1 2.9 %collective-permute-start = (f32[2,2,128,128]{3,2,1,0:T(8,128)S(1)}, f32[2,2,128,128]{3,2,1,0:T(8,128)S(1)}, u32[]{:S(2)}, u32[]{:S(2)}) collective-permute-start(f32[2,2,128,128]{3,2,1,0:T(8,128)S(1)} %pad_maximum_fusion), channel_id=1, source_target_pairs={{0,16},{16,0},{32,48},{48,32},{64,80},{80,64},{96,112},{112,96},{1... | collective-permute-start | bytes 786440 | tf_op jit(solution)/shard_map/ppermute | solution.py:70
  59.1 1.0 collective-permute-done
  60.2 3.1 %collective-permute-start.1 = (f32[2,128,128]{2,1,0:T(8,128)S(1)}, f32[2,128,128]{2,1,0:T(8,128)S(1)}, u32[]{:S(2)}, u32[]{:S(2)}) collective-permute-start(f32[2,128,128]{2,1,0:T(8,128)S(1)} %get-tuple-element.20), channel_id=1, source_target_pairs={{0,32},{16,48},{32,0},{48,16},{64,96},{80,112},{96,64},{112,80},{1... | collective-permute-start | bytes 393224 | tf_op jit(solution)/shard_map/ppermute | solution.py:74
  63.6 3.2 %collective-permute-done.1 = f32[2,128,128]{2,1,0:T(8,128)S(1)} collective-permute-done((f32[2,128,128]{2,1,0:T(8,128)S(1)}, f32[2,128,128]{2,1,0:T(8,128)S(1)}, u32[]{:S(2)}, u32[]{:S(2)}) %collective-permute-start.1) | collective-permute-done | bytes 131104 | tf_op jit(solution)/shard_map/ppermute | solution.py:74
  66.9 4.7 %collective-permute-start.2 = (f32[2,128,128]{2,1,0:T(8,128)S(1)}, f32[2,128,128]{2,1,0:T(8,128)S(1)}, u32[]{:S(2)}, u32[]{:S(2)}) collective-permute-start(f32[2,128,128]{2,1,0:T(8,128)S(1)} %broadcast_select_fusion.3), channel_id=1, source_target_pairs={{0,64},{16,80},{32,96},{48,112},{64,0},{80,16},{96,32},{112,48},{1... | collective-permute-start | bytes 393224 | tf_op jit(solution)/shard_map/ppermute | solution.py:74
  71.8 2.3 %collective-permute-done.2 = f32[2,128,128]{2,1,0:T(8,128)S(1)} collective-permute-done((f32[2,128,128]{2,1,0:T(8,128)S(1)}, f32[2,128,128]{2,1,0:T(8,128)S(1)}, u32[]{:S(2)}, u32[]{:S(2)}) %collective-permute-start.2) | collective-permute-done | bytes 131104 | tf_op jit(solution)/shard_map/ppermute | solution.py:74
  74.3 3.0 %collective-permute-start.3 = (f32[2,128,128]{2,1,0:T(8,128)S(1)}, f32[2,128,128]{2,1,0:T(8,128)S(1)}, u32[]{:S(2)}, u32[]{:S(2)}) collective-permute-start(f32[2,128,128]{2,1,0:T(8,128)S(1)} %get-tuple-element.17), channel_id=1, source_target_pairs={{0,128},{16,144},{32,160},{48,176},{64,192},{80,208},{96,224},{112... | collective-permute-start | bytes 393224 | tf_op jit(solution)/shard_map/ppermute | solution.py:74
  77.5 2.5 %collective-permute-done.3 = f32[2,128,128]{2,1,0:T(8,128)S(1)} collective-permute-done((f32[2,128,128]{2,1,0:T(8,128)S(1)}, f32[2,128,128]{2,1,0:T(8,128)S(1)}, u32[]{:S(2)}, u32[]{:S(2)}) %collective-permute-start.3) | collective-permute-done | bytes 131104 | tf_op jit(solution)/shard_map/ppermute | solution.py:74
  80.1 3.8 %collective-permute-start.4 = (f32[2,128,128]{2,1,0:T(8,128)S(1)}, f32[2,128,128]{2,1,0:T(8,128)S(1)}, u32[]{:S(2)}, u32[]{:S(2)}) collective-permute-start(f32[2,128,128]{2,1,0:T(8,128)S(1)} %broadcast_select_fusion.1), channel_id=1, source_target_pairs={{0,256},{32,288},{64,320},{96,352},{128,384},{160,416},{192,448},{... | collective-permute-start | bytes 393224 | tf_op jit(solution)/shard_map/ppermute | solution.py:74
  84.1 4.0 %collective-permute-done.4 = f32[2,128,128]{2,1,0:T(8,128)S(1)} collective-permute-done((f32[2,128,128]{2,1,0:T(8,128)S(1)}, f32[2,128,128]{2,1,0:T(8,128)S(1)}, u32[]{:S(2)}, u32[]{:S(2)}) %collective-permute-start.4) | collective-permute-done | bytes 131104 | tf_op jit(solution)/shard_map/ppermute | solution.py:74
  88.3 1.3 %collective-permute-start.5 = (f32[2,128,128]{2,1,0:T(8,128)S(1)}, f32[2,128,128]{2,1,0:T(8,128)S(1)}, u32[]{:S(2)}, u32[]{:S(2)}) collective-permute-start(f32[2,128,128]{2,1,0:T(8,128)S(1)} %add_select_fusion), channel_id=1, source_target_pairs={{0,512},{32,544},{64,576},{96,608},{128,640},{160,672},{192,704},{... | collective-permute-start | bytes 393224 | tf_op jit(solution)/shard_map/ppermute | solution.py:74
  89.8 1.7 %collective-permute-done.5 = f32[2,128,128]{2,1,0:T(8,128)S(1)} collective-permute-done((f32[2,128,128]{2,1,0:T(8,128)S(1)}, f32[2,128,128]{2,1,0:T(8,128)S(1)}, u32[]{:S(2)}, u32[]{:S(2)}) %collective-permute-start.5) | collective-permute-done | bytes 131104 | tf_op jit(solution)/shard_map/ppermute | solution.py:74
  91.7 14.2 %collective-permute-start.6 = (f32[2,128,128]{2,1,0:T(8,128)S(1)}, f32[2,128,128]{2,1,0:T(8,128)S(1)}, u32[]{:S(2)}, u32[]{:S(2)}) collective-permute-start(f32[2,128,128]{2,1,0:T(8,128)S(1)} %get-tuple-element.14), channel_id=1, source_target_pairs={{0,16},{16,0},{32,48},{48,32},{64,80},{80,64},{96,112},{112,96},{1... | collective-permute-start | bytes 393224 | tf_op jit(solution)/shard_map/ppermute | solution.py:101
  106.1 0.7 collective-permute-done.6
  106.9 0.4 fusion.13
  107.4 0.8 copy.86
  108.6 0.8 copy.85
  109.4 0.3 fusion.11
  109.8 0.8 copy.84
  110.6 0.3 fusion.10
  111.1 0.8 copy.83
  (39 shorter events, 3.8 us)
Async XLA Ops:
  2.7 52.2 %all-to-all-start = ((bf16[64,32,128]{2,0,1:T(8,128)(2,1)}), bf16[64,32,128]{2,0,1:T(8,128)(2,1)S(1)}, u32[]{:S(2)}, u32[]{:S(2)}) async-start(bf16[64,32,128]{2,0,1:T(8,128)(2,1)} %copy_bitcast_fusion), calls=%async_computation | async-start | bytes 1048576 | tf_op jit(solution)/shard_map/all_to_all | solution.py:127
  21.7 0.7 copy-start.1
  52.8 0.7 copy-start
  56.1 4.0 %collective-permute-start = (f32[2,2,128,128]{3,2,1,0:T(8,128)S(1)}, f32[2,2,128,128]{3,2,1,0:T(8,128)S(1)}, u32[]{:S(2)}, u32[]{:S(2)}) collective-permute-start(f32[2,2,128,128]{3,2,1,0:T(8,128)S(1)} %pad_maximum_fusion), channel_id=1, source_target_pairs={{0,16},{16,0},{32,48},{48,32},{64,80},{80,64},{96,112},{112,96},{1... | collective-permute-start | bytes 786440 | tf_op jit(solution)/shard_map/ppermute | solution.py:70
  60.2 6.6 %collective-permute-start.1 = (f32[2,128,128]{2,1,0:T(8,128)S(1)}, f32[2,128,128]{2,1,0:T(8,128)S(1)}, u32[]{:S(2)}, u32[]{:S(2)}) collective-permute-start(f32[2,128,128]{2,1,0:T(8,128)S(1)} %get-tuple-element.20), channel_id=1, source_target_pairs={{0,32},{16,48},{32,0},{48,16},{64,96},{80,112},{96,64},{112,80},{1... | collective-permute-start | bytes 393224 | tf_op jit(solution)/shard_map/ppermute | solution.py:74
  66.9 7.2 %collective-permute-start.2 = (f32[2,128,128]{2,1,0:T(8,128)S(1)}, f32[2,128,128]{2,1,0:T(8,128)S(1)}, u32[]{:S(2)}, u32[]{:S(2)}) collective-permute-start(f32[2,128,128]{2,1,0:T(8,128)S(1)} %broadcast_select_fusion.3), channel_id=1, source_target_pairs={{0,64},{16,80},{32,96},{48,112},{64,0},{80,16},{96,32},{112,48},{1... | collective-permute-start | bytes 393224 | tf_op jit(solution)/shard_map/ppermute | solution.py:74
  74.3 5.7 %collective-permute-start.3 = (f32[2,128,128]{2,1,0:T(8,128)S(1)}, f32[2,128,128]{2,1,0:T(8,128)S(1)}, u32[]{:S(2)}, u32[]{:S(2)}) collective-permute-start(f32[2,128,128]{2,1,0:T(8,128)S(1)} %get-tuple-element.17), channel_id=1, source_target_pairs={{0,128},{16,144},{32,160},{48,176},{64,192},{80,208},{96,224},{112... | collective-permute-start | bytes 393224 | tf_op jit(solution)/shard_map/ppermute | solution.py:74
  80.1 8.0 %collective-permute-start.4 = (f32[2,128,128]{2,1,0:T(8,128)S(1)}, f32[2,128,128]{2,1,0:T(8,128)S(1)}, u32[]{:S(2)}, u32[]{:S(2)}) collective-permute-start(f32[2,128,128]{2,1,0:T(8,128)S(1)} %broadcast_select_fusion.1), channel_id=1, source_target_pairs={{0,256},{32,288},{64,320},{96,352},{128,384},{160,416},{192,448},{... | collective-permute-start | bytes 393224 | tf_op jit(solution)/shard_map/ppermute | solution.py:74
  88.3 3.2 %collective-permute-start.5 = (f32[2,128,128]{2,1,0:T(8,128)S(1)}, f32[2,128,128]{2,1,0:T(8,128)S(1)}, u32[]{:S(2)}, u32[]{:S(2)}) collective-permute-start(f32[2,128,128]{2,1,0:T(8,128)S(1)} %add_select_fusion), channel_id=1, source_target_pairs={{0,512},{32,544},{64,576},{96,608},{128,640},{160,672},{192,704},{... | collective-permute-start | bytes 393224 | tf_op jit(solution)/shard_map/ppermute | solution.py:74
  91.7 15.2 %collective-permute-start.6 = (f32[2,128,128]{2,1,0:T(8,128)S(1)}, f32[2,128,128]{2,1,0:T(8,128)S(1)}, u32[]{:S(2)}, u32[]{:S(2)}) collective-permute-start(f32[2,128,128]{2,1,0:T(8,128)S(1)} %get-tuple-element.14), channel_id=1, source_target_pairs={{0,16},{16,0},{32,48},{48,32},{64,80},{80,64},{96,112},{112,96},{1... | collective-permute-start | bytes 393224 | tf_op jit(solution)/shard_map/ppermute | solution.py:101

commit v12 on v10

--- a/solution.py
+++ b/solution.py
@@ -105,7 +105,7 @@
 
 
 def on_device(queries, keys, values, out_grad, decay_rate, doc_lengths):
-    precise = lax.Precision.HIGHEST
+    precise = lax.Precision.HIGH
     rows_in = queries.shape[0]
     count = lax.axis_size("ctx")
     group_len = rows_in * lax.axis_size("exp")

time: 113 us -> 113 us (level)
  no operation moved by 1% of the time
where the time goes in v12:
time: 113 us; the launch traced here: 111 us
  starting transfers between devices  51.4 us (45%)
  between operations  28.8 us (25%)
  waiting for transfers between devices  15.4 us (14%)
  local copies, waits for them, and re-layouts  6.99 us (6%)
  other arithmetic  5.34 us (5%)
  matrix products  3.55 us (3%)
    ppermute x5, starting transfers between devices, butterfly_scan(): got_f = got_b = lax.ppermute(jnp.where(odd, total_b, total_f), 'ctx', pairs)  18.8 us
    all_to_all x1, starting transfers between devices, on_device(): lax.all_to_all(joined, 'exp', split_axis=1, concat_axis=0, tiled=True)  18.6 us
    ppermute x5, waiting for transfers between devices, butterfly_scan(): got_f = got_b = lax.ppermute(jnp.where(odd, total_b, total_f), 'ctx', pairs)  13.7 us
    ppermute x1, starting transfers between devices, butterfly_scan(): lax.ppermute(jnp.where(odd, behind, ahead), 'ctx', [(i, i ^ 1) for i in r...  11.1 us
    unnamed x8, local copies, waits for them, and re-layouts  4.35 us
    ppermute x1, starting transfers between devices, butterfly_scan(): got = lax.ppermute(jnp.stack([total_f, total_b]), 'ctx', pairs)  2.86 us
  transfers between devices with their start and end apart: 8, of which 7 were waited for; matrix products, arithmetic and copies ran while one was open for 5% of the time, Pallas kernels for 0%

profile of v12, /device:TPU:57, one launch (start us, length us, event | category | flops | bytes accessed | tf_op | source)
XLA Modules:
  0.0 111.4 jit_solution(16497375229193693590)
XLA Ops:
  0.6 2.0 %copy_bitcast_fusion = bf16[64,32,128]{2,0,1:T(8,128)(2,1)} fusion(bf16[16,4096]{1,0:T(8,128)(2,1)} %param.9, bf16[16,4096]{1,0:T(8,128)(2,1)} %param.8, bf16[16,4096]{1,0:T(8,128)(2,1)} %param.7, bf16[16,4096]{1,0:T(8,128)(2,1)} %param.6), kind=kLoop, calls=%fused_computation.24 | loop fusion | flops 2097152 | bytes 1048576 | tf_op jit(solution)/shard_map/reshape | solution.py:119
  2.7 18.6 %all-to-all-start = ((bf16[64,32,128]{2,0,1:T(8,128)(2,1)}), bf16[64,32,128]{2,0,1:T(8,128)(2,1)S(1)}, u32[]{:S(2)}, u32[]{:S(2)}) async-start(bf16[64,32,128]{2,0,1:T(8,128)(2,1)} %copy_bitcast_fusion), calls=%async_computation | async-start | bytes 1048576 | tf_op jit(solution)/shard_map/all_to_all | solution.py:120
  21.7 0.6 copy-done.1
  22.6 0.7 fusion.28
  27.0 0.8 fusion.27
  51.6 0.6 slice.24
  52.2 0.6 fusion.23
  52.8 0.7 copy-done
  53.5 1.2 %compare_convert_fusion.2 = (f32[256]{0:T(256)S(1)}, f32[256]{0:T(256)S(1)}) fusion(s32[256]{0:T(256)S(1)} %convert_reduce_fusion, s32[]{:T(128)} %bitcast.11, s32[]{:T(128)} %fusion.23), kind=kLoop, calls=%fused_computation.66 | loop fusion | flops 1024 | bytes 3080 | tf_op jit(solution)/shard_map/convert_element_type | solution.py:27
  55.0 0.4 fusion.17
  55.5 0.4 fusion.14
  56.0 2.9 %collective-permute-start = (f32[2,2,128,128]{3,2,1,0:T(8,128)S(1)}, f32[2,2,128,128]{3,2,1,0:T(8,128)S(1)}, u32[]{:S(2)}, u32[]{:S(2)}) collective-permute-start(f32[2,2,128,128]{3,2,1,0:T(8,128)S(1)} %pad_maximum_fusion), channel_id=1, source_target_pairs={{0,16},{16,0},{32,48},{48,32},{64,80},{80,64},{96,112},{112,96},{1... | collective-permute-start | bytes 786440 | tf_op jit(solution)/shard_map/ppermute | solution.py:63
  59.0 1.0 collective-permute-done
  60.1 3.1 %collective-permute-start.1 = (f32[2,128,128]{2,1,0:T(8,128)S(1)}, f32[2,128,128]{2,1,0:T(8,128)S(1)}, u32[]{:S(2)}, u32[]{:S(2)}) collective-permute-start(f32[2,128,128]{2,1,0:T(8,128)S(1)} %get-tuple-element.20), channel_id=1, source_target_pairs={{0,32},{16,48},{32,0},{48,16},{64,96},{80,112},{96,64},{112,80},{1... | collective-permute-start | bytes 393224 | tf_op jit(solution)/shard_map/ppermute | solution.py:67
  63.4 3.2 %collective-permute-done.1 = f32[2,128,128]{2,1,0:T(8,128)S(1)} collective-permute-done((f32[2,128,128]{2,1,0:T(8,128)S(1)}, f32[2,128,128]{2,1,0:T(8,128)S(1)}, u32[]{:S(2)}, u32[]{:S(2)}) %collective-permute-start.1) | collective-permute-done | bytes 131104 | tf_op jit(solution)/shard_map/ppermute | solution.py:67
  66.8 4.7 %collective-permute-start.2 = (f32[2,128,128]{2,1,0:T(8,128)S(1)}, f32[2,128,128]{2,1,0:T(8,128)S(1)}, u32[]{:S(2)}, u32[]{:S(2)}) collective-permute-start(f32[2,128,128]{2,1,0:T(8,128)S(1)} %broadcast_select_fusion.3), channel_id=1, source_target_pairs={{0,64},{16,80},{32,96},{48,112},{64,0},{80,16},{96,32},{112,48},{1... | collective-permute-start | bytes 393224 | tf_op jit(solution)/shard_map/ppermute | solution.py:67
  71.7 2.3 %collective-permute-done.2 = f32[2,128,128]{2,1,0:T(8,128)S(1)} collective-permute-done((f32[2,128,128]{2,1,0:T(8,128)S(1)}, f32[2,128,128]{2,1,0:T(8,128)S(1)}, u32[]{:S(2)}, u32[]{:S(2)}) %collective-permute-start.2) | collective-permute-done | bytes 131104 | tf_op jit(solution)/shard_map/ppermute | solution.py:67
  74.1 3.0 %collective-permute-start.3 = (f32[2,128,128]{2,1,0:T(8,128)S(1)}, f32[2,128,128]{2,1,0:T(8,128)S(1)}, u32[]{:S(2)}, u32[]{:S(2)}) collective-permute-start(f32[2,128,128]{2,1,0:T(8,128)S(1)} %get-tuple-element.17), channel_id=1, source_target_pairs={{0,128},{16,144},{32,160},{48,176},{64,192},{80,208},{96,224},{112... | collective-permute-start | bytes 393224 | tf_op jit(solution)/shard_map/ppermute | solution.py:67
  77.4 2.5 %collective-permute-done.3 = f32[2,128,128]{2,1,0:T(8,128)S(1)} collective-permute-done((f32[2,128,128]{2,1,0:T(8,128)S(1)}, f32[2,128,128]{2,1,0:T(8,128)S(1)}, u32[]{:S(2)}, u32[]{:S(2)}) %collective-permute-start.3) | collective-permute-done | bytes 131104 | tf_op jit(solution)/shard_map/ppermute | solution.py:67
  80.0 3.8 %collective-permute-start.4 = (f32[2,128,128]{2,1,0:T(8,128)S(1)}, f32[2,128,128]{2,1,0:T(8,128)S(1)}, u32[]{:S(2)}, u32[]{:S(2)}) collective-permute-start(f32[2,128,128]{2,1,0:T(8,128)S(1)} %broadcast_select_fusion.1), channel_id=1, source_target_pairs={{0,256},{16,272},{32,288},{48,304},{64,320},{80,336},{96,352},{112... | collective-permute-start | bytes 393224 | tf_op jit(solution)/shard_map/ppermute | solution.py:67
  83.9 4.0 %collective-permute-done.4 = f32[2,128,128]{2,1,0:T(8,128)S(1)} collective-permute-done((f32[2,128,128]{2,1,0:T(8,128)S(1)}, f32[2,128,128]{2,1,0:T(8,128)S(1)}, u32[]{:S(2)}, u32[]{:S(2)}) %collective-permute-start.4) | collective-permute-done | bytes 131104 | tf_op jit(solution)/shard_map/ppermute | solution.py:67
  88.1 4.3 %collective-permute-start.5 = (f32[2,128,128]{2,1,0:T(8,128)S(1)}, f32[2,128,128]{2,1,0:T(8,128)S(1)}, u32[]{:S(2)}, u32[]{:S(2)}) collective-permute-start(f32[2,128,128]{2,1,0:T(8,128)S(1)} %add_select_fusion), channel_id=1, source_target_pairs={{0,512},{32,544},{64,576},{96,608},{128,640},{160,672},{192,704},{... | collective-permute-start | bytes 393224 | tf_op jit(solution)/shard_map/ppermute | solution.py:67
  92.7 1.7 %collective-permute-done.5 = f32[2,128,128]{2,1,0:T(8,128)S(1)} collective-permute-done((f32[2,128,128]{2,1,0:T(8,128)S(1)}, f32[2,128,128]{2,1,0:T(8,128)S(1)}, u32[]{:S(2)}, u32[]{:S(2)}) %collective-permute-start.5) | collective-permute-done | bytes 131104 | tf_op jit(solution)/shard_map/ppermute | solution.py:67
  94.6 11.1 %collective-permute-start.6 = (f32[2,128,128]{2,1,0:T(8,128)S(1)}, f32[2,128,128]{2,1,0:T(8,128)S(1)}, u32[]{:S(2)}, u32[]{:S(2)}) collective-permute-start(f32[2,128,128]{2,1,0:T(8,128)S(1)} %get-tuple-element.14), channel_id=1, source_target_pairs={{0,16},{16,0},{32,48},{48,32},{64,80},{80,64},{96,112},{112,96},{1... | collective-permute-start | bytes 393224 | tf_op jit(solution)/shard_map/ppermute | solution.py:94
  105.9 0.7 collective-permute-done.6
  106.6 0.3 fusion.13
  107.1 0.8 copy.86
  107.8 0.3 fusion.12
  108.3 0.8 copy.85
  109.0 0.3 fusion.11
  109.5 0.8 copy.84
  110.7 0.8 copy.83
  (39 shorter events, 3.8 us)
Async XLA Ops:
  2.7 52.2 %all-to-all-start = ((bf16[64,32,128]{2,0,1:T(8,128)(2,1)}), bf16[64,32,128]{2,0,1:T(8,128)(2,1)S(1)}, u32[]{:S(2)}, u32[]{:S(2)}) async-start(bf16[64,32,128]{2,0,1:T(8,128)(2,1)} %copy_bitcast_fusion), calls=%async_computation | async-start | bytes 1048576 | tf_op jit(solution)/shard_map/all_to_all | solution.py:120
  21.7 0.7 copy-start.1
  52.8 0.7 copy-start
  56.0 4.0 %collective-permute-start = (f32[2,2,128,128]{3,2,1,0:T(8,128)S(1)}, f32[2,2,128,128]{3,2,1,0:T(8,128)S(1)}, u32[]{:S(2)}, u32[]{:S(2)}) collective-permute-start(f32[2,2,128,128]{3,2,1,0:T(8,128)S(1)} %pad_maximum_fusion), channel_id=1, source_target_pairs={{0,16},{16,0},{32,48},{48,32},{64,80},{80,64},{96,112},{112,96},{1... | collective-permute-start | bytes 786440 | tf_op jit(solution)/shard_map/ppermute | solution.py:63
  60.1 6.6 %collective-permute-start.1 = (f32[2,128,128]{2,1,0:T(8,128)S(1)}, f32[2,128,128]{2,1,0:T(8,128)S(1)}, u32[]{:S(2)}, u32[]{:S(2)}) collective-permute-start(f32[2,128,128]{2,1,0:T(8,128)S(1)} %get-tuple-element.20), channel_id=1, source_target_pairs={{0,32},{16,48},{32,0},{48,16},{64,96},{80,112},{96,64},{112,80},{1... | collective-permute-start | bytes 393224 | tf_op jit(solution)/shard_map/ppermute | solution.py:67
  66.8 7.2 %collective-permute-start.2 = (f32[2,128,128]{2,1,0:T(8,128)S(1)}, f32[2,128,128]{2,1,0:T(8,128)S(1)}, u32[]{:S(2)}, u32[]{:S(2)}) collective-permute-start(f32[2,128,128]{2,1,0:T(8,128)S(1)} %broadcast_select_fusion.3), channel_id=1, source_target_pairs={{0,64},{16,80},{32,96},{48,112},{64,0},{80,16},{96,32},{112,48},{1... | collective-permute-start | bytes 393224 | tf_op jit(solution)/shard_map/ppermute | solution.py:67
  74.1 5.7 %collective-permute-start.3 = (f32[2,128,128]{2,1,0:T(8,128)S(1)}, f32[2,128,128]{2,1,0:T(8,128)S(1)}, u32[]{:S(2)}, u32[]{:S(2)}) collective-permute-start(f32[2,128,128]{2,1,0:T(8,128)S(1)} %get-tuple-element.17), channel_id=1, source_target_pairs={{0,128},{16,144},{32,160},{48,176},{64,192},{80,208},{96,224},{112... | collective-permute-start | bytes 393224 | tf_op jit(solution)/shard_map/ppermute | solution.py:67
  80.0 8.0 %collective-permute-start.4 = (f32[2,128,128]{2,1,0:T(8,128)S(1)}, f32[2,128,128]{2,1,0:T(8,128)S(1)}, u32[]{:S(2)}, u32[]{:S(2)}) collective-permute-start(f32[2,128,128]{2,1,0:T(8,128)S(1)} %broadcast_select_fusion.1), channel_id=1, source_target_pairs={{0,256},{16,272},{32,288},{48,304},{64,320},{80,336},{96,352},{112... | collective-permute-start | bytes 393224 | tf_op jit(solution)/shard_map/ppermute | solution.py:67
  88.1 6.3 %collective-permute-start.5 = (f32[2,128,128]{2,1,0:T(8,128)S(1)}, f32[2,128,128]{2,1,0:T(8,128)S(1)}, u32[]{:S(2)}, u32[]{:S(2)}) collective-permute-start(f32[2,128,128]{2,1,0:T(8,128)S(1)} %add_select_fusion), channel_id=1, source_target_pairs={{0,512},{32,544},{64,576},{96,608},{128,640},{160,672},{192,704},{... | collective-permute-start | bytes 393224 | tf_op jit(solution)/shard_map/ppermute | solution.py:67
  94.6 12.0 %collective-permute-start.6 = (f32[2,128,128]{2,1,0:T(8,128)S(1)}, f32[2,128,128]{2,1,0:T(8,128)S(1)}, u32[]{:S(2)}, u32[]{:S(2)}) collective-permute-start(f32[2,128,128]{2,1,0:T(8,128)S(1)} %get-tuple-element.14), channel_id=1, source_target_pairs={{0,16},{16,0},{32,48},{48,32},{64,80},{80,64},{96,112},{112,96},{1... | collective-permute-start | bytes 393224 | tf_op jit(solution)/shard_map/ppermute | solution.py:94
